TPU v7x, 512 devices: a whole 4x8x8 slice. The times are simulated.
512 devices in a mesh: freq: 16 (over y, core), sky: 32 (over z, x).
Axes of the slice: x: 4, y: 8, z: 8, core: 2. Of those that a mesh axis runs over, the one named last changes fastest.
Arguments:
- visibilities: bfloat16 [128, 2, 1024, 1024], P('freq', None, 'sky'), may hold values from -30 to 30
- templates: float32 [16, 128], replicated, may hold values from -0.5 to 0.5
Outputs:
- scores: float32 [16, 1024, 1024], P(None, 'freq', 'sky')
- continuum: float32 [9, 1024, 1024], P(None, 'freq', 'sky')
All inputs are finite; a program needn't handle non-finite values.
Results may differ from a plain program's by a relative error of at most 0.006.
Values may be sent and summed in bfloat16 or wider, within the bound.
No kernel may reach another device: no remote copies, remote signals or barrier semaphores. Data moves between devices by JAX's collectives and lax.ppermute only.
A program may use at most 128 MiB of HBM per device.

v0:
```python
import numpy as np

import jax
import jax.numpy as jnp
from jax import lax
from jax.sharding import PartitionSpec as P

ORDER = 8


epsilon = 1e-06


def tables(points):
    block = 32
    index = jnp.arange(points, dtype=jnp.int32)
    step = jnp.arange(block, dtype=jnp.int32)
    factor = jnp.float32(points ** (-0.5))
    scale = jnp.float32(2.0 * np.pi / points)
    high = ((block * step)[:, None] * index[None, :]) % points
    low = (step[:, None] * index[None, :]) % points
    high_c = jnp.cos(scale * high.astype(jnp.float32))
    high_s = jnp.sin(scale * high.astype(jnp.float32))
    low_c = jnp.cos(scale * low.astype(jnp.float32))
    low_s = jnp.sin(scale * low.astype(jnp.float32))
    cos = high_c[:, None, :] * low_c[None, :, :] - high_s[:, None, :] * low_s[None, :, :]
    sin = high_s[:, None, :] * low_c[None, :, :] + high_c[:, None, :] * low_s[None, :, :]
    cos = (cos * factor).astype(jnp.bfloat16).reshape(points, points)
    sin = (sin * factor).astype(jnp.bfloat16).reshape(points, points)
    return lax.optimization_barrier((cos, sin))


def distances(row_pos, col_pos, points):
    half = jnp.float32(points / 2.0)
    row_term = (row_pos - half) * (row_pos - half)
    col_term = (col_pos - half) * (col_pos - half)
    return (row_term[:, None] + col_term[None, :]) / (half * half)


def basis_rows(channels, degree):
    abscissa = (2.0 * np.arange(channels, dtype=np.float64) - (channels - 1)) / (channels - 1)
    legendre = [np.ones((channels,), np.float64), abscissa]
    for order_idx in range(1, degree):
        legendre.append(
            (
                (2 * order_idx + 1) * abscissa * legendre[order_idx]
                - order_idx * legendre[order_idx - 1]
            )
            / (order_idx + 1)
        )
    legendre = legendre[: degree + 1]
    rows = []
    for vector in legendre:
        for sweep in range(2):
            for earlier in rows:
                vector = vector - np.sum(vector * earlier) * earlier
        vector = vector / np.sqrt(np.sum(vector * vector))
        rows.append(vector)
    return np.stack(rows).astype(np.float32)


def filters(templates, channels, degree):
    basis = jnp.asarray(basis_rows(channels, degree))
    coeffs = jnp.dot(templates, basis.T, precision=lax.Precision.HIGHEST)
    matched = templates - jnp.dot(coeffs, basis, precision=lax.Precision.HIGHEST)
    return jnp.concatenate([matched, basis], axis=0).astype(jnp.bfloat16)


def body(visibilities, templates):
    channels = visibilities.shape[0]
    row_count = visibilities.shape[2]
    points = visibilities.shape[3]
    num_templates = templates.shape[0]
    freq_count = lax.axis_size("freq")
    sky_count = lax.axis_size("sky")
    all_channels = channels * freq_count
    columns = points // sky_count
    lines = points // freq_count
    cosine, sine = tables(points)

    rows = visibilities.reshape(channels * 2 * row_count, points)
    with_cos = jnp.dot(rows, cosine, preferred_element_type=jnp.float32).reshape(
        channels, 2, row_count, points
    )
    with_sin = jnp.dot(rows, sine, preferred_element_type=jnp.float32).reshape(
        channels, 2, row_count, points
    )
    section_real = (with_cos[:, 0] - with_sin[:, 1]).astype(jnp.bfloat16)
    section_imag = (with_sin[:, 0] + with_cos[:, 1]).astype(jnp.bfloat16)
    stacked = jnp.stack([section_real, section_imag])
    stacked = stacked.reshape(2, channels, row_count, sky_count, columns)
    send = jnp.transpose(stacked, (3, 0, 2, 1, 4)).reshape(
        sky_count, 2, row_count, channels * columns
    )
    turned = lax.all_to_all(send, "sky", 0, 0, tiled=True)
    turned = turned.reshape(sky_count * 2 * row_count, channels * columns)

    table = jnp.stack(
        [
            cosine.reshape(points, sky_count, row_count),
            -sine.reshape(points, sky_count, row_count),
        ],
        axis=2,
    ).reshape(points, sky_count * 2 * row_count)
    picture = jnp.dot(table, turned, preferred_element_type=jnp.float32).reshape(
        points, channels, columns
    )
    row_pos = jnp.arange(points, dtype=jnp.float32)
    col_pos = (lax.axis_index("sky") * columns + jnp.arange(columns, dtype=jnp.int32)).astype(
        jnp.float32
    )
    chan_pos = (lax.axis_index("freq") * channels + jnp.arange(channels, dtype=jnp.int32)).astype(
        jnp.float32
    )
    stretch = 1.0 + 0.5 * chan_pos / jnp.float32(all_channels - 1)
    coef = -0.7 * stretch * stretch
    dist = distances(row_pos, col_pos, points)
    spectra = (jnp.exp(coef[None, :, None] * dist[:, None, :]) * picture).astype(jnp.bfloat16)
    widened = spectra.astype(jnp.float32)
    power_sum = lax.psum(jnp.sum(widened * widened), ("freq", "sky"))

    outgoing = jnp.transpose(
        spectra.reshape(freq_count, lines, channels, columns), (0, 2, 1, 3)
    )
    gathered = lax.all_to_all(outgoing, "freq", 0, 0, tiled=True)
    gathered = gathered.reshape(all_channels, lines * columns)
    weights = filters(templates, all_channels, ORDER)
    result = jnp.dot(weights, gathered, preferred_element_type=jnp.float32).reshape(
        weights.shape[0], lines, columns
    )
    spread = jnp.sqrt(power_sum / (all_channels * points * points) + epsilon)
    return (result[:num_templates] / spread, result[num_templates:])


def solution(mesh):
    return jax.shard_map(
        body,
        mesh=mesh,
        in_specs=(P("freq", None, "sky", None), P()),
        out_specs=(P(None, "freq", "sky"), P(None, "freq", "sky")),
        check_vma=False,
    )
```

profile of v0, /device:TPU:1, one launch (start us, length us, event | category | flops | bytes accessed | tf_op | source)
XLA Modules:
  0.0 200.1 jit_solution(8614768619738902606)
XLA Ops:
  1.8 1.6 multiply_convert_fusion
  3.4 1.3 fusion.30
  4.6 1.3 fusion.29
  5.9 1.3 fusion.5
  7.2 3.7 %convert_element_type.100 = bf16[1,8,32,32,32]{4,3,2,1,0:T(8,128)(2,1)} reshape(bf16[8,1,32,1024]{3,2,0,1:T(8,128)(2,1)} %get-tuple-element.15) | data formatting | bytes 1048576 | tf_op jit(solution)/shard_map/convert_element_type | solution.py:89
  10.9 3.7 %convert_element_type.98 = bf16[1,8,32,32,32]{4,3,2,1,0:T(8,128)(2,1)} reshape(bf16[8,1,32,1024]{3,2,0,1:T(8,128)(2,1)} %get-tuple-element.14) | data formatting | bytes 1048576 | tf_op jit(solution)/shard_map/convert_element_type | solution.py:88
  14.6 3.2 %maximum_bitcast_fusion = bf16[32,2,32,8,32]{4,0,2,3,1:T(8,128)(2,1)S(1)} fusion(bf16[1,8,32,32,32]{4,3,2,1,0:T(8,128)(2,1)} %convert_element_type.100, bf16[1,8,32,32,32]{4,3,2,1,0:T(8,128)(2,1)} %convert_element_type.98), kind=kLoop, calls=%fused_computation.1 | loop fusion | flops 524288 | bytes 2097152 | tf_op jit(solution)/shard_map/transpose | solution.py:92
  17.8 4.6 %copy.33 = bf16[32,2,32,8,32]{4,3,2,1,0:T(8,128)(2,1)} copy(bf16[32,2,32,8,32]{4,0,2,3,1:T(8,128)(2,1)S(1)} %maximum_bitcast_fusion) | data formatting | bytes 2097152 | tf_op jit(solution)/shard_map/transpose | solution.py:92
  22.4 6.2 %reshape.256 = bf16[32,2,32,256]{3,2,1,0:T(8,128)(2,1)} reshape(bf16[32,2,32,8,32]{4,3,2,1,0:T(8,128)(2,1)} %copy.33) | data formatting | bytes 2097152 | tf_op jit(solution)/shard_map/reshape | solution.py:92
  28.6 14.1 %all-to-all-start = ((bf16[32,2,32,256]{3,2,1,0:T(8,128)(2,1)}), bf16[32,2,32,256]{3,2,1,0:T(8,128)(2,1)}, u32[]{:S(2)}, u32[]{:S(2)}) async-start(bf16[32,2,32,256]{3,2,1,0:T(8,128)(2,1)} %reshape.256), calls=%async_computation | async-start | bytes 2097152 | tf_op jit(solution)/shard_map/all_to_all | solution.py:95
  42.7 3.4 %neg.13 = bf16[1024,1024]{1,0:T(8,128)(2,1)} negate(bf16[1024,1024]{1,0:T(8,128)(2,1)} %bitcast.79) | non-fusion elementwise | flops 1048576 | bytes 4194304 | tf_op jit(solution)/shard_map/neg | solution.py:101
  46.1 2.5 %copy.26 = bf16[1024,1024]{0,1:T(8,128)(2,1)} copy(bf16[1024,1024]{1,0:T(8,128)(2,1)S(1)} %bitcast.77) | data formatting | bytes 4194304 | tf_op jit(solution)/shard_map/optimization_barrier | solution.py:30
  48.6 4.1 %copy.27 = bf16[1024,1024]{0,1:T(8,128)(2,1)} copy(bf16[1024,1024]{1,0:T(8,128)(2,1)} %neg.13) | data formatting | bytes 4194304 | tf_op jit(solution)/shard_map/neg | solution.py:101
  52.7 2.0 pad_maximum_fusion
  54.7 2.4 %copy.28 = bf16[1024,32,2,32]{0,3,2,1:T(8,128)(2,1)} copy(bf16[1024,32,2,32]{0,3,1,2:T(8,128)(2,1)S(1)} %pad_maximum_fusion) | data formatting | bytes 8388608 | tf_op jit(solution)/shard_map/stack | solution.py:98
  57.2 11.4 %all-to-all-done = bf16[32,2,32,256]{3,2,1,0:T(8,128)(2,1)} async-done(((bf16[32,2,32,256]{3,2,1,0:T(8,128)(2,1)}), bf16[32,2,32,256]{3,2,1,0:T(8,128)(2,1)}, u32[]{:S(2)}, u32[]{:S(2)}) %all-to-all-start) | async-done | bytes 1048608 | tf_op jit(solution)/shard_map/all_to_all | solution.py:95
  68.6 1.5 copy.34
  70.1 4.2 %multiply_reduce_fusion = (f32[]{:T(128)}, bf16[1024,8,32]{0,2,1:T(8,128)(2,1)S(1)}) fusion(bf16[1024,2048,1]{0,1,2:T(8,128)(2,1)} %bitcast.83, bf16[8,32,2048]{2,1,0:T(8,128)(2,1)S(1)} %bitcast.87, f32[1024,32]{0,1:T(8,128)S(1)} %add_multiply_fusion, f32[8]{0:T(128)S(1)} %multiply_multiply_fusion), kind=kOutput, calls=%fused_computation.17 | convolution fusion | flops 1075314688 | bytes 5898276 | tf_op jit(solution)/shard_map/dot_general | solution.py:105
  75.2 1.5 reshape.261
  76.8 10.1 %all-to-all-start.1 = ((bf16[16,2,8192]{2,1,0:T(2,128)(2,1)}), bf16[16,2,8192]{2,1,0:T(2,128)(2,1)S(1)}, u32[]{:S(2)}, u32[]{:S(2)}) async-start(bf16[16,2,8192]{2,1,0:T(2,128)(2,1)} %reshape.261), calls=%async_computation.1 | async-start | bytes 1048576 | tf_op jit(solution)/shard_map/all_to_all | solution.py:125
  87.2 102.3 %psum.7 = f32[]{:T(128)} all-reduce(f32[]{:T(128)} %get-tuple-element.20), channel_id=1, replica_groups=mesh['freq'=16,'sky'=32] {'freq','sky'}, use_global_device_ids=true, to_apply=%region_1.2 | all-reduce | flops 1 | bytes 8 | tf_op jit(solution)/shard_map/psum | solution.py:120
  190.2 1.6 reshape.262
  191.8 2.0 copy.37
  193.8 3.0 %reshape.259 = bf16[128,2048]{1,0:T(8,128)(2,1)} reshape(bf16[16,8,64,32]{3,2,1,0:T(8,128)(2,1)S(1)} %copy.37) | data formatting | bytes 1048576 | tf_op jit(solution)/shard_map/reshape | solution.py:126
  (31 shorter events, 5.8 us)
Async XLA Ops:
  0.6 2.7 %copy-start = (bf16[8,2,32,1024]{3,2,1,0:T(8,128)(2,1)S(1)}, bf16[8,2,32,1024]{3,2,1,0:T(8,128)(2,1)}, u32[]{:S(2)}) copy-start(bf16[8,2,32,1024]{3,2,1,0:T(8,128)(2,1)} %param.3) | copy-start | bytes 3145732
  3.4 2.5 %copy-start.1 = (bf16[32,32,1024]{2,1,0:T(8,128)(2,1)}, bf16[32,32,1024]{2,1,0:T(8,128)(2,1)S(1)}, u32[]{:S(2)}) copy-start(bf16[32,32,1024]{2,1,0:T(8,128)(2,1)S(1)} %get-tuple-element.16) | copy-start | bytes 6291460
  28.6 40.0 %all-to-all-start = ((bf16[32,2,32,256]{3,2,1,0:T(8,128)(2,1)}), bf16[32,2,32,256]{3,2,1,0:T(8,128)(2,1)}, u32[]{:S(2)}, u32[]{:S(2)}) async-start(bf16[32,2,32,256]{3,2,1,0:T(8,128)(2,1)} %reshape.256), calls=%async_computation | async-start | bytes 2097152 | tf_op jit(solution)/shard_map/all_to_all | solution.py:95
  48.6 4.1 %copy-start.2 = (bf16[1024,1024]{0,1:T(8,128)(2,1)S(1)}, bf16[1024,1024]{0,1:T(8,128)(2,1)}, u32[]{:S(2)}) copy-start(bf16[1024,1024]{0,1:T(8,128)(2,1)} %copy.26) | copy-start | bytes 6291460
  74.3 12.5 %copy-start.3 = (f32[16,128]{1,0:T(8,128)S(1)}, f32[16,128]{1,0:T(8,128)}, u32[]{:S(2)}) copy-start(f32[16,128]{1,0:T(8,128)} %param.4) | copy-start | bytes 24580
  74.3 12.5 %copy-start.4 = (f32[9,128]{1,0:T(8,128)S(1)}, f32[9,128]{1,0:T(8,128)}, u32[]{:S(2)}) copy-start(f32[9,128]{1,0:T(8,128)} %constant.64.clone) | copy-start | bytes 13828
  76.8 120.0 %copy-start.5 = (bf16[9,128]{1,0:T(8,128)(2,1)S(1)}, bf16[9,128]{1,0:T(8,128)(2,1)}, u32[]{:S(2)}) copy-start(bf16[9,128]{1,0:T(8,128)(2,1)} %constant.66) | copy-start | bytes 6916
  76.8 113.4 %all-to-all-start.1 = ((bf16[16,2,8192]{2,1,0:T(2,128)(2,1)}), bf16[16,2,8192]{2,1,0:T(2,128)(2,1)S(1)}, u32[]{:S(2)}, u32[]{:S(2)}) async-start(bf16[16,2,8192]{2,1,0:T(2,128)(2,1)} %reshape.261), calls=%async_computation.1 | async-start | bytes 1048576 | tf_op jit(solution)/shard_map/all_to_all | solution.py:125
where the time goes:
time: 201 us; the launch traced here: 200 us
  blocking collectives  102 us (51%)
  local copies, waits for them, and re-layouts  39.8 us (20%)
  starting transfers between devices  24.1 us (12%)
  other arithmetic  12.7 us (6%)
  waiting for transfers between devices  11.4 us (6%)
  matrix products  8.27 us (4%)
    psum x1, blocking collectives, body(): power_sum = lax.psum(jnp.sum(widened * widened), ('freq', 'sky'))  102 us
    all_to_all x1, starting transfers between devices, body(): turned = lax.all_to_all(send, 'sky', 0, 0, tiled=True)  14.1 us
    all_to_all x1, waiting for transfers between devices, body(): turned = lax.all_to_all(send, 'sky', 0, 0, tiled=True)  11.4 us
    all_to_all x1, starting transfers between devices, body(): gathered = lax.all_to_all(outgoing, 'freq', 0, 0, tiled=True)  10.1 us
    reshape x1, local copies, waits for them, and re-layouts, body(): jnp.transpose(stacked, (3, 0, 2, 1, 4))  6.18 us
    unnamed x16, local copies, waits for them, and re-layouts  4.88 us
    transpose x1, local copies, waits for them, and re-layouts, body(): jnp.transpose(stacked, (3, 0, 2, 1, 4))  4.65 us
    dot_general x1, matrix products, body(): jnp.dot(table, turned, preferred_element_type=jnp.float32)  4.19 us
  transfers between devices with their start and end apart: 2, of which 1 were waited for; matrix products, arithmetic and copies ran while one was open for 7% of the time, Pallas kernels for 0%

commit v1 on v0

--- a/solution.py
+++ b/solution.py
@@ -117,15 +117,29 @@
     dist = distances(row_pos, col_pos, points)
     spectra = (jnp.exp(coef[None, :, None] * dist[:, None, :]) * picture).astype(jnp.bfloat16)
     widened = spectra.astype(jnp.float32)
-    power_sum = lax.psum(jnp.sum(widened * widened), ("freq", "sky"))
+    power_part = jnp.sum(widened * widened)
 
     outgoing = jnp.transpose(
         spectra.reshape(freq_count, lines, channels, columns), (0, 2, 1, 3)
+    ).reshape(freq_count, channels * lines * columns)
+    high = power_part.astype(jnp.bfloat16)
+    rest = power_part - high.astype(jnp.float32)
+    middle = rest.astype(jnp.bfloat16)
+    low = (rest - middle.astype(jnp.float32)).astype(jnp.bfloat16)
+    pieces = jnp.zeros((128,), jnp.bfloat16).at[0].set(high).at[1].set(middle).at[2].set(low)
+    outgoing = jnp.concatenate(
+        [outgoing, jnp.broadcast_to(pieces[None, :], (freq_count, 128))], axis=1
     )
     gathered = lax.all_to_all(outgoing, "freq", 0, 0, tiled=True)
-    gathered = gathered.reshape(all_channels, lines * columns)
+    shares = gathered[:, channels * lines * columns :][:, :3].astype(jnp.float32)
+    power_freq = jnp.sum(shares)
+    images = gathered[:, : channels * lines * columns].reshape(all_channels, lines * columns)
+    column_power = lax.all_to_all(
+        jnp.broadcast_to(power_freq, (sky_count, 128)), "sky", 0, 0, tiled=True
+    )
+    power_sum = jnp.sum(column_power[:, 0])
     weights = filters(templates, all_channels, ORDER)
-    result = jnp.dot(weights, gathered, preferred_element_type=jnp.float32).reshape(
+    result = jnp.dot(weights, images, preferred_element_type=jnp.float32).reshape(
         weights.shape[0], lines, columns
     )
     spread = jnp.sqrt(power_sum / (all_channels * points * points) + epsilon)

time: 201 us -> 134 us (0.67)
  blocking collectives: 102 us -> 0 us
  waiting for transfers between devices: 11.4 us -> 35.8 us
  starting transfers between devices: 24.1 us -> 29.3 us
  other arithmetic: 12.7 us -> 16.1 us
    psum x1 -> x0, blocking collectives: 102 us -> none  [body(): power_sum = lax.psum(jnp.sum(widened * widened), ('freq', 'sky'))]
    all_to_all x1, waiting for transfers between devices: 0.01 us -> 17 us  [body(): gathered = lax.all_to_all(outgoing, 'freq', 0, 0, tiled=True)]
    all_to_all x0 -> x1, waiting for transfers between devices: none -> 7.37 us  [body(): lax.all_to_all(jnp.broadcast_to(power_freq, (sky_count, 128)), 'sky', 0,...]
    all_to_all x0 -> x1, starting transfers between devices: none -> 5.3 us  [body(): lax.all_to_all(jnp.broadcast_to(power_freq, (sky_count, 128)), 'sky', 0,...]
    reshape x2, local copies, waits for them, and re-layouts: 0.92 us -> 3.73 us  [body(): spectra.reshape(freq_count, lines, channels, columns)]
    all_to_all x0 -> x2, other arithmetic: none -> 2.18 us  [body(): gathered = lax.all_to_all(outgoing, 'freq', 0, 0, tiled=True)]
    unnamed x16 -> x17, local copies, waits for them, and re-layouts: 4.88 us -> 3.67 us
  transfers between devices with their start and end apart: 2 -> 3, of which waited for: 1 -> 3; matrix products, arithmetic and copies ran while one was open for 7% -> 12% of each run, Pallas kernels for 0% -> 0%
where the time goes in v1:
time: 134 us; the launch traced here: 133 us
  local copies, waits for them, and re-layouts  41.6 us (31%)
  waiting for transfers between devices  35.8 us (27%)
  starting transfers between devices  29.3 us (22%)
  other arithmetic  16.1 us (12%)
  matrix products  7.22 us (5%)
  between operations  2.84 us (2%)
    all_to_all x1, waiting for transfers between devices, body(): gathered = lax.all_to_all(outgoing, 'freq', 0, 0, tiled=True)  17 us
    all_to_all x1, starting transfers between devices, body(): turned = lax.all_to_all(send, 'sky', 0, 0, tiled=True)  14.1 us
    all_to_all x1, waiting for transfers between devices, body(): turned = lax.all_to_all(send, 'sky', 0, 0, tiled=True)  11.4 us
    all_to_all x1, starting transfers between devices, body(): gathered = lax.all_to_all(outgoing, 'freq', 0, 0, tiled=True)  9.92 us
    all_to_all x1, waiting for transfers between devices, body(): lax.all_to_all(jnp.broadcast_to(power_freq, (sky_count, 128)), 'sky', 0,...  7.37 us
    reshape x1, local copies, waits for them, and re-layouts, body(): jnp.transpose(stacked, (3, 0, 2, 1, 4))  6.17 us
    all_to_all x1, starting transfers between devices, body(): lax.all_to_all(jnp.broadcast_to(power_freq, (sky_count, 128)), 'sky', 0,...  5.3 us
    transpose x1, local copies, waits for them, and re-layouts, body(): jnp.transpose(stacked, (3, 0, 2, 1, 4))  4.63 us
  transfers between devices with their start and end apart: 3, of which 3 were waited for; matrix products, arithmetic and copies ran while one was open for 12% of the time, Pallas kernels for 0%

profile of v1, /device:TPU:1, one launch (start us, length us, event | category | flops | bytes accessed | tf_op | source)
XLA Modules:
  0.0 132.8 jit_solution(12869016322855499342)
XLA Ops:
  1.8 1.6 %multiply_convert_fusion = (bf16[32,32,1024]{2,1,0:T(8,128)(2,1)S(1)}, bf16[32,32,1024]{2,1,0:T(8,128)(2,1)S(1)}) fusion(f32[32,1024]{1,0:T(8,128)S(1)} %get-tuple-element.64, f32[32,1024]{1,0:T(8,128)S(1)} %get-tuple-element.61, f32[32,1024]{1,0:T(8,128)S(1)} %get-tuple-element.65, f32[32,1024]{1,0:T(8,128)S(1)} %get-tuple-element.60), kind=kLoop, calls=%fused_computation.2 | loop fusion | flops 10485760 | bytes 4718592 | tf_op jit(solution)/shard_map/convert_element_type | solution.py:29
  5.9 1.3 fusion.5
  7.2 3.7 %convert_element_type.116 = bf16[1,8,32,32,32]{4,3,2,1,0:T(8,128)(2,1)} reshape(bf16[8,1,32,1024]{3,2,0,1:T(8,128)(2,1)} %get-tuple-element.56) | data formatting | bytes 1048576 | tf_op jit(solution)/shard_map/convert_element_type | solution.py:88
  10.9 3.7 %convert_element_type.118 = bf16[1,8,32,32,32]{4,3,2,1,0:T(8,128)(2,1)} reshape(bf16[8,1,32,1024]{3,2,0,1:T(8,128)(2,1)} %get-tuple-element.57) | data formatting | bytes 1048576 | tf_op jit(solution)/shard_map/convert_element_type | solution.py:89
  14.6 3.2 %maximum_bitcast_fusion = bf16[32,2,32,8,32]{4,0,2,3,1:T(8,128)(2,1)S(1)} fusion(bf16[1,8,32,32,32]{4,3,2,1,0:T(8,128)(2,1)} %convert_element_type.118, bf16[1,8,32,32,32]{4,3,2,1,0:T(8,128)(2,1)} %convert_element_type.116), kind=kLoop, calls=%fused_computation.1 | loop fusion | flops 524288 | bytes 2097152 | tf_op jit(solution)/shard_map/transpose | solution.py:92
  17.8 4.6 %copy.75 = bf16[32,2,32,8,32]{4,3,2,1,0:T(8,128)(2,1)} copy(bf16[32,2,32,8,32]{4,0,2,3,1:T(8,128)(2,1)S(1)} %maximum_bitcast_fusion) | data formatting | bytes 2097152 | tf_op jit(solution)/shard_map/transpose | solution.py:92
  22.4 6.2 %reshape.337 = bf16[32,2,32,256]{3,2,1,0:T(8,128)(2,1)} reshape(bf16[32,2,32,8,32]{4,3,2,1,0:T(8,128)(2,1)} %copy.75) | data formatting | bytes 2097152 | tf_op jit(solution)/shard_map/reshape | solution.py:92
  28.6 14.1 %all-to-all-start = ((bf16[32,2,32,256]{3,2,1,0:T(8,128)(2,1)}), bf16[32,2,32,256]{3,2,1,0:T(8,128)(2,1)}, u32[]{:S(2)}, u32[]{:S(2)}) async-start(bf16[32,2,32,256]{3,2,1,0:T(8,128)(2,1)} %reshape.337), calls=%async_computation | async-start | bytes 2097152 | tf_op jit(solution)/shard_map/all_to_all | solution.py:95
  42.7 3.4 %neg.13 = bf16[1024,1024]{1,0:T(8,128)(2,1)} negate(bf16[1024,1024]{1,0:T(8,128)(2,1)} %bitcast.81) | non-fusion elementwise | flops 1048576 | bytes 4194304 | tf_op jit(solution)/shard_map/neg | solution.py:101
  46.1 2.5 %copy.68 = bf16[1024,1024]{0,1:T(8,128)(2,1)} copy(bf16[1024,1024]{1,0:T(8,128)(2,1)S(1)} %bitcast.79) | data formatting | bytes 4194304 | tf_op jit(solution)/shard_map/optimization_barrier | solution.py:30
  48.6 4.1 %copy.69 = bf16[1024,1024]{0,1:T(8,128)(2,1)} copy(bf16[1024,1024]{1,0:T(8,128)(2,1)} %neg.13) | data formatting | bytes 4194304 | tf_op jit(solution)/shard_map/neg | solution.py:101
  52.7 2.0 %pad_maximum_fusion = bf16[1024,32,2,32]{0,3,1,2:T(8,128)(2,1)S(1)} fusion(bf16[1024,32,1,32]{0,3,1,2:T(8,128)(2,1)} %bitcast.83, bf16[1024,32,1,32]{0,3,1,2:T(8,128)(2,1)S(1)} %bitcast.82), kind=kLoop, calls=%fused_computation | loop fusion | flops 2097152 | bytes 8388608 | tf_op jit(solution)/shard_map/stack | solution.py:98
  54.7 2.4 %copy.70 = bf16[1024,32,2,32]{0,3,2,1:T(8,128)(2,1)} copy(bf16[1024,32,2,32]{0,3,1,2:T(8,128)(2,1)S(1)} %pad_maximum_fusion) | data formatting | bytes 8388608 | tf_op jit(solution)/shard_map/stack | solution.py:98
  57.2 11.4 %all-to-all-done = bf16[32,2,32,256]{3,2,1,0:T(8,128)(2,1)} async-done(((bf16[32,2,32,256]{3,2,1,0:T(8,128)(2,1)}), bf16[32,2,32,256]{3,2,1,0:T(8,128)(2,1)}, u32[]{:S(2)}, u32[]{:S(2)}) %all-to-all-start) | async-done | bytes 1048608 | tf_op jit(solution)/shard_map/all_to_all | solution.py:95
  68.6 1.5 %copy.76 = bf16[256,2048]{1,0:T(8,128)(2,1)S(1)} copy(bf16[256,2048]{0,1:T(8,128)(2,1)} %bitcast.15) | data formatting | bytes 2097152 | tf_op jit(solution)/shard_map/dot_general | solution.py:105
  70.1 4.2 %multiply_reduce_fusion = (f32[]{:T(128)}, bf16[1024,8,32]{0,2,1:T(8,128)(2,1)S(1)}) fusion(bf16[1024,2048,1]{0,1,2:T(8,128)(2,1)} %bitcast.84, bf16[8,32,2048]{2,1,0:T(8,128)(2,1)S(1)} %bitcast.89, f32[1024,32]{0,1:T(8,128)S(1)} %add_multiply_fusion, f32[8]{0:T(128)S(1)} %multiply_multiply_fusion), kind=kOutput, calls=%fused_computation.16 | convolution fusion | flops 1075314688 | bytes 5898276 | tf_op jit(solution)/shard_map/dot_general | solution.py:105
  75.6 1.6 %reshape.339 = bf16[16,64,8,32]{1,0,3,2:T(8,128)(2,1)} reshape(bf16[1024,8,32]{0,2,1:T(8,128)(2,1)S(1)} %get-tuple-element.63) | data formatting | bytes 1048576 | tf_op jit(solution)/shard_map/reshape | solution.py:123
  77.3 2.1 %copy.78 = bf16[16,64,8,32]{3,1,2,0:T(8,128)(2,1)S(1)} copy(bf16[16,64,8,32]{1,0,3,2:T(8,128)(2,1)} %reshape.339) | data formatting | bytes 1048576 | tf_op jit(solution)/shard_map/reshape | solution.py:123
  79.4 3.0 %reshape.340 = bf16[16,16384]{1,0:T(8,128)(2,1)} reshape(bf16[16,8,64,32]{3,2,1,0:T(8,128)(2,1)S(1)} %bitcast.77) | data formatting | bytes 1048576 | tf_op jit(solution)/shard_map/reshape | solution.py:124
  86.5 9.9 %all-to-all-start.1 = ((bf16[16,2,8256]{2,1,0:T(2,128)(2,1)}), bf16[16,2,8256]{2,1,0:T(2,128)(2,1)S(1)}, u32[]{:S(2)}, u32[]{:S(2)}) async-start(bf16[16,2,8256]{2,1,0:T(2,128)(2,1)} %reshape.346), calls=%async_computation.1 | async-start | bytes 1064960 | tf_op jit(solution)/shard_map/all_to_all | solution.py:133
  96.7 17.0 %all-to-all-done.1 = bf16[16,2,8256]{2,1,0:T(2,128)(2,1)S(1)} async-done(((bf16[16,2,8256]{2,1,0:T(2,128)(2,1)}), bf16[16,2,8256]{2,1,0:T(2,128)(2,1)S(1)}, u32[]{:S(2)}, u32[]{:S(2)}) %all-to-all-start.1) | async-done | bytes 528416 | tf_op jit(solution)/shard_map/all_to_all | solution.py:133
  115.3 1.3 broadcast_in_dim.8
  116.6 5.3 %all-to-all-start.2 = ((f32[32,1,128]{2,1,0:T(1,128)}), f32[32,1,128]{2,1,0:T(1,128)S(1)}, u32[]{:S(2)}, u32[]{:S(2)}) async-start(f32[32,1,128]{2,1,0:T(1,128)} %broadcast_in_dim.8), calls=%async_computation.2 | async-start | bytes 32768 | tf_op jit(solution)/shard_map/all_to_all | solution.py:137
  123.1 7.4 %all-to-all-done.2 = f32[32,1,128]{2,1,0:T(1,128)S(1)} async-done(((f32[32,1,128]{2,1,0:T(1,128)}), f32[32,1,128]{2,1,0:T(1,128)S(1)}, u32[]{:S(2)}, u32[]{:S(2)}) %all-to-all-start.2) | async-done | bytes 16416 | tf_op jit(solution)/shard_map/all_to_all | solution.py:137
  (44 shorter events, 12.7 us)
Async XLA Ops:
  0.6 2.7 %copy-start = (bf16[8,2,32,1024]{3,2,1,0:T(8,128)(2,1)S(1)}, bf16[8,2,32,1024]{3,2,1,0:T(8,128)(2,1)}, u32[]{:S(2)}) copy-start(bf16[8,2,32,1024]{3,2,1,0:T(8,128)(2,1)} %param.9) | copy-start | bytes 3145732
  3.4 1.3 copy-start.1
  28.6 40.0 %all-to-all-start = ((bf16[32,2,32,256]{3,2,1,0:T(8,128)(2,1)}), bf16[32,2,32,256]{3,2,1,0:T(8,128)(2,1)}, u32[]{:S(2)}, u32[]{:S(2)}) async-start(bf16[32,2,32,256]{3,2,1,0:T(8,128)(2,1)} %reshape.337), calls=%async_computation | async-start | bytes 2097152 | tf_op jit(solution)/shard_map/all_to_all | solution.py:95
  48.6 4.1 %copy-start.2 = (bf16[1024,1024]{0,1:T(8,128)(2,1)S(1)}, bf16[1024,1024]{0,1:T(8,128)(2,1)}, u32[]{:S(2)}) copy-start(bf16[1024,1024]{0,1:T(8,128)(2,1)} %copy.68) | copy-start | bytes 6291460
  82.6 13.8 %copy-start.3 = (f32[16,128]{1,0:T(8,128)S(1)}, f32[16,128]{1,0:T(8,128)}, u32[]{:S(2)}) copy-start(f32[16,128]{1,0:T(8,128)} %param.10) | copy-start | bytes 24580
  82.6 13.8 %copy-start.4 = (f32[9,128]{1,0:T(8,128)S(1)}, f32[9,128]{1,0:T(8,128)}, u32[]{:S(2)}) copy-start(f32[9,128]{1,0:T(8,128)} %constant.137.clone) | copy-start | bytes 13828
  86.5 27.3 %all-to-all-start.1 = ((bf16[16,2,8256]{2,1,0:T(2,128)(2,1)}), bf16[16,2,8256]{2,1,0:T(2,128)(2,1)S(1)}, u32[]{:S(2)}, u32[]{:S(2)}) async-start(bf16[16,2,8256]{2,1,0:T(2,128)(2,1)} %reshape.346), calls=%async_computation.1 | async-start | bytes 1064960 | tf_op jit(solution)/shard_map/all_to_all | solution.py:133
  114.4 7.6 %copy-start.5 = (bf16[9,128]{1,0:T(8,128)(2,1)S(1)}, bf16[9,128]{1,0:T(8,128)(2,1)}, u32[]{:S(2)}) copy-start(bf16[9,128]{1,0:T(8,128)(2,1)} %constant.141) | copy-start | bytes 6916
  116.6 13.8 %all-to-all-start.2 = ((f32[32,1,128]{2,1,0:T(1,128)}), f32[32,1,128]{2,1,0:T(1,128)S(1)}, u32[]{:S(2)}, u32[]{:S(2)}) async-start(f32[32,1,128]{2,1,0:T(1,128)} %broadcast_in_dim.8), calls=%async_computation.2 | async-start | bytes 32768 | tf_op jit(solution)/shard_map/all_to_all | solution.py:137

commit v2 on v1

--- a/solution.py
+++ b/solution.py
@@ -11,7 +11,7 @@
 epsilon = 1e-06
 
 
-def tables(points):
+def tables(points, sources, depth):
     block = 32
     index = jnp.arange(points, dtype=jnp.int32)
     step = jnp.arange(block, dtype=jnp.int32)
@@ -27,7 +27,18 @@
     sin = high_s[:, None, :] * low_c[None, :, :] + high_c[:, None, :] * low_s[None, :, :]
     cos = (cos * factor).astype(jnp.bfloat16).reshape(points, points)
     sin = (sin * factor).astype(jnp.bfloat16).reshape(points, points)
-    return lax.optimization_barrier((cos, sin))
+
+    def spread(x):
+        x = x.reshape(block, sources, 1, depth)
+        return jnp.concatenate([x, x], axis=2).reshape(block, sources * 2 * depth)
+
+    part = (jnp.arange(sources * 2 * depth, dtype=jnp.int32) // depth) % 2 == 0
+    hc, hs, lc, ls = spread(high_c), spread(high_s), spread(low_c), spread(low_s)
+    first = jnp.where(part[None, :], hc, -hs)
+    second = jnp.where(part[None, :], -hs, -hc)
+    table = first[:, None, :] * lc[None, :, :] + second[:, None, :] * ls[None, :, :]
+    table = (table * factor).astype(jnp.bfloat16).reshape(points, sources * 2 * depth)
+    return lax.optimization_barrier((cos, sin)) + (lax.optimization_barrier(table),)
 
 
 def distances(row_pos, col_pos, points):
@@ -76,7 +87,7 @@
     all_channels = channels * freq_count
     columns = points // sky_count
     lines = points // freq_count
-    cosine, sine = tables(points)
+    cosine, sine, table = tables(points, sky_count, row_count)
 
     rows = visibilities.reshape(channels * 2 * row_count, points)
     with_cos = jnp.dot(rows, cosine, preferred_element_type=jnp.float32).reshape(
@@ -95,13 +106,6 @@
     turned = lax.all_to_all(send, "sky", 0, 0, tiled=True)
     turned = turned.reshape(sky_count * 2 * row_count, channels * columns)
 
-    table = jnp.stack(
-        [
-            cosine.reshape(points, sky_count, row_count),
-            -sine.reshape(points, sky_count, row_count),
-        ],
-        axis=2,
-    ).reshape(points, sky_count * 2 * row_count)
     picture = jnp.dot(table, turned, preferred_element_type=jnp.float32).reshape(
         points, channels, columns
     )
@@ -119,28 +123,29 @@
     widened = spectra.astype(jnp.float32)
     power_part = jnp.sum(widened * widened)
 
-    outgoing = jnp.transpose(
-        spectra.reshape(freq_count, lines, channels, columns), (0, 2, 1, 3)
-    ).reshape(freq_count, channels * lines * columns)
     high = power_part.astype(jnp.bfloat16)
     rest = power_part - high.astype(jnp.float32)
     middle = rest.astype(jnp.bfloat16)
     low = (rest - middle.astype(jnp.float32)).astype(jnp.bfloat16)
-    pieces = jnp.zeros((128,), jnp.bfloat16).at[0].set(high).at[1].set(middle).at[2].set(low)
+    pieces = jnp.zeros((channels * columns,), jnp.bfloat16)
+    pieces = pieces.at[0].set(high).at[1].set(middle).at[2].set(low)
     outgoing = jnp.concatenate(
-        [outgoing, jnp.broadcast_to(pieces[None, :], (freq_count, 128))], axis=1
+        [
+            spectra.reshape(freq_count, lines, channels * columns),
+            jnp.broadcast_to(pieces, (freq_count, 1, channels * columns)),
+        ],
+        axis=1,
     )
     gathered = lax.all_to_all(outgoing, "freq", 0, 0, tiled=True)
-    shares = gathered[:, channels * lines * columns :][:, :3].astype(jnp.float32)
-    power_freq = jnp.sum(shares)
-    images = gathered[:, : channels * lines * columns].reshape(all_channels, lines * columns)
+    power_freq = jnp.sum(gathered[:, lines, :3].astype(jnp.float32))
     column_power = lax.all_to_all(
         jnp.broadcast_to(power_freq, (sky_count, 128)), "sky", 0, 0, tiled=True
     )
     power_sum = jnp.sum(column_power[:, 0])
-    weights = filters(templates, all_channels, ORDER)
-    result = jnp.dot(weights, images, preferred_element_type=jnp.float32).reshape(
-        weights.shape[0], lines, columns
+    images = gathered[:, :lines].reshape(freq_count, lines, channels, columns)
+    weights = filters(templates, all_channels, ORDER).reshape(-1, freq_count, channels)
+    result = jnp.einsum(
+        "kfc,flcm->klm", weights, images, preferred_element_type=jnp.float32
     )
     spread = jnp.sqrt(power_sum / (all_channels * points * points) + epsilon)
     return (result[:num_templates] / spread, result[num_templates:])

time: 134 us -> 125 us (0.933)
  waiting for transfers between devices: 35.8 us -> 29.1 us
  local copies, waits for them, and re-layouts: 41.6 us -> 35.6 us
  other arithmetic: 16.1 us -> 20.1 us
    all_to_all x1, waiting for transfers between devices: 11.4 us -> 4.06 us  [body(): turned = lax.all_to_all(send, 'sky', 0, 0, tiled=True)]
    cos x0 -> x1, other arithmetic: none -> 4.98 us  [tables(): low_c = jnp.cos(scale * low.astype(jnp.float32))]
    reshape x4 -> x2, local copies, waits for them, and re-layouts: 6.94 us -> 2.71 us  [the longest x1 2.05 us: spread(): return jnp.concatenate([x, x], axis=2).reshape(block, sources * 2 * depth)]
    concatenate x1 -> x5, local copies, waits for them, and re-layouts: 0.01 us -> 4.09 us  [the longest x3 2.51 us: spread(): return jnp.concatenate([x, x], axis=2).reshape(block, sources * 2 * depth)]
    convert_element_type x0 -> x1, other arithmetic: none -> 3.56 us  [tables(): (table * factor).astype(jnp.bfloat16).reshape(points, sources * 2 * depth)]
    neg x1 -> x0, other arithmetic: 3.44 us -> none  [body(): -sine.reshape(points, sky_count, row_count)]
    mul x0 -> x2, local copies, waits for them, and re-layouts: none -> 2.7 us  [the longest x1 1.35 us: tables(): first[:, None, :] * lc[None, :, :] + second[:, None, :] * ls[None, :, :]]
    optimization_barrier x1 -> x0, local copies, waits for them, and re-layouts: 2.53 us -> none  [tables(): return lax.optimization_barrier((cos, sin))]
  transfers between devices with their start and end apart: 3 -> 3, of which waited for: 3 -> 3; matrix products, arithmetic and copies ran while one was open for 12% -> 19% of each run, Pallas kernels for 0% -> 0%
where the time goes in v2:
time: 125 us
  local copies, waits for them, and re-layouts  35.6 us (28%)
  starting transfers between devices  29.3 us (23%)
  waiting for transfers between devices  29.1 us (23%)
  other arithmetic  20.1 us (16%)
  matrix products  7.75 us (6%)
  between operations  2.9 us (2%)
    all_to_all x1, waiting for transfers between devices, body(): gathered = lax.all_to_all(outgoing, 'freq', 0, 0, tiled=True)  18 us
    all_to_all x1, starting transfers between devices, body(): turned = lax.all_to_all(send, 'sky', 0, 0, tiled=True)  14.1 us
    all_to_all x1, starting transfers between devices, body(): gathered = lax.all_to_all(outgoing, 'freq', 0, 0, tiled=True)  9.92 us
    all_to_all x1, waiting for transfers between devices, body(): lax.all_to_all(jnp.broadcast_to(power_freq, (sky_count, 128)), 'sky', 0,...  7.04 us
    reshape x1, local copies, waits for them, and re-layouts, body(): jnp.transpose(stacked, (3, 0, 2, 1, 4))  6.17 us
    all_to_all x1, starting transfers between devices, body(): lax.all_to_all(jnp.broadcast_to(power_freq, (sky_count, 128)), 'sky', 0,...  5.3 us
    cos x1, other arithmetic, tables(): low_c = jnp.cos(scale * low.astype(jnp.float32))  4.98 us
    transpose x1, local copies, waits for them, and re-layouts, body(): jnp.transpose(stacked, (3, 0, 2, 1, 4))  4.65 us
  transfers between devices with their start and end apart: 3, of which 3 were waited for; matrix products, arithmetic and copies ran while one was open for 19% of the time, Pallas kernels for 0%

profile of v2, /device:TPU:1, one launch (start us, length us, event | category | flops | bytes accessed | tf_op | source)
XLA Modules:
  0.0 124.7 jit_solution(4354882076451423936)
XLA Ops:
  1.8 1.6 %multiply_convert_fusion.1 = (bf16[32,32,1024]{2,1,0:T(8,128)(2,1)S(1)}, bf16[32,32,1024]{2,1,0:T(8,128)(2,1)S(1)}) fusion(f32[32,1024]{1,0:T(8,128)S(1)} %get-tuple-element.74, f32[32,1024]{1,0:T(8,128)S(1)} %get-tuple-element.71, f32[32,1024]{1,0:T(8,128)S(1)} %get-tuple-element.75, f32[32,1024]{1,0:T(8,128)S(1)} %get-tuple-element.70), kind=kLoop, calls=%fused_computation.4 | loop fusion | flops 10485760 | bytes 4718592 | tf_op jit(solution)/shard_map/convert_element_type | solution.py:29
  5.9 1.4 %fusion.12 = (bf16[8,1,32,1024]{3,2,0,1:T(8,128)(2,1)}, bf16[8,1,32,1024]{3,2,0,1:T(8,128)(2,1)}) fusion(f32[8,2,32,1024]{3,2,1,0:T(8,128)S(1)} %bitcast.84, f32[8,2,32,1024]{3,2,1,0:T(8,128)S(1)} %bitcast.85), kind=kLoop, calls=%fused_computation.17 | loop fusion | flops 1048576 | bytes 5242880 | tf_op jit(solution)/shard_map/convert_element_type | solution.py:99
  7.2 2.8 %convert_element_type.167 = bf16[1,8,32,32,32]{4,3,2,1,0:T(8,128)(2,1)S(1)} reshape(bf16[8,1,32,1024]{3,2,0,1:T(8,128)(2,1)} %get-tuple-element.58) | data formatting | bytes 1048576 | tf_op jit(solution)/shard_map/convert_element_type | solution.py:99
  10.1 3.7 %convert_element_type.169 = bf16[1,8,32,32,32]{4,3,2,1,0:T(8,128)(2,1)} reshape(bf16[8,1,32,1024]{3,2,0,1:T(8,128)(2,1)} %get-tuple-element.59) | data formatting | bytes 1048576 | tf_op jit(solution)/shard_map/convert_element_type | solution.py:100
  13.8 2.5 %maximum_bitcast_fusion = bf16[32,2,32,8,32]{4,0,2,3,1:T(8,128)(2,1)S(1)} fusion(bf16[1,8,32,32,32]{4,3,2,1,0:T(8,128)(2,1)} %convert_element_type.169, bf16[1,8,32,32,32]{4,3,2,1,0:T(8,128)(2,1)S(1)} %convert_element_type.167), kind=kLoop, calls=%fused_computation.1 | loop fusion | flops 524288 | bytes 2097152 | tf_op jit(solution)/shard_map/transpose | solution.py:103
  16.3 4.6 %copy.91 = bf16[32,2,32,8,32]{4,3,2,1,0:T(8,128)(2,1)} copy(bf16[32,2,32,8,32]{4,0,2,3,1:T(8,128)(2,1)S(1)} %maximum_bitcast_fusion) | data formatting | bytes 2097152 | tf_op jit(solution)/shard_map/transpose | solution.py:103
  21.0 6.2 %reshape.543 = bf16[32,2,32,256]{3,2,1,0:T(8,128)(2,1)} reshape(bf16[32,2,32,8,32]{4,3,2,1,0:T(8,128)(2,1)} %copy.91) | data formatting | bytes 2097152 | tf_op jit(solution)/shard_map/reshape | solution.py:103
  27.2 14.1 %all-to-all-start = ((bf16[32,2,32,256]{3,2,1,0:T(8,128)(2,1)}), bf16[32,2,32,256]{3,2,1,0:T(8,128)(2,1)}, u32[]{:S(2)}, u32[]{:S(2)}) async-start(bf16[32,2,32,256]{3,2,1,0:T(8,128)(2,1)} %reshape.543), calls=%async_computation | async-start | bytes 2097152 | tf_op jit(solution)/shard_map/all_to_all | solution.py:106
  41.2 5.0 %fusion.24 = (f32[32,32,1,32]{3,1,2,0:T(8,128)}, f32[32,32,1,32]{3,1,2,0:T(8,128)}, f32[32,32,1,32]{3,1,2,0:T(8,128)S(1)}, f32[32,32,1,32]{3,1,2,0:T(8,128)S(1)}) fusion(s32[32,32]{1,0:T(8,128)S(1)} %multiply_add_fusion, s32[32]{0:T(128)S(1)} %iota_multiply_fusion), kind=kLoop, calls=%fused_computation.46 | loop fusion | flops 917504 | bytes 528512 | tf_op jit(solution)/shard_map/cos | solution.py:24
  47.2 2.1 %neg.22 = f32[32,2048]{1,0:T(8,128)} reshape(f32[32,32,2,32]{3,2,1,0:T(2,128)S(1)} %copy.84) | data formatting | bytes 524288 | tf_op jit(solution)/shard_map/neg | solution.py:37
  50.1 2.1 %reshape.539 = f32[32,2048]{1,0:T(8,128)} reshape(f32[32,32,2,32]{3,2,1,0:T(2,128)S(1)} %copy.83) | data formatting | bytes 524288 | tf_op jit(solution)/shard_map/reshape | solution.py:33
  52.2 1.8 %pad_maximum_fusion.1 = (f32[32,32,2,32]{3,1,2,0:T(8,128)S(1)}, f32[32,32,2,32]{3,1,2,0:T(8,128)S(1)}) fusion(f32[32,32,1,32]{3,1,2,0:T(8,128)} %get-tuple-element.66, f32[32,32,1,32]{3,1,2,0:T(8,128)} %get-tuple-element.67), kind=kLoop, calls=%fused_computation.21 | loop fusion | flops 131072 | bytes 786432 | tf_op jit(solution)/shard_map/concatenate | solution.py:33
  54.8 1.4 %mul.429 = f32[32,2048]{1,0:T(8,128)S(1)} reshape(f32[32,32,2,32]{3,2,1,0:T(2,128)S(1)} %copy.85) | data formatting | bytes 524288 | tf_op jit(solution)/shard_map/mul | solution.py:39
  57.0 1.4 %mul.433 = f32[32,2048]{1,0:T(8,128)S(1)} reshape(f32[32,32,2,32]{3,2,1,0:T(2,128)S(1)} %copy.86) | data formatting | bytes 524288 | tf_op jit(solution)/shard_map/mul | solution.py:39
  59.4 3.6 %multiply_convert_fusion = bf16[32,32,2048]{2,1,0:T(8,128)(2,1)} fusion(f32[32,2048]{1,0:T(8,128)S(1)} %mul.433, f32[32,2048]{1,0:T(8,128)S(1)} %get-tuple-element.61, f32[32,2048]{1,0:T(8,128)S(1)} %mul.429, f32[32,2048]{1,0:T(8,128)S(1)} %get-tuple-element.60), kind=kLoop, calls=%fused_computation | loop fusion | flops 10485760 | bytes 5242880 | tf_op jit(solution)/shard_map/convert_element_type | solution.py:40
  63.1 4.1 %all-to-all-done = bf16[32,2,32,256]{3,2,1,0:T(8,128)(2,1)} async-done(((bf16[32,2,32,256]{3,2,1,0:T(8,128)(2,1)}), bf16[32,2,32,256]{3,2,1,0:T(8,128)(2,1)}, u32[]{:S(2)}, u32[]{:S(2)}) %all-to-all-start) | async-done | bytes 1048608 | tf_op jit(solution)/shard_map/all_to_all | solution.py:106
  67.2 1.7 %copy.92 = bf16[256,2048]{1,0:T(8,128)(2,1)S(1)} copy(bf16[256,2048]{0,1:T(8,128)(2,1)} %bitcast.15) | data formatting | bytes 2097152 | tf_op jit(solution)/shard_map/dot_general | solution.py:109
  68.9 4.2 %multiply_reduce_fusion = (f32[]{:T(128)}, bf16[1024,8,32]{0,2,1:T(8,128)(2,1)S(1)}) fusion(bf16[8,32,2048]{2,1,0:T(8,128)(2,1)S(1)} %bitcast.86, bf16[1024,2048]{1,0:T(8,128)(2,1)} %bitcast.80, f32[1024,32]{0,1:T(8,128)S(1)} %add_multiply_fusion, f32[8]{0:T(128)S(1)} %multiply_multiply_fusion), kind=kOutput, calls=%fused_computation.25 | convolution fusion | flops 1075314688 | bytes 5898276 | tf_op jit(solution)/shard_map/dot_general | solution.py:109
  76.3 1.6 %copy.93 = bf16[16,65,256]{2,1,0:T(8,128)(2,1)} copy(bf16[16,65,256]{1,0,2:T(8,128)(2,1)S(1)} %pad_maximum_fusion.3) | data formatting | bytes 1064960 | tf_op jit(solution)/shard_map/concatenate | solution.py:132
  77.9 9.9 %all-to-all-start.1 = ((bf16[16,65,256]{2,1,0:T(8,128)(2,1)}), bf16[16,65,256]{2,1,0:T(8,128)(2,1)S(1)}, u32[]{:S(2)}, u32[]{:S(2)}) async-start(bf16[16,65,256]{2,1,0:T(8,128)(2,1)} %copy.93), calls=%async_computation.1 | async-start | bytes 1179648 | tf_op jit(solution)/shard_map/all_to_all | solution.py:139
  88.3 18.0 %all-to-all-done.1 = bf16[16,65,256]{2,1,0:T(8,128)(2,1)S(1)} async-done(((bf16[16,65,256]{2,1,0:T(8,128)(2,1)}), bf16[16,65,256]{2,1,0:T(8,128)(2,1)S(1)}, u32[]{:S(2)}, u32[]{:S(2)}) %all-to-all-start.1) | async-done | bytes 532512 | tf_op jit(solution)/shard_map/all_to_all | solution.py:139
  107.5 1.3 %broadcast_in_dim.16 = f32[32,1,128]{2,1,0:T(1,128)} broadcast(f32[]{:T(128)} %fusion.49), dimensions={} | broadcast | bytes 16388 | tf_op jit(solution)/shard_map/broadcast_in_dim | solution.py:142
  108.7 5.3 %all-to-all-start.2 = ((f32[32,1,128]{2,1,0:T(1,128)}), f32[32,1,128]{2,1,0:T(1,128)S(1)}, u32[]{:S(2)}, u32[]{:S(2)}) async-start(f32[32,1,128]{2,1,0:T(1,128)} %broadcast_in_dim.16), calls=%async_computation.2 | async-start | bytes 32768 | tf_op jit(solution)/shard_map/all_to_all | solution.py:141
  115.5 7.0 %all-to-all-done.2 = f32[32,1,128]{2,1,0:T(1,128)S(1)} async-done(((f32[32,1,128]{2,1,0:T(1,128)}), f32[32,1,128]{2,1,0:T(1,128)S(1)}, u32[]{:S(2)}, u32[]{:S(2)}) %all-to-all-start.2) | async-done | bytes 16416 | tf_op jit(solution)/shard_map/all_to_all | solution.py:141
  (44 shorter events, 14.7 us)
Async XLA Ops:
  0.6 2.7 %copy-start = (bf16[8,2,32,1024]{3,2,1,0:T(8,128)(2,1)S(1)}, bf16[8,2,32,1024]{3,2,1,0:T(8,128)(2,1)}, u32[]{:S(2)}) copy-start(bf16[8,2,32,1024]{3,2,1,0:T(8,128)(2,1)} %param.9) | copy-start | bytes 3145732
  27.2 40.0 %all-to-all-start = ((bf16[32,2,32,256]{3,2,1,0:T(8,128)(2,1)}), bf16[32,2,32,256]{3,2,1,0:T(8,128)(2,1)}, u32[]{:S(2)}, u32[]{:S(2)}) async-start(bf16[32,2,32,256]{3,2,1,0:T(8,128)(2,1)} %reshape.543), calls=%async_computation | async-start | bytes 2097152 | tf_op jit(solution)/shard_map/all_to_all | solution.py:106
  74.4 13.4 %copy-start.2 = (f32[16,128]{1,0:T(8,128)S(1)}, f32[16,128]{1,0:T(8,128)}, u32[]{:S(2)}) copy-start(f32[16,128]{1,0:T(8,128)} %param.10) | copy-start | bytes 24580
  74.4 13.4 %copy-start.3 = (f32[9,128]{1,0:T(8,128)S(1)}, f32[9,128]{1,0:T(8,128)}, u32[]{:S(2)}) copy-start(f32[9,128]{1,0:T(8,128)} %constant.180.clone) | copy-start | bytes 13828
  75.7 38.4 %copy-start.1 = (bf16[9,16,8]{0,1,2:T(8,128)(2,1)S(1)}, bf16[9,16,8]{0,1,2:T(8,128)(2,1)}, u32[]{:S(2)}) copy-start(bf16[9,16,8]{0,1,2:T(8,128)(2,1)} %constant.185) | copy-start | bytes 6916
  77.9 28.5 %all-to-all-start.1 = ((bf16[16,65,256]{2,1,0:T(8,128)(2,1)}), bf16[16,65,256]{2,1,0:T(8,128)(2,1)S(1)}, u32[]{:S(2)}, u32[]{:S(2)}) async-start(bf16[16,65,256]{2,1,0:T(8,128)(2,1)} %copy.93), calls=%async_computation.1 | async-start | bytes 1179648 | tf_op jit(solution)/shard_map/all_to_all | solution.py:139
  108.7 13.8 %all-to-all-start.2 = ((f32[32,1,128]{2,1,0:T(1,128)}), f32[32,1,128]{2,1,0:T(1,128)S(1)}, u32[]{:S(2)}, u32[]{:S(2)}) async-start(f32[32,1,128]{2,1,0:T(1,128)} %broadcast_in_dim.16), calls=%async_computation.2 | async-start | bytes 32768 | tf_op jit(solution)/shard_map/all_to_all | solution.py:141

commit v3 on v2

--- a/solution.py
+++ b/solution.py
@@ -89,18 +89,17 @@
     lines = points // freq_count
     cosine, sine, table = tables(points, sky_count, row_count)
 
-    rows = visibilities.reshape(channels * 2 * row_count, points)
-    with_cos = jnp.dot(rows, cosine, preferred_element_type=jnp.float32).reshape(
-        channels, 2, row_count, points
+    with_cos = jnp.einsum(
+        "vm,cpuv->mcpu", cosine, visibilities, preferred_element_type=jnp.float32
     )
-    with_sin = jnp.dot(rows, sine, preferred_element_type=jnp.float32).reshape(
-        channels, 2, row_count, points
+    with_sin = jnp.einsum(
+        "vm,cpuv->mcpu", sine, visibilities, preferred_element_type=jnp.float32
     )
-    section_real = (with_cos[:, 0] - with_sin[:, 1]).astype(jnp.bfloat16)
-    section_imag = (with_sin[:, 0] + with_cos[:, 1]).astype(jnp.bfloat16)
-    stacked = jnp.stack([section_real, section_imag])
-    stacked = stacked.reshape(2, channels, row_count, sky_count, columns)
-    send = jnp.transpose(stacked, (3, 0, 2, 1, 4)).reshape(
+    section_real = (with_cos[:, :, 0] - with_sin[:, :, 1]).astype(jnp.bfloat16)
+    section_imag = (with_sin[:, :, 0] + with_cos[:, :, 1]).astype(jnp.bfloat16)
+    stacked = jnp.stack([section_real, section_imag], axis=2)
+    stacked = stacked.reshape(sky_count, columns, channels, 2, row_count)
+    send = jnp.transpose(stacked, (0, 3, 4, 2, 1)).reshape(
         sky_count, 2, row_count, channels * columns
     )
     turned = lax.all_to_all(send, "sky", 0, 0, tiled=True)

time: 125 us -> 124 us (level)
  local copies, waits for them, and re-layouts: 35.6 us -> 34.3 us
    another operation x1 -> x5, local copies, waits for them, and re-layouts: 0.13 us -> 9.85 us  [the longest x4 9.73 us: body(): stacked = jnp.stack([section_real, section_imag], axis=2)]
    convert_element_type x2 -> x0, local copies, waits for them, and re-layouts: 6.57 us -> none  [the longest x1 3.73 us: body(): section_imag = (with_sin[:, 0] + with_cos[:, 1]).astype(jnp.bfloat16)]
    transpose x1 -> x0, local copies, waits for them, and re-layouts: 4.65 us -> none  [body(): jnp.transpose(stacked, (3, 0, 2, 1, 4))]
where the time goes in v3:
time: 124 us
  local copies, waits for them, and re-layouts  34.3 us (28%)
  starting transfers between devices  29.3 us (24%)
  waiting for transfers between devices  29.2 us (24%)
  other arithmetic  20.3 us (16%)
  matrix products  7.75 us (6%)
  between operations  2.93 us (2%)
    all_to_all x1, waiting for transfers between devices, body(): gathered = lax.all_to_all(outgoing, 'freq', 0, 0, tiled=True)  18 us
    all_to_all x1, starting transfers between devices, body(): turned = lax.all_to_all(send, 'sky', 0, 0, tiled=True)  14 us
    all_to_all x1, starting transfers between devices, body(): gathered = lax.all_to_all(outgoing, 'freq', 0, 0, tiled=True)  9.92 us
    another operation x4, local copies, waits for them, and re-layouts, body(): stacked = jnp.stack([section_real, section_imag], axis=2)  9.73 us
    all_to_all x1, waiting for transfers between devices, body(): lax.all_to_all(jnp.broadcast_to(power_freq, (sky_count, 128)), 'sky', 0,...  7.04 us
    reshape x1, local copies, waits for them, and re-layouts, body(): jnp.transpose(stacked, (0, 3, 4, 2, 1))  6.16 us
    all_to_all x1, starting transfers between devices, body(): lax.all_to_all(jnp.broadcast_to(power_freq, (sky_count, 128)), 'sky', 0,...  5.3 us
    cos x1, other arithmetic, tables(): low_c = jnp.cos(scale * low.astype(jnp.float32))  4.96 us
  transfers between devices with their start and end apart: 3, of which 3 were waited for; matrix products, arithmetic and copies ran while one was open for 19% of the time, Pallas kernels for 0%

profile of v3, /device:TPU:1, one launch (start us, length us, event | category | flops | bytes accessed | tf_op | source)
XLA Modules:
  0.0 123.6 jit_solution(1780778909586662990)
XLA Ops:
  1.8 1.6 %multiply_convert_fusion.1 = (bf16[32,32,1024]{2,1,0:T(8,128)(2,1)S(1)}, bf16[32,32,1024]{2,1,0:T(8,128)(2,1)S(1)}) fusion(f32[32,1024]{1,0:T(8,128)S(1)} %get-tuple-element.72, f32[32,1024]{1,0:T(8,128)S(1)} %get-tuple-element.69, f32[32,1024]{1,0:T(8,128)S(1)} %get-tuple-element.73, f32[32,1024]{1,0:T(8,128)S(1)} %get-tuple-element.68), kind=kLoop, calls=%fused_computation.4 | loop fusion | flops 10485760 | bytes 4718592 | tf_op jit(solution)/shard_map/convert_element_type | solution.py:29
  5.9 1.3 %fusion.14 = (bf16[1024,8,1,32]{0,3,2,1:T(8,128)(2,1)}, bf16[1024,8,1,32]{0,3,2,1:T(8,128)(2,1)}) fusion(f32[1024,8,2,32]{0,3,2,1:T(8,128)S(1)} %fusion.2, f32[1024,8,2,32]{0,3,2,1:T(8,128)S(1)} %fusion.4), kind=kLoop, calls=%fused_computation.18 | loop fusion | flops 1048576 | bytes 5242880 | tf_op jit(solution)/shard_map/convert_element_type | solution.py:98
  7.2 2.8 %stack.9 = bf16[32,32,8,1,32]{1,0,4,2,3:T(8,128)(2,1)S(1)} reshape(bf16[1024,8,1,32]{0,3,2,1:T(8,128)(2,1)} %get-tuple-element.56) | data formatting | bytes 1048576 | tf_op jit(solution)/shard_map/stack | solution.py:100
  10.0 2.7 %copy.65 = bf16[32,32,8,1,32]{1,2,4,3,0:T(8,128)(2,1)} copy(bf16[32,32,8,1,32]{1,0,4,2,3:T(8,128)(2,1)S(1)} %stack.9) | data formatting | bytes 1048576 | tf_op jit(solution)/shard_map/stack | solution.py:100
  12.7 2.8 %stack.10 = bf16[32,32,8,1,32]{1,0,4,2,3:T(8,128)(2,1)S(1)} reshape(bf16[1024,8,1,32]{0,3,2,1:T(8,128)(2,1)} %get-tuple-element.57) | data formatting | bytes 1048576 | tf_op jit(solution)/shard_map/stack | solution.py:100
  15.6 1.4 %copy.66 = bf16[32,32,8,1,32]{1,2,4,3,0:T(8,128)(2,1)S(1)} copy(bf16[32,32,8,1,32]{1,0,4,2,3:T(8,128)(2,1)S(1)} %stack.10) | data formatting | bytes 1048576 | tf_op jit(solution)/shard_map/stack | solution.py:100
  17.2 2.8 %maximum_bitcast_fusion = bf16[32,2,32,8,32]{4,3,2,1,0:T(8,128)(2,1)} fusion(bf16[32,32,8,1,32]{1,2,4,3,0:T(8,128)(2,1)S(1)} %copy.66, bf16[32,32,8,1,32]{1,2,4,3,0:T(8,128)(2,1)S(1)} %copy-done.1), kind=kLoop, calls=%fused_computation.1 | loop fusion | flops 524288 | bytes 2097152 | tf_op jit(solution)/shard_map/transpose | solution.py:102
  19.9 6.2 %reshape.483 = bf16[32,2,32,256]{3,2,1,0:T(8,128)(2,1)} reshape(bf16[32,2,32,8,32]{4,3,2,1,0:T(8,128)(2,1)} %maximum_bitcast_fusion) | data formatting | bytes 2097152 | tf_op jit(solution)/shard_map/reshape | solution.py:102
  26.1 14.0 %all-to-all-start = ((bf16[32,2,32,256]{3,2,1,0:T(8,128)(2,1)}), bf16[32,2,32,256]{3,2,1,0:T(8,128)(2,1)}, u32[]{:S(2)}, u32[]{:S(2)}) async-start(bf16[32,2,32,256]{3,2,1,0:T(8,128)(2,1)} %reshape.483), calls=%async_computation | async-start | bytes 2097152 | tf_op jit(solution)/shard_map/all_to_all | solution.py:105
  40.2 5.0 %fusion.26 = (f32[32,32,1,32]{3,1,2,0:T(8,128)}, f32[32,32,1,32]{3,1,2,0:T(8,128)}, f32[32,32,1,32]{3,1,2,0:T(8,128)S(1)}, f32[32,32,1,32]{3,1,2,0:T(8,128)S(1)}) fusion(s32[32,32]{1,0:T(8,128)S(1)} %multiply_add_fusion, s32[32]{0:T(128)S(1)} %iota_multiply_fusion), kind=kLoop, calls=%fused_computation.46 | loop fusion | flops 917504 | bytes 528512 | tf_op jit(solution)/shard_map/cos | solution.py:24
  46.2 2.1 %neg.22 = f32[32,2048]{1,0:T(8,128)} reshape(f32[32,32,2,32]{3,2,1,0:T(2,128)S(1)} %copy.62) | data formatting | bytes 524288 | tf_op jit(solution)/shard_map/neg | solution.py:37
  49.1 2.1 %reshape.482 = f32[32,2048]{1,0:T(8,128)} reshape(f32[32,32,2,32]{3,2,1,0:T(2,128)S(1)} %copy.61) | data formatting | bytes 524288 | tf_op jit(solution)/shard_map/reshape | solution.py:33
  51.1 1.8 %pad_maximum_fusion.1 = (f32[32,32,2,32]{3,1,2,0:T(8,128)S(1)}, f32[32,32,2,32]{3,1,2,0:T(8,128)S(1)}) fusion(f32[32,32,1,32]{3,1,2,0:T(8,128)} %get-tuple-element.64, f32[32,32,1,32]{3,1,2,0:T(8,128)} %get-tuple-element.65), kind=kLoop, calls=%fused_computation.21 | loop fusion | flops 131072 | bytes 786432 | tf_op jit(solution)/shard_map/concatenate | solution.py:33
  53.7 1.4 %mul.429 = f32[32,2048]{1,0:T(8,128)S(1)} reshape(f32[32,32,2,32]{3,2,1,0:T(2,128)S(1)} %copy.63) | data formatting | bytes 524288 | tf_op jit(solution)/shard_map/mul | solution.py:39
  55.9 1.4 %mul.433 = f32[32,2048]{1,0:T(8,128)S(1)} reshape(f32[32,32,2,32]{3,2,1,0:T(2,128)S(1)} %copy.64) | data formatting | bytes 524288 | tf_op jit(solution)/shard_map/mul | solution.py:39
  58.4 3.6 %multiply_convert_fusion = bf16[32,32,2048]{2,1,0:T(8,128)(2,1)} fusion(f32[32,2048]{1,0:T(8,128)S(1)} %mul.433, f32[32,2048]{1,0:T(8,128)S(1)} %get-tuple-element.59, f32[32,2048]{1,0:T(8,128)S(1)} %mul.429, f32[32,2048]{1,0:T(8,128)S(1)} %get-tuple-element.58), kind=kLoop, calls=%fused_computation | loop fusion | flops 10485760 | bytes 5242880 | tf_op jit(solution)/shard_map/convert_element_type | solution.py:40
  62.0 4.1 %all-to-all-done = bf16[32,2,32,256]{3,2,1,0:T(8,128)(2,1)} async-done(((bf16[32,2,32,256]{3,2,1,0:T(8,128)(2,1)}), bf16[32,2,32,256]{3,2,1,0:T(8,128)(2,1)}, u32[]{:S(2)}, u32[]{:S(2)}) %all-to-all-start) | async-done | bytes 1048608 | tf_op jit(solution)/shard_map/all_to_all | solution.py:105
  66.1 1.7 %copy.67 = bf16[256,2048]{1,0:T(8,128)(2,1)S(1)} copy(bf16[256,2048]{0,1:T(8,128)(2,1)} %bitcast.12) | data formatting | bytes 2097152 | tf_op jit(solution)/shard_map/dot_general | solution.py:108
  67.9 4.2 %multiply_reduce_fusion = (f32[]{:T(128)}, bf16[1024,8,32]{0,2,1:T(8,128)(2,1)S(1)}) fusion(bf16[8,32,2048]{2,1,0:T(8,128)(2,1)S(1)} %bitcast.63, bf16[1024,2048]{1,0:T(8,128)(2,1)} %bitcast.59, f32[1024,32]{0,1:T(8,128)S(1)} %add_multiply_fusion, f32[8]{0:T(128)S(1)} %multiply_multiply_fusion), kind=kOutput, calls=%fused_computation.25 | convolution fusion | flops 1075314688 | bytes 5898276 | tf_op jit(solution)/shard_map/dot_general | solution.py:108
  75.2 1.6 %copy.68 = bf16[16,65,256]{2,1,0:T(8,128)(2,1)} copy(bf16[16,65,256]{1,0,2:T(8,128)(2,1)S(1)} %pad_maximum_fusion.3) | data formatting | bytes 1064960 | tf_op jit(solution)/shard_map/concatenate | solution.py:131
  76.8 9.9 %all-to-all-start.1 = ((bf16[16,65,256]{2,1,0:T(8,128)(2,1)}), bf16[16,65,256]{2,1,0:T(8,128)(2,1)S(1)}, u32[]{:S(2)}, u32[]{:S(2)}) async-start(bf16[16,65,256]{2,1,0:T(8,128)(2,1)} %copy.68), calls=%async_computation.1 | async-start | bytes 1179648 | tf_op jit(solution)/shard_map/all_to_all | solution.py:138
  87.2 18.0 %all-to-all-done.1 = bf16[16,65,256]{2,1,0:T(8,128)(2,1)S(1)} async-done(((bf16[16,65,256]{2,1,0:T(8,128)(2,1)}), bf16[16,65,256]{2,1,0:T(8,128)(2,1)S(1)}, u32[]{:S(2)}, u32[]{:S(2)}) %all-to-all-start.1) | async-done | bytes 532512 | tf_op jit(solution)/shard_map/all_to_all | solution.py:138
  107.7 5.3 %all-to-all-start.2 = ((f32[32,1,128]{2,1,0:T(1,128)}), f32[32,1,128]{2,1,0:T(1,128)S(1)}, u32[]{:S(2)}, u32[]{:S(2)}) async-start(f32[32,1,128]{2,1,0:T(1,128)} %broadcast_in_dim.16), calls=%async_computation.2 | async-start | bytes 32768 | tf_op jit(solution)/shard_map/all_to_all | solution.py:140
  114.5 7.0 %all-to-all-done.2 = f32[32,1,128]{2,1,0:T(1,128)S(1)} async-done(((f32[32,1,128]{2,1,0:T(1,128)}), f32[32,1,128]{2,1,0:T(1,128)S(1)}, u32[]{:S(2)}, u32[]{:S(2)}) %all-to-all-start.2) | async-done | bytes 16416 | tf_op jit(solution)/shard_map/all_to_all | solution.py:140
  (47 shorter events, 16.1 us)
Async XLA Ops:
  0.6 2.7 %copy-start = (bf16[8,2,32,1024]{3,2,1,0:T(8,128)(2,1)S(1)}, bf16[8,2,32,1024]{3,2,1,0:T(8,128)(2,1)}, u32[]{:S(2)}) copy-start(bf16[8,2,32,1024]{3,2,1,0:T(8,128)(2,1)} %param.9) | copy-start | bytes 3145732
  15.6 1.6 %copy-start.1 = (bf16[32,32,8,1,32]{1,2,4,3,0:T(8,128)(2,1)S(1)}, bf16[32,32,8,1,32]{1,2,4,3,0:T(8,128)(2,1)}, u32[]{:S(2)}) copy-start(bf16[32,32,8,1,32]{1,2,4,3,0:T(8,128)(2,1)} %copy.65) | copy-start | bytes 1572868
  26.1 40.0 %all-to-all-start = ((bf16[32,2,32,256]{3,2,1,0:T(8,128)(2,1)}), bf16[32,2,32,256]{3,2,1,0:T(8,128)(2,1)}, u32[]{:S(2)}, u32[]{:S(2)}) async-start(bf16[32,2,32,256]{3,2,1,0:T(8,128)(2,1)} %reshape.483), calls=%async_computation | async-start | bytes 2097152 | tf_op jit(solution)/shard_map/all_to_all | solution.py:105
  73.4 13.4 %copy-start.3 = (f32[16,128]{1,0:T(8,128)S(1)}, f32[16,128]{1,0:T(8,128)}, u32[]{:S(2)}) copy-start(f32[16,128]{1,0:T(8,128)} %param.10) | copy-start | bytes 24580
  73.4 13.4 %copy-start.4 = (f32[9,128]{1,0:T(8,128)S(1)}, f32[9,128]{1,0:T(8,128)}, u32[]{:S(2)}) copy-start(f32[9,128]{1,0:T(8,128)} %constant.180.clone) | copy-start | bytes 13828
  74.6 38.4 %copy-start.2 = (bf16[9,16,8]{0,1,2:T(8,128)(2,1)S(1)}, bf16[9,16,8]{0,1,2:T(8,128)(2,1)}, u32[]{:S(2)}) copy-start(bf16[9,16,8]{0,1,2:T(8,128)(2,1)} %constant.185) | copy-start | bytes 6916
  76.8 28.5 %all-to-all-start.1 = ((bf16[16,65,256]{2,1,0:T(8,128)(2,1)}), bf16[16,65,256]{2,1,0:T(8,128)(2,1)S(1)}, u32[]{:S(2)}, u32[]{:S(2)}) async-start(bf16[16,65,256]{2,1,0:T(8,128)(2,1)} %copy.68), calls=%async_computation.1 | async-start | bytes 1179648 | tf_op jit(solution)/shard_map/all_to_all | solution.py:138
  107.7 13.8 %all-to-all-start.2 = ((f32[32,1,128]{2,1,0:T(1,128)}), f32[32,1,128]{2,1,0:T(1,128)S(1)}, u32[]{:S(2)}, u32[]{:S(2)}) async-start(f32[32,1,128]{2,1,0:T(1,128)} %broadcast_in_dim.16), calls=%async_computation.2 | async-start | bytes 32768 | tf_op jit(solution)/shard_map/all_to_all | solution.py:140

commit v4 on v2

--- a/solution.py
+++ b/solution.py
@@ -3,6 +3,8 @@
 import jax
 import jax.numpy as jnp
 from jax import lax
+from jax.experimental import pallas as pl
+from jax.experimental.pallas import tpu as pltpu
 from jax.sharding import PartitionSpec as P
 
 ORDER = 8
@@ -77,6 +79,48 @@
     return jnp.concatenate([matched, basis], axis=0).astype(jnp.bfloat16)
 
 
+def send_kernel(cos_ref, sin_ref, out_ref):
+    channels = cos_ref.shape[0]
+    lanes = cos_ref.shape[3]
+    width = out_ref.shape[3] // channels
+    per_vreg = lanes // width
+    real = cos_ref[:, 0] - sin_ref[:, 1]
+    imag = sin_ref[:, 0] + cos_ref[:, 1]
+    lane_group = lax.broadcasted_iota(jnp.int32, real.shape[1:], 1) // width
+    for q in range(out_ref.shape[0]):
+        for p, part in enumerate((real, imag)):
+            for h in range(channels // per_vreg):
+                acc = jnp.zeros(part.shape[1:], jnp.float32)
+                for j in range(per_vreg):
+                    shift = (width * (j - q)) % lanes
+                    piece = part[h * per_vreg + j]
+                    if shift:
+                        piece = pltpu.roll(piece, shift, 1)
+                    acc = jnp.where(lane_group == j, piece, acc)
+                out_ref[q, p, :, h * lanes:(h + 1) * lanes] = acc.astype(out_ref.dtype)
+
+
+def make_send(with_cos, with_sin, sky_count, columns):
+    channels, _, row_count, points = with_cos.shape
+    lanes = 128
+    per_step = lanes // columns
+    spec_in = pl.BlockSpec((channels, 2, row_count, lanes), lambda t: (0, 0, 0, t))
+    return pl.pallas_call(
+        send_kernel,
+        grid=(points // lanes,),
+        in_specs=[spec_in, spec_in],
+        out_specs=pl.BlockSpec(
+            (per_step, 2, row_count, channels * columns), lambda t: (t, 0, 0, 0)
+        ),
+        out_shape=jax.ShapeDtypeStruct(
+            (sky_count, 2, row_count, channels * columns), jnp.bfloat16
+        ),
+        cost_estimate=pl.CostEstimate(
+            flops=2 * with_cos.size, transcendentals=0, bytes_accessed=5 * with_cos.size
+        ),
+    )(with_cos, with_sin)
+
+
 def body(visibilities, templates):
     channels = visibilities.shape[0]
     row_count = visibilities.shape[2]
@@ -96,13 +140,7 @@
     with_sin = jnp.dot(rows, sine, preferred_element_type=jnp.float32).reshape(
         channels, 2, row_count, points
     )
-    section_real = (with_cos[:, 0] - with_sin[:, 1]).astype(jnp.bfloat16)
-    section_imag = (with_sin[:, 0] + with_cos[:, 1]).astype(jnp.bfloat16)
-    stacked = jnp.stack([section_real, section_imag])
-    stacked = stacked.reshape(2, channels, row_count, sky_count, columns)
-    send = jnp.transpose(stacked, (3, 0, 2, 1, 4)).reshape(
-        sky_count, 2, row_count, channels * columns
-    )
+    send = make_send(with_cos, with_sin, sky_count, columns)
     turned = lax.all_to_all(send, "sky", 0, 0, tiled=True)
     turned = turned.reshape(sky_count * 2 * row_count, channels * columns)
 

time: 125 us -> 115 us (0.920)
  local copies, waits for them, and re-layouts: 35.6 us -> 22.4 us
  Pallas kernels: 0 us -> 6.36 us
  waiting for transfers between devices: 29.1 us -> 25.1 us
  other arithmetic: 20.1 us -> 16.2 us
  matrix products: 7.75 us -> 10.4 us
  starting transfers between devices: 29.3 us -> 31.3 us
    convert_element_type x2 -> x0, local copies, waits for them, and re-layouts: 6.57 us -> none  [the longest x1 3.73 us: body(): section_imag = (with_sin[:, 0] + with_cos[:, 1]).astype(jnp.bfloat16)]
    pallas_call x0 -> x1, Pallas kernels: none -> 6.36 us  [make_send(): pl.pallas_call(send_kernel, grid=(points // lanes,), in_specs=[spec_in, s...]
    reshape x1 -> x0, local copies, waits for them, and re-layouts: 6.17 us -> none  [body(): jnp.transpose(stacked, (3, 0, 2, 1, 4))]
    transpose x1 -> x0, local copies, waits for them, and re-layouts: 4.65 us -> none  [body(): jnp.transpose(stacked, (3, 0, 2, 1, 4))]
    all_to_all x1, waiting for transfers between devices: 4.06 us -> 0.01 us  [body(): turned = lax.all_to_all(send, 'sky', 0, 0, tiled=True)]
    transpose x1 -> x0, other arithmetic: 2.53 us -> none  [body(): jnp.transpose(stacked, (3, 0, 2, 1, 4))]
    all_to_all x1, starting transfers between devices: 5.3 us -> 7.63 us  [body(): lax.all_to_all(jnp.broadcast_to(power_freq, (sky_count, 128)), 'sky', 0,...]
    neg x2, local copies, waits for them, and re-layouts: 2.89 us -> 5.05 us  [tables(): first = jnp.where(part[None, :], hc, -hs)]
  transfers between devices with their start and end apart: 3 -> 3, of which waited for: 3 -> 2; matrix products, arithmetic and copies ran while one was open for 19% -> 25% of each run, Pallas kernels for 0% -> 0%
where the time goes in v4:
time: 115 us
  starting transfers between devices  31.3 us (27%)
  waiting for transfers between devices  25.1 us (22%)
  local copies, waits for them, and re-layouts  22.4 us (19%)
  other arithmetic  16.2 us (14%)
  matrix products  10.4 us (9%)
  Pallas kernels  6.36 us (6%)
  between operations  2.88 us (3%)
    all_to_all x1, waiting for transfers between devices, body(): gathered = lax.all_to_all(outgoing, 'freq', 0, 0, tiled=True)  18 us
    all_to_all x1, starting transfers between devices, body(): turned = lax.all_to_all(send, 'sky', 0, 0, tiled=True)  14 us
    all_to_all x1, starting transfers between devices, body(): gathered = lax.all_to_all(outgoing, 'freq', 0, 0, tiled=True)  9.69 us
    all_to_all x1, starting transfers between devices, body(): lax.all_to_all(jnp.broadcast_to(power_freq, (sky_count, 128)), 'sky', 0,...  7.63 us
    all_to_all x1, waiting for transfers between devices, body(): lax.all_to_all(jnp.broadcast_to(power_freq, (sky_count, 128)), 'sky', 0,...  7.04 us
    pallas_call x1, Pallas kernels, make_send(): pl.pallas_call(send_kernel, grid=(points // lanes,), in_specs=[spec_in, s...  6.36 us
    neg x2, local copies, waits for them, and re-layouts, tables(): first = jnp.where(part[None, :], hc, -hs)  5.05 us
    cos x1, other arithmetic, tables(): low_c = jnp.cos(scale * low.astype(jnp.float32))  5 us
  transfers between devices with their start and end apart: 3, of which 2 were waited for; matrix products, arithmetic and copies ran while one was open for 25% of the time, Pallas kernels for 0%

profile of v4, /device:TPU:1, one launch (start us, length us, event | category | flops | bytes accessed | tf_op | source)
XLA Modules:
  0.0 114.7 jit_solution(3072021818542577516)
XLA Ops:
  1.8 1.6 %multiply_convert_fusion.1 = (bf16[32,32,1024]{2,1,0:T(8,128)(2,1)S(1)}, bf16[32,32,1024]{2,1,0:T(8,128)(2,1)S(1)}) fusion(f32[32,1024]{1,0:T(8,128)S(1)} %get-tuple-element.70, f32[32,1024]{1,0:T(8,128)S(1)} %get-tuple-element.67, f32[32,1024]{1,0:T(8,128)S(1)} %get-tuple-element.71, f32[32,1024]{1,0:T(8,128)S(1)} %get-tuple-element.66), kind=kLoop, calls=%fused_computation.3 | loop fusion | flops 10485760 | bytes 4718592 | tf_op jit(solution)/shard_map/convert_element_type | solution.py:31
  3.4 2.6 %fusion.49 = f32[1024,512]{0,1:T(8,128)} fusion(bf16[512,1024]{1,0:T(8,128)(2,1)S(1)} %bitcast.47, bf16[1024,1024]{1,0:T(8,128)(2,1)S(1)} %bitcast.51), kind=kOutput, calls=%fused_computation.89 | convolution fusion | flops 1073741824 | bytes 5242880 | tf_op jit(solution)/shard_map/dot_general | solution.py:137
  6.0 2.6 %fusion.50 = f32[1024,512]{0,1:T(8,128)} fusion(bf16[512,1024]{1,0:T(8,128)(2,1)S(1)} %bitcast.46, bf16[1024,1024]{1,0:T(8,128)(2,1)S(1)} %bitcast.50), kind=kOutput, calls=%fused_computation.90 | convolution fusion | flops 1073741824 | bytes 5242880 | tf_op jit(solution)/shard_map/dot_general | solution.py:140
  8.5 6.4 %shard_map.50 = bf16[32,2,32,256]{3,2,1,0:T(8,128)(2,1)} custom-call(f32[8,2,32,1024]{3,2,1,0:T(8,128)} %bitcast.52, f32[8,2,32,1024]{3,2,1,0:T(8,128)} %bitcast.53), custom_call_target="tpu_custom_call" | custom-call | flops 1048576 | bytes 2621440 | tf_op jit(solution)/shard_map/pallas_call | solution.py:108
  14.9 14.0 %all-to-all-start = ((bf16[32,2,32,256]{3,2,1,0:T(8,128)(2,1)}), bf16[32,2,32,256]{3,2,1,0:T(8,128)(2,1)}, u32[]{:S(2)}, u32[]{:S(2)}) async-start(bf16[32,2,32,256]{3,2,1,0:T(8,128)(2,1)} %shard_map.50), calls=%async_computation | async-start | bytes 2097152 | tf_op jit(solution)/shard_map/all_to_all | solution.py:144
  28.9 5.0 %fusion.20 = (f32[32,32,1,32]{3,1,2,0:T(8,128)S(1)}, f32[32,32,1,32]{3,1,2,0:T(8,128)S(1)}, f32[32,32,1,32]{3,1,2,0:T(8,128)}, f32[32,32,1,32]{3,1,2,0:T(8,128)}) fusion(s32[32,32]{1,0:T(8,128)S(1)} %multiply_add_fusion, s32[32]{0:T(128)S(1)} %iota_multiply_fusion), kind=kLoop, calls=%fused_computation.37 | loop fusion | flops 917504 | bytes 528512 | tf_op jit(solution)/shard_map/cos | solution.py:26
  34.1 0.8 copy.55
  34.9 1.4 %mul.433 = f32[32,2048]{1,0:T(8,128)S(1)} reshape(f32[32,32,2,32]{3,2,1,0:T(2,128)S(1)} %copy.55) | data formatting | bytes 524288 | tf_op jit(solution)/shard_map/mul | solution.py:41
  36.3 1.8 %pad_maximum_fusion = (f32[32,32,2,32]{3,1,2,0:T(8,128)S(1)}, f32[32,32,2,32]{3,1,2,0:T(8,128)S(1)}) fusion(f32[32,32,1,32]{3,1,2,0:T(8,128)} %get-tuple-element.65, f32[32,32,1,32]{3,1,2,0:T(8,128)} %get-tuple-element.64), kind=kLoop, calls=%fused_computation.10 | loop fusion | flops 196608 | bytes 786432 | tf_op jit(solution)/shard_map/concatenate | solution.py:35
  38.1 1.8 %copy.52 = f32[32,32,2,32]{3,2,1,0:T(2,128)} copy(f32[32,32,2,32]{3,1,2,0:T(8,128)S(1)} %get-tuple-element.72) | data formatting | bytes 524288 | tf_op jit(solution)/shard_map/concatenate | solution.py:35
  39.8 3.3 %reshape.485 = f32[32,2048]{1,0:T(8,128)} reshape(f32[32,32,2,32]{3,2,1,0:T(2,128)} %copy.52) | data formatting | bytes 524288 | tf_op jit(solution)/shard_map/reshape | solution.py:35
  43.1 1.8 %copy.53 = f32[32,32,2,32]{3,2,1,0:T(2,128)} copy(f32[32,32,2,32]{3,1,2,0:T(8,128)S(1)} %get-tuple-element.73) | data formatting | bytes 524288 | tf_op jit(solution)/shard_map/neg | solution.py:39
  44.9 3.3 %neg.22 = f32[32,2048]{1,0:T(8,128)} reshape(f32[32,32,2,32]{3,2,1,0:T(2,128)} %copy.53) | data formatting | bytes 524288 | tf_op jit(solution)/shard_map/neg | solution.py:39
  49.0 1.4 %mul.429 = f32[32,2048]{1,0:T(8,128)S(1)} reshape(f32[32,32,2,32]{3,2,1,0:T(2,128)S(1)} %copy.54) | data formatting | bytes 524288 | tf_op jit(solution)/shard_map/mul | solution.py:41
  50.4 1.1 broadcast_select_fusion
  51.4 3.6 %multiply_convert_fusion = bf16[32,32,2048]{2,1,0:T(8,128)(2,1)} fusion(f32[32,2048]{1,0:T(8,128)S(1)} %mul.433, f32[32,2048]{1,0:T(8,128)S(1)} %get-tuple-element.57, f32[32,2048]{1,0:T(8,128)S(1)} %mul.429, f32[32,2048]{1,0:T(8,128)S(1)} %get-tuple-element.56), kind=kLoop, calls=%fused_computation | loop fusion | flops 10485760 | bytes 5242880 | tf_op jit(solution)/shard_map/convert_element_type | solution.py:42
  55.1 1.7 %copy.56 = bf16[256,2048]{1,0:T(8,128)(2,1)S(1)} copy(bf16[256,2048]{0,1:T(8,128)(2,1)} %bitcast.12) | data formatting | bytes 2097152 | tf_op jit(solution)/shard_map/dot_general | solution.py:147
  56.8 4.2 %multiply_reduce_fusion = (f32[]{:T(128)}, bf16[1024,8,32]{0,2,1:T(8,128)(2,1)S(1)}) fusion(bf16[8,32,2048]{2,1,0:T(8,128)(2,1)S(1)} %bitcast.54, bf16[1024,2048]{1,0:T(8,128)(2,1)} %bitcast.48, f32[1024,32]{0,1:T(8,128)S(1)} %add_multiply_fusion, f32[8]{0:T(128)S(1)} %multiply_multiply_fusion), kind=kOutput, calls=%fused_computation.16 | convolution fusion | flops 1075314688 | bytes 5898276 | tf_op jit(solution)/shard_map/dot_general | solution.py:147
  64.2 1.6 %copy.57 = bf16[16,65,256]{2,1,0:T(8,128)(2,1)} copy(bf16[16,65,256]{1,0,2:T(8,128)(2,1)S(1)} %pad_maximum_fusion.3) | data formatting | bytes 1064960 | tf_op jit(solution)/shard_map/concatenate | solution.py:170
  65.8 9.7 %all-to-all-start.1 = ((bf16[16,65,256]{2,1,0:T(8,128)(2,1)}), bf16[16,65,256]{2,1,0:T(8,128)(2,1)S(1)}, u32[]{:S(2)}, u32[]{:S(2)}) async-start(bf16[16,65,256]{2,1,0:T(8,128)(2,1)} %copy.57), calls=%async_computation.1 | async-start | bytes 1179648 | tf_op jit(solution)/shard_map/all_to_all | solution.py:177
  76.0 18.0 %all-to-all-done.1 = bf16[16,65,256]{2,1,0:T(8,128)(2,1)S(1)} async-done(((bf16[16,65,256]{2,1,0:T(8,128)(2,1)}), bf16[16,65,256]{2,1,0:T(8,128)(2,1)S(1)}, u32[]{:S(2)}, u32[]{:S(2)}) %all-to-all-start.1) | async-done | bytes 532512 | tf_op jit(solution)/shard_map/all_to_all | solution.py:177
  95.1 1.3 %broadcast_in_dim.16 = f32[32,1,128]{2,1,0:T(1,128)} broadcast(f32[]{:T(128)} %fusion.45), dimensions={} | broadcast | bytes 16388 | tf_op jit(solution)/shard_map/broadcast_in_dim | solution.py:180
  96.4 7.6 %all-to-all-start.2 = ((f32[32,1,128]{2,1,0:T(1,128)}), f32[32,1,128]{2,1,0:T(1,128)S(1)}, u32[]{:S(2)}, u32[]{:S(2)}) async-start(f32[32,1,128]{2,1,0:T(1,128)} %broadcast_in_dim.16), calls=%async_computation.2 | async-start | bytes 32768 | tf_op jit(solution)/shard_map/all_to_all | solution.py:179
  105.5 7.0 %all-to-all-done.2 = f32[32,1,128]{2,1,0:T(1,128)S(1)} async-done(((f32[32,1,128]{2,1,0:T(1,128)}), f32[32,1,128]{2,1,0:T(1,128)S(1)}, u32[]{:S(2)}, u32[]{:S(2)}) %all-to-all-start.2) | async-done | bytes 16416 | tf_op jit(solution)/shard_map/all_to_all | solution.py:179
  (39 shorter events, 8.6 us)
Async XLA Ops:
  0.6 2.7 %copy-start = (bf16[8,2,32,1024]{3,2,1,0:T(8,128)(2,1)S(1)}, bf16[8,2,32,1024]{3,2,1,0:T(8,128)(2,1)}, u32[]{:S(2)}) copy-start(bf16[8,2,32,1024]{3,2,1,0:T(8,128)(2,1)} %param.9) | copy-start | bytes 3145732
  14.9 40.2 %all-to-all-start = ((bf16[32,2,32,256]{3,2,1,0:T(8,128)(2,1)}), bf16[32,2,32,256]{3,2,1,0:T(8,128)(2,1)}, u32[]{:S(2)}, u32[]{:S(2)}) async-start(bf16[32,2,32,256]{3,2,1,0:T(8,128)(2,1)} %shard_map.50), calls=%async_computation | async-start | bytes 2097152 | tf_op jit(solution)/shard_map/all_to_all | solution.py:144
  62.3 13.1 %copy-start.2 = (f32[16,128]{1,0:T(8,128)S(1)}, f32[16,128]{1,0:T(8,128)}, u32[]{:S(2)}) copy-start(f32[16,128]{1,0:T(8,128)} %param.10) | copy-start | bytes 24580
  62.3 13.1 %copy-start.3 = (f32[9,128]{1,0:T(8,128)S(1)}, f32[9,128]{1,0:T(8,128)}, u32[]{:S(2)}) copy-start(f32[9,128]{1,0:T(8,128)} %constant.180.clone) | copy-start | bytes 13828
  63.6 40.5 %copy-start.1 = (bf16[9,16,8]{0,1,2:T(8,128)(2,1)S(1)}, bf16[9,16,8]{0,1,2:T(8,128)(2,1)}, u32[]{:S(2)}) copy-start(bf16[9,16,8]{0,1,2:T(8,128)(2,1)} %constant.185) | copy-start | bytes 6916
  65.8 28.2 %all-to-all-start.1 = ((bf16[16,65,256]{2,1,0:T(8,128)(2,1)}), bf16[16,65,256]{2,1,0:T(8,128)(2,1)S(1)}, u32[]{:S(2)}, u32[]{:S(2)}) async-start(bf16[16,65,256]{2,1,0:T(8,128)(2,1)} %copy.57), calls=%async_computation.1 | async-start | bytes 1179648 | tf_op jit(solution)/shard_map/all_to_all | solution.py:177
  96.4 16.2 %all-to-all-start.2 = ((f32[32,1,128]{2,1,0:T(1,128)}), f32[32,1,128]{2,1,0:T(1,128)S(1)}, u32[]{:S(2)}, u32[]{:S(2)}) async-start(f32[32,1,128]{2,1,0:T(1,128)} %broadcast_in_dim.16), calls=%async_computation.2 | async-start | bytes 32768 | tf_op jit(solution)/shard_map/all_to_all | solution.py:179

commit v5 on v4

--- a/solution.py
+++ b/solution.py
@@ -161,25 +161,14 @@
     widened = spectra.astype(jnp.float32)
     power_part = jnp.sum(widened * widened)
 
-    high = power_part.astype(jnp.bfloat16)
-    rest = power_part - high.astype(jnp.float32)
-    middle = rest.astype(jnp.bfloat16)
-    low = (rest - middle.astype(jnp.float32)).astype(jnp.bfloat16)
-    pieces = jnp.zeros((channels * columns,), jnp.bfloat16)
-    pieces = pieces.at[0].set(high).at[1].set(middle).at[2].set(low)
-    outgoing = jnp.concatenate(
-        [
-            spectra.reshape(freq_count, lines, channels * columns),
-            jnp.broadcast_to(pieces, (freq_count, 1, channels * columns)),
-        ],
-        axis=1,
+    totals = lax.psum_scatter(
+        jnp.broadcast_to(power_part, (freq_count * sky_count, 128)),
+        ("freq", "sky"), scatter_dimension=0, tiled=True,
     )
+    power_sum = totals[0, 0]
+
+    outgoing = spectra.reshape(freq_count, lines, channels * columns)
     gathered = lax.all_to_all(outgoing, "freq", 0, 0, tiled=True)
-    power_freq = jnp.sum(gathered[:, lines, :3].astype(jnp.float32))
-    column_power = lax.all_to_all(
-        jnp.broadcast_to(power_freq, (sky_count, 128)), "sky", 0, 0, tiled=True
-    )
-    power_sum = jnp.sum(column_power[:, 0])
     images = gathered[:, :lines].reshape(freq_count, lines, channels, columns)
     weights = filters(templates, all_channels, ORDER).reshape(-1, freq_count, channels)
     result = jnp.einsum(

time: 115 us -> 367 us (3.19)
  waiting for transfers between devices: 25.1 us -> 275 us
  between operations: 2.88 us -> 14.3 us
  starting transfers between devices: 31.3 us -> 23.7 us
    unnamed x0 -> x2, waiting for transfers between devices: none -> 275 us
    all_to_all x1, waiting for transfers between devices: 18 us -> 0.01 us  [body(): gathered = lax.all_to_all(outgoing, 'freq', 0, 0, tiled=True)]
    all_to_all x1 -> x0, starting transfers between devices: 7.63 us -> none  [body(): lax.all_to_all(jnp.broadcast_to(power_freq, (sky_count, 128)), 'sky', 0,...]
    all_to_all x1 -> x0, waiting for transfers between devices: 7.04 us -> none  [body(): lax.all_to_all(jnp.broadcast_to(power_freq, (sky_count, 128)), 'sky', 0,...]
  transfers between devices with their start and end apart: 3 -> 3, of which waited for: 2 -> 1; matrix products, arithmetic and copies ran while one was open for 25% -> 8% of each run, Pallas kernels for 0% -> 0%
where the time goes in v5:
time: 367 us
  waiting for transfers between devices  275 us (75%)
  starting transfers between devices  23.7 us (6%)
  local copies, waits for them, and re-layouts  22.7 us (6%)
  other arithmetic  14.4 us (4%)
  between operations  14.3 us (4%)
  matrix products  10.4 us (3%)
  Pallas kernels  6.36 us (2%)
    unnamed x2, waiting for transfers between devices  275 us
    all_to_all x1, starting transfers between devices, body(): turned = lax.all_to_all(send, 'sky', 0, 0, tiled=True)  14 us
    all_to_all x1, starting transfers between devices, body(): gathered = lax.all_to_all(outgoing, 'freq', 0, 0, tiled=True)  9.64 us
  transfers between devices with their start and end apart: 3, of which 1 were waited for; matrix products, arithmetic and copies ran while one was open for 8% of the time, Pallas kernels for 0%

profile of v5, /device:TPU:1, one launch (start us, length us, event | category | flops | bytes accessed | tf_op | source)
XLA Modules:
  0.0 366.6 jit_solution(8732501694660542587)
XLA Ops:
  8.3 1.6 multiply_convert_fusion.1
  9.9 2.6 fusion.48
  12.5 2.6 fusion.49
  15.0 6.4 %shard_map.50 = bf16[32,2,32,256]{3,2,1,0:T(8,128)(2,1)} custom-call(f32[8,2,32,1024]{3,2,1,0:T(8,128)} %bitcast.50, f32[8,2,32,1024]{3,2,1,0:T(8,128)} %bitcast.51), custom_call_target="tpu_custom_call" | custom-call | flops 1048576 | bytes 2621440 | tf_op jit(solution)/shard_map/pallas_call | solution.py:108
  21.4 14.0 %all-to-all-start = ((bf16[32,2,32,256]{3,2,1,0:T(8,128)(2,1)}), bf16[32,2,32,256]{3,2,1,0:T(8,128)(2,1)}, u32[]{:S(2)}, u32[]{:S(2)}) async-start(bf16[32,2,32,256]{3,2,1,0:T(8,128)(2,1)} %shard_map.50), calls=%async_computation | async-start | bytes 2097152 | tf_op jit(solution)/shard_map/all_to_all | solution.py:144
  35.4 5.0 %fusion.20 = (f32[32,32,1,32]{3,1,2,0:T(8,128)S(1)}, f32[32,32,1,32]{3,1,2,0:T(8,128)S(1)}, f32[32,32,1,32]{3,1,2,0:T(8,128)}, f32[32,32,1,32]{3,1,2,0:T(8,128)}) fusion(s32[32,32]{1,0:T(8,128)S(1)} %multiply_add_fusion, s32[32]{0:T(128)S(1)} %iota_multiply_fusion), kind=kLoop, calls=%fused_computation.36 | loop fusion | flops 917504 | bytes 528512 | tf_op jit(solution)/shard_map/cos | solution.py:26
  40.6 0.8 copy.37
  41.5 1.4 mul.433
  42.8 1.8 pad_maximum_fusion
  44.6 1.8 copy.34
  46.4 3.3 reshape.417
  49.7 1.8 copy.35
  51.4 3.3 neg.22
  54.7 0.8 copy.36
  55.6 1.4 mul.429
  56.9 1.1 broadcast_select_fusion
  58.0 3.6 multiply_convert_fusion
  61.7 1.7 copy.38
  63.4 4.2 %multiply_reduce_fusion = (f32[]{:T(128)}, bf16[1024,8,32]{0,2,1:T(8,128)(2,1)S(1)}) fusion(bf16[8,32,2048]{2,1,0:T(8,128)(2,1)S(1)} %bitcast.52, bf16[1024,2048]{1,0:T(8,128)(2,1)} %bitcast.46, f32[1024,32]{0,1:T(8,128)S(1)} %add_multiply_fusion, f32[8]{0:T(128)S(1)} %multiply_multiply_fusion), kind=kOutput, calls=%fused_computation.15 | convolution fusion | flops 1075314688 | bytes 5898276 | tf_op jit(solution)/shard_map/dot_general | solution.py:147
  68.2 1.6 copy.39
  69.9 9.6 %all-to-all-start.1 = ((bf16[16,64,256]{2,1,0:T(8,128)(2,1)}), bf16[16,64,256]{2,1,0:T(8,128)(2,1)S(1)}, u32[]{:S(2)}, u32[]{:S(2)}) async-start(bf16[16,64,256]{2,1,0:T(8,128)(2,1)} %copy.39), calls=%async_computation.1 | async-start | bytes 1048576 | tf_op jit(solution)/shard_map/all_to_all | solution.py:171
  79.7 1.4 broadcast_in_dim.13
  81.5 274.7 %all-reduce.3.cloned.1.call-done = f32[512,128]{1,0:T(8,128)} async-done(((f32[512,128]{1,0:T(8,128)}), f32[512,128]{1,0:T(8,128)}) %all-reduce.3.cloned.1.call-update) | async-done | bytes 262160
  358.3 0.8 copy.42
  (33 shorter events, 5.3 us)
Async XLA Ops:
  7.2 2.7 copy-start
  21.4 40.3 %all-to-all-start = ((bf16[32,2,32,256]{3,2,1,0:T(8,128)(2,1)}), bf16[32,2,32,256]{3,2,1,0:T(8,128)(2,1)}, u32[]{:S(2)}, u32[]{:S(2)}) async-start(bf16[32,2,32,256]{3,2,1,0:T(8,128)(2,1)} %shard_map.50), calls=%async_computation | async-start | bytes 2097152 | tf_op jit(solution)/shard_map/all_to_all | solution.py:144
  67.6 12.0 %copy-start.2 = (f32[16,128]{1,0:T(8,128)S(1)}, f32[16,128]{1,0:T(8,128)}, u32[]{:S(2)}) copy-start(f32[16,128]{1,0:T(8,128)} %param.4) | copy-start | bytes 24580
  67.6 12.0 %copy-start.3 = (f32[9,128]{1,0:T(8,128)S(1)}, f32[9,128]{1,0:T(8,128)}, u32[]{:S(2)}) copy-start(f32[9,128]{1,0:T(8,128)} %constant.113.clone) | copy-start | bytes 13828
  67.6 289.9 %copy-start.1 = (bf16[9,16,8]{0,1,2:T(8,128)(2,1)S(1)}, bf16[9,16,8]{0,1,2:T(8,128)(2,1)}, u32[]{:S(2)}) copy-start(bf16[9,16,8]{0,1,2:T(8,128)(2,1)} %constant.116) | copy-start | bytes 6916
  69.9 287.1 %all-to-all-start.1 = ((bf16[16,64,256]{2,1,0:T(8,128)(2,1)}), bf16[16,64,256]{2,1,0:T(8,128)(2,1)S(1)}, u32[]{:S(2)}, u32[]{:S(2)}) async-start(bf16[16,64,256]{2,1,0:T(8,128)(2,1)} %copy.39), calls=%async_computation.1 | async-start | bytes 1048576 | tf_op jit(solution)/shard_map/all_to_all | solution.py:171
  79.5 276.7 %all-reduce.3.cloned.1.call-start = ((), (), s32[]{:S(2)}) async-start(), calls=%async_computation.2 | async-start | bytes 524288
Sparse Core Ops, SparseCore 0:
  85.9 270.2 all-reduce.2

commit v6 on v4

--- a/solution.py
+++ b/solution.py
@@ -176,10 +176,13 @@
     )
     gathered = lax.all_to_all(outgoing, "freq", 0, 0, tiled=True)
     power_freq = jnp.sum(gathered[:, lines, :3].astype(jnp.float32))
-    column_power = lax.all_to_all(
-        jnp.broadcast_to(power_freq, (sky_count, 128)), "sky", 0, 0, tiled=True
-    )
-    power_sum = jnp.sum(column_power[:, 0])
+    power_sum = jnp.broadcast_to(power_freq, (8, 128))
+    distance = 1
+    while distance < sky_count:
+        pairs = [(i, i ^ distance) for i in range(sky_count)]
+        power_sum = power_sum + lax.ppermute(power_sum, "sky", pairs)
+        distance *= 2
+    power_sum = power_sum[0, 0]
     images = gathered[:, :lines].reshape(freq_count, lines, channels, columns)
     weights = filters(templates, all_channels, ORDER).reshape(-1, freq_count, channels)
     result = jnp.einsum(

time: 115 us -> 132 us (1.15)
  the two profiles are of different devices: /device:TPU:1 before, /device:TPU:2 now
where the time goes in v6:
time: 132 us; the launch traced here: 131 us
  starting transfers between devices  30.5 us (23%)
  blocking collectives  25.9 us (20%)
  local copies, waits for them, and re-layouts  21.6 us (16%)
  other arithmetic  16.9 us (13%)
  waiting for transfers between devices  16.1 us (12%)
  matrix products  10.4 us (8%)
  Pallas kernels  6.36 us (5%)
  between operations  2.94 us (2%)
    all_to_all x1, blocking collectives, body(): gathered = lax.all_to_all(outgoing, 'freq', 0, 0, tiled=True)  25.9 us
    ppermute x5, starting transfers between devices, body(): power_sum = power_sum + lax.ppermute(power_sum, 'sky', pairs)  16.9 us
    ppermute x5, waiting for transfers between devices, body(): power_sum = power_sum + lax.ppermute(power_sum, 'sky', pairs)  14.3 us
    all_to_all x1, starting transfers between devices, body(): turned = lax.all_to_all(send, 'sky', 0, 0, tiled=True)  13.5 us
    pallas_call x1, Pallas kernels, make_send(): pl.pallas_call(send_kernel, grid=(points // lanes,), in_specs=[spec_in, s...  6.36 us
    neg x2, local copies, waits for them, and re-layouts, tables(): first = jnp.where(part[None, :], hc, -hs)  5.07 us
    cos x1, other arithmetic, tables(): low_c = jnp.cos(scale * low.astype(jnp.float32))  4.99 us
    dot_general x1, matrix products, body(): jnp.dot(table, turned, preferred_element_type=jnp.float32)  4.18 us
  transfers between devices with their start and end apart: 6, of which 6 were waited for; matrix products, arithmetic and copies ran while one was open for 22% of the time, Pallas kernels for 0%

profile of v6, /device:TPU:2, one launch (start us, length us, event | category | flops | bytes accessed | tf_op | source)
XLA Modules:
  0.0 130.8 jit_solution(8447513368378770937)
XLA Ops:
  3.4 2.6 %fusion.49 = f32[1024,512]{0,1:T(8,128)} fusion(bf16[512,1024]{1,0:T(8,128)(2,1)S(1)} %bitcast.47, bf16[1024,1024]{1,0:T(8,128)(2,1)S(1)} %bitcast.51), kind=kOutput, calls=%fused_computation.89 | convolution fusion | flops 1073741824 | bytes 5242880 | tf_op jit(solution)/shard_map/dot_general | solution.py:137
  5.9 2.6 %fusion.50 = f32[1024,512]{0,1:T(8,128)} fusion(bf16[512,1024]{1,0:T(8,128)(2,1)S(1)} %bitcast.46, bf16[1024,1024]{1,0:T(8,128)(2,1)S(1)} %bitcast.50), kind=kOutput, calls=%fused_computation.90 | convolution fusion | flops 1073741824 | bytes 5242880 | tf_op jit(solution)/shard_map/dot_general | solution.py:140
  8.5 6.4 %shard_map.50 = bf16[32,2,32,256]{3,2,1,0:T(8,128)(2,1)} custom-call(f32[8,2,32,1024]{3,2,1,0:T(8,128)} %bitcast.52, f32[8,2,32,1024]{3,2,1,0:T(8,128)} %bitcast.53), custom_call_target="tpu_custom_call" | custom-call | flops 1048576 | bytes 2621440 | tf_op jit(solution)/shard_map/pallas_call | solution.py:108
  14.9 13.5 %all-to-all-start = ((bf16[32,2,32,256]{3,2,1,0:T(8,128)(2,1)}), bf16[32,2,32,256]{3,2,1,0:T(8,128)(2,1)}, u32[]{:S(2)}, u32[]{:S(2)}) async-start(bf16[32,2,32,256]{3,2,1,0:T(8,128)(2,1)} %shard_map.50), calls=%async_computation | async-start | bytes 2097152 | tf_op jit(solution)/shard_map/all_to_all | solution.py:144
  28.4 5.0 %fusion.20 = (f32[32,32,1,32]{3,1,2,0:T(8,128)S(1)}, f32[32,32,1,32]{3,1,2,0:T(8,128)S(1)}, f32[32,32,1,32]{3,1,2,0:T(8,128)}, f32[32,32,1,32]{3,1,2,0:T(8,128)}) fusion(s32[32,32]{1,0:T(8,128)S(1)} %multiply_add_fusion, s32[32]{0:T(128)S(1)} %iota_multiply_fusion), kind=kLoop, calls=%fused_computation.37 | loop fusion | flops 917504 | bytes 528512 | tf_op jit(solution)/shard_map/cos | solution.py:26
  35.8 1.8 %pad_maximum_fusion = (f32[32,32,2,32]{3,1,2,0:T(8,128)S(1)}, f32[32,32,2,32]{3,1,2,0:T(8,128)S(1)}) fusion(f32[32,32,1,32]{3,1,2,0:T(8,128)} %get-tuple-element.61, f32[32,32,1,32]{3,1,2,0:T(8,128)} %get-tuple-element.60), kind=kLoop, calls=%fused_computation.10 | loop fusion | flops 196608 | bytes 786432 | tf_op jit(solution)/shard_map/concatenate | solution.py:35
  37.6 1.8 %copy.34 = f32[32,32,2,32]{3,2,1,0:T(2,128)} copy(f32[32,32,2,32]{3,1,2,0:T(8,128)S(1)} %get-tuple-element.68) | data formatting | bytes 524288 | tf_op jit(solution)/shard_map/concatenate | solution.py:35
  39.4 3.3 %reshape.488 = f32[32,2048]{1,0:T(8,128)} reshape(f32[32,32,2,32]{3,2,1,0:T(2,128)} %copy.34) | data formatting | bytes 524288 | tf_op jit(solution)/shard_map/reshape | solution.py:35
  42.6 1.8 %copy.35 = f32[32,32,2,32]{3,2,1,0:T(2,128)} copy(f32[32,32,2,32]{3,1,2,0:T(8,128)S(1)} %get-tuple-element.69) | data formatting | bytes 524288 | tf_op jit(solution)/shard_map/neg | solution.py:39
  44.4 3.3 %neg.22 = f32[32,2048]{1,0:T(8,128)} reshape(f32[32,32,2,32]{3,2,1,0:T(2,128)} %copy.35) | data formatting | bytes 524288 | tf_op jit(solution)/shard_map/neg | solution.py:39
  51.0 3.6 %multiply_convert_fusion = bf16[32,32,2048]{2,1,0:T(8,128)(2,1)} fusion(f32[32,2048]{1,0:T(8,128)S(1)} %mul.433, f32[32,2048]{1,0:T(8,128)S(1)} %get-tuple-element.53, f32[32,2048]{1,0:T(8,128)S(1)} %mul.429, f32[32,2048]{1,0:T(8,128)S(1)} %get-tuple-element.52), kind=kLoop, calls=%fused_computation | loop fusion | flops 10485760 | bytes 5242880 | tf_op jit(solution)/shard_map/convert_element_type | solution.py:42
  54.7 1.8 %all-to-all-done = bf16[32,2,32,256]{3,2,1,0:T(8,128)(2,1)} async-done(((bf16[32,2,32,256]{3,2,1,0:T(8,128)(2,1)}), bf16[32,2,32,256]{3,2,1,0:T(8,128)(2,1)}, u32[]{:S(2)}, u32[]{:S(2)}) %all-to-all-start) | async-done | bytes 1048608 | tf_op jit(solution)/shard_map/all_to_all | solution.py:144
  58.2 4.2 %multiply_reduce_fusion = (f32[]{:T(128)}, bf16[1024,8,32]{0,2,1:T(8,128)(2,1)S(1)}) fusion(bf16[8,32,2048]{2,1,0:T(8,128)(2,1)S(1)} %bitcast.54, bf16[1024,2048]{1,0:T(8,128)(2,1)} %bitcast.48, f32[1024,32]{0,1:T(8,128)S(1)} %add_multiply_fusion, f32[8]{0:T(128)S(1)} %multiply_multiply_fusion), kind=kOutput, calls=%fused_computation.16 | convolution fusion | flops 1075314688 | bytes 5898276 | tf_op jit(solution)/shard_map/dot_general | solution.py:147
  66.4 25.9 %all_to_all.10 = bf16[16,65,256]{2,1,0:T(8,128)(2,1)S(1)} all-to-all(bf16[16,65,256]{2,1,0:T(8,128)(2,1)S(1)} %copy.39), channel_id=1, replica_groups=mesh['freq'=16,'sky'=32] {'freq'}, dimensions={0} | all-to-all | bytes 1064960 | tf_op jit(solution)/shard_map/all_to_all | solution.py:177
  93.7 2.1 %collective-permute-start = (f32[8,128]{1,0:T(8,128)S(1)}, f32[8,128]{1,0:T(8,128)S(1)}, u32[]{:S(2)}, u32[]{:S(2)}) collective-permute-start(f32[8,128]{1,0:T(8,128)S(1)} %broadcast_in_dim.16), channel_id=1, source_target_pairs={{0,1},{1,0},{2,3},{3,2},{4,5},{5,4},{6,7},{7,6},{8,9},{9,8},{10,11... | collective-permute-start | bytes 12296 | tf_op jit(solution)/shard_map/ppermute | solution.py:183
  95.8 3.4 %collective-permute-done = f32[8,128]{1,0:T(8,128)S(1)} collective-permute-done((f32[8,128]{1,0:T(8,128)S(1)}, f32[8,128]{1,0:T(8,128)S(1)}, u32[]{:S(2)}, u32[]{:S(2)}) %collective-permute-start) | collective-permute-done | bytes 4128 | tf_op jit(solution)/shard_map/ppermute | solution.py:183
  99.8 4.0 %collective-permute-start.1 = (f32[8,128]{1,0:T(8,128)S(1)}, f32[8,128]{1,0:T(8,128)S(1)}, u32[]{:S(2)}, u32[]{:S(2)}) collective-permute-start(f32[8,128]{1,0:T(8,128)S(1)} %broadcast_add_fusion), channel_id=1, source_target_pairs={{0,2},{1,3},{2,0},{3,1},{4,6},{5,7},{6,4},{7,5},{8,10},{9,11},{10,... | collective-permute-start | bytes 12296 | tf_op jit(solution)/shard_map/ppermute | solution.py:183
  103.8 3.0 %collective-permute-done.1 = f32[8,128]{1,0:T(8,128)S(1)} collective-permute-done((f32[8,128]{1,0:T(8,128)S(1)}, f32[8,128]{1,0:T(8,128)S(1)}, u32[]{:S(2)}, u32[]{:S(2)}) %collective-permute-start.1) | collective-permute-done | bytes 4128 | tf_op jit(solution)/shard_map/ppermute | solution.py:183
  107.5 2.5 %collective-permute-start.2 = (f32[8,128]{1,0:T(8,128)S(1)}, f32[8,128]{1,0:T(8,128)S(1)}, u32[]{:S(2)}, u32[]{:S(2)}) collective-permute-start(f32[8,128]{1,0:T(8,128)S(1)} %fusion.60), channel_id=1, source_target_pairs={{0,4},{1,5},{2,6},{3,7},{4,0},{5,1},{6,2},{7,3},{8,12},{9,13},{10,... | collective-permute-start | bytes 12296 | tf_op jit(solution)/shard_map/ppermute | solution.py:183
  110.1 2.9 %collective-permute-done.2 = f32[8,128]{1,0:T(8,128)S(1)} collective-permute-done((f32[8,128]{1,0:T(8,128)S(1)}, f32[8,128]{1,0:T(8,128)S(1)}, u32[]{:S(2)}, u32[]{:S(2)}) %collective-permute-start.2) | collective-permute-done | bytes 4128 | tf_op jit(solution)/shard_map/ppermute | solution.py:183
  113.0 2.9 %collective-permute-start.3 = (f32[8,128]{1,0:T(8,128)S(1)}, f32[8,128]{1,0:T(8,128)S(1)}, u32[]{:S(2)}, u32[]{:S(2)}) collective-permute-start(f32[8,128]{1,0:T(8,128)S(1)} %add.202), channel_id=1, source_target_pairs={{0,8},{1,9},{2,10},{3,11},{4,12},{5,13},{6,14},{7,15},{8,0},{9,1},... | collective-permute-start | bytes 12296 | tf_op jit(solution)/shard_map/ppermute | solution.py:183
  116.8 2.6 %collective-permute-done.3 = f32[8,128]{1,0:T(8,128)S(1)} collective-permute-done((f32[8,128]{1,0:T(8,128)S(1)}, f32[8,128]{1,0:T(8,128)S(1)}, u32[]{:S(2)}, u32[]{:S(2)}) %collective-permute-start.3) | collective-permute-done | bytes 4128 | tf_op jit(solution)/shard_map/ppermute | solution.py:183
  119.4 5.4 %collective-permute-start.4 = (f32[8,128]{1,0:T(8,128)S(1)}, f32[8,128]{1,0:T(8,128)S(1)}, u32[]{:S(2)}, u32[]{:S(2)}) collective-permute-start(f32[8,128]{1,0:T(8,128)S(1)} %add.203), channel_id=1, source_target_pairs={{0,16},{1,17},{2,18},{3,19},{4,20},{5,21},{6,22},{7,23},{8,24},{9,... | collective-permute-start | bytes 12296 | tf_op jit(solution)/shard_map/ppermute | solution.py:183
  126.3 2.4 %collective-permute-done.4 = f32[8,128]{1,0:T(8,128)S(1)} collective-permute-done((f32[8,128]{1,0:T(8,128)S(1)}, f32[8,128]{1,0:T(8,128)S(1)}, u32[]{:S(2)}, u32[]{:S(2)}) %collective-permute-start.4) | collective-permute-done | bytes 4128 | tf_op jit(solution)/shard_map/ppermute | solution.py:183
  (51 shorter events, 19.2 us)
Async XLA Ops:
  0.6 2.7 %copy-start = (bf16[8,2,32,1024]{3,2,1,0:T(8,128)(2,1)S(1)}, bf16[8,2,32,1024]{3,2,1,0:T(8,128)(2,1)}, u32[]{:S(2)}) copy-start(bf16[8,2,32,1024]{3,2,1,0:T(8,128)(2,1)} %param.9) | copy-start | bytes 3145732
  14.9 41.6 %all-to-all-start = ((bf16[32,2,32,256]{3,2,1,0:T(8,128)(2,1)}), bf16[32,2,32,256]{3,2,1,0:T(8,128)(2,1)}, u32[]{:S(2)}, u32[]{:S(2)}) async-start(bf16[32,2,32,256]{3,2,1,0:T(8,128)(2,1)} %shard_map.50), calls=%async_computation | async-start | bytes 2097152 | tf_op jit(solution)/shard_map/all_to_all | solution.py:144
  63.7 46.3 %copy-start.2 = (f32[16,128]{1,0:T(8,128)S(1)}, f32[16,128]{1,0:T(8,128)}, u32[]{:S(2)}) copy-start(f32[16,128]{1,0:T(8,128)} %param.10) | copy-start | bytes 24580
  63.7 46.3 %copy-start.3 = (f32[9,128]{1,0:T(8,128)S(1)}, f32[9,128]{1,0:T(8,128)}, u32[]{:S(2)}) copy-start(f32[9,128]{1,0:T(8,128)} %constant.182.clone) | copy-start | bytes 13828
  65.0 59.9 %copy-start.1 = (bf16[9,16,8]{0,1,2:T(8,128)(2,1)S(1)}, bf16[9,16,8]{0,1,2:T(8,128)(2,1)}, u32[]{:S(2)}) copy-start(bf16[9,16,8]{0,1,2:T(8,128)(2,1)} %constant.187) | copy-start | bytes 6916
  93.7 5.5 %collective-permute-start = (f32[8,128]{1,0:T(8,128)S(1)}, f32[8,128]{1,0:T(8,128)S(1)}, u32[]{:S(2)}, u32[]{:S(2)}) collective-permute-start(f32[8,128]{1,0:T(8,128)S(1)} %broadcast_in_dim.16), channel_id=1, source_target_pairs={{0,1},{1,0},{2,3},{3,2},{4,5},{5,4},{6,7},{7,6},{8,9},{9,8},{10,11... | collective-permute-start | bytes 12296 | tf_op jit(solution)/shard_map/ppermute | solution.py:183
  99.8 7.0 %collective-permute-start.1 = (f32[8,128]{1,0:T(8,128)S(1)}, f32[8,128]{1,0:T(8,128)S(1)}, u32[]{:S(2)}, u32[]{:S(2)}) collective-permute-start(f32[8,128]{1,0:T(8,128)S(1)} %broadcast_add_fusion), channel_id=1, source_target_pairs={{0,2},{1,3},{2,0},{3,1},{4,6},{5,7},{6,4},{7,5},{8,10},{9,11},{10,... | collective-permute-start | bytes 12296 | tf_op jit(solution)/shard_map/ppermute | solution.py:183
  107.5 5.5 %collective-permute-start.2 = (f32[8,128]{1,0:T(8,128)S(1)}, f32[8,128]{1,0:T(8,128)S(1)}, u32[]{:S(2)}, u32[]{:S(2)}) collective-permute-start(f32[8,128]{1,0:T(8,128)S(1)} %fusion.60), channel_id=1, source_target_pairs={{0,4},{1,5},{2,6},{3,7},{4,0},{5,1},{6,2},{7,3},{8,12},{9,13},{10,... | collective-permute-start | bytes 12296 | tf_op jit(solution)/shard_map/ppermute | solution.py:183
  113.0 6.4 %collective-permute-start.3 = (f32[8,128]{1,0:T(8,128)S(1)}, f32[8,128]{1,0:T(8,128)S(1)}, u32[]{:S(2)}, u32[]{:S(2)}) collective-permute-start(f32[8,128]{1,0:T(8,128)S(1)} %add.202), channel_id=1, source_target_pairs={{0,8},{1,9},{2,10},{3,11},{4,12},{5,13},{6,14},{7,15},{8,0},{9,1},... | collective-permute-start | bytes 12296 | tf_op jit(solution)/shard_map/ppermute | solution.py:183
  119.4 9.4 %collective-permute-start.4 = (f32[8,128]{1,0:T(8,128)S(1)}, f32[8,128]{1,0:T(8,128)S(1)}, u32[]{:S(2)}, u32[]{:S(2)}) collective-permute-start(f32[8,128]{1,0:T(8,128)S(1)} %add.203), channel_id=1, source_target_pairs={{0,16},{1,17},{2,18},{3,19},{4,20},{5,21},{6,22},{7,23},{8,24},{9,... | collective-permute-start | bytes 12296 | tf_op jit(solution)/shard_map/ppermute | solution.py:183

commit v7 on v4

--- a/solution.py
+++ b/solution.py
@@ -84,20 +84,20 @@
     lanes = cos_ref.shape[3]
     width = out_ref.shape[3] // channels
     per_vreg = lanes // width
-    real = cos_ref[:, 0] - sin_ref[:, 1]
-    imag = sin_ref[:, 0] + cos_ref[:, 1]
+    real = (cos_ref[:, 0] - sin_ref[:, 1]).astype(out_ref.dtype)
+    imag = (sin_ref[:, 0] + cos_ref[:, 1]).astype(out_ref.dtype)
     lane_group = lax.broadcasted_iota(jnp.int32, real.shape[1:], 1) // width
     for q in range(out_ref.shape[0]):
         for p, part in enumerate((real, imag)):
             for h in range(channels // per_vreg):
-                acc = jnp.zeros(part.shape[1:], jnp.float32)
+                acc = jnp.zeros(part.shape[1:], part.dtype)
                 for j in range(per_vreg):
                     shift = (width * (j - q)) % lanes
                     piece = part[h * per_vreg + j]
                     if shift:
                         piece = pltpu.roll(piece, shift, 1)
                     acc = jnp.where(lane_group == j, piece, acc)
-                out_ref[q, p, :, h * lanes:(h + 1) * lanes] = acc.astype(out_ref.dtype)
+                out_ref[q, p, :, h * lanes:(h + 1) * lanes] = acc
 
 
 def make_send(with_cos, with_sin, sky_count, columns):

time: 115 us -> 115 us (level)
  no operation moved by 1% of the time
where the time goes in v7:
time: 115 us
  starting transfers between devices  31.3 us (27%)
  waiting for transfers between devices  25.1 us (22%)
  local copies, waits for them, and re-layouts  22.4 us (19%)
  other arithmetic  16.2 us (14%)
  matrix products  10.4 us (9%)
  Pallas kernels  6.36 us (6%)
  between operations  2.88 us (3%)
    all_to_all x1, waiting for transfers between devices, body(): gathered = lax.all_to_all(outgoing, 'freq', 0, 0, tiled=True)  18 us
    all_to_all x1, starting transfers between devices, body(): turned = lax.all_to_all(send, 'sky', 0, 0, tiled=True)  14 us
    all_to_all x1, starting transfers between devices, body(): gathered = lax.all_to_all(outgoing, 'freq', 0, 0, tiled=True)  9.69 us
    all_to_all x1, starting transfers between devices, body(): lax.all_to_all(jnp.broadcast_to(power_freq, (sky_count, 128)), 'sky', 0,...  7.63 us
    all_to_all x1, waiting for transfers between devices, body(): lax.all_to_all(jnp.broadcast_to(power_freq, (sky_count, 128)), 'sky', 0,...  7.04 us
    pallas_call x1, Pallas kernels, make_send(): pl.pallas_call(send_kernel, grid=(points // lanes,), in_specs=[spec_in, s...  6.36 us
    neg x2, local copies, waits for them, and re-layouts, tables(): first = jnp.where(part[None, :], hc, -hs)  5.05 us
    cos x1, other arithmetic, tables(): low_c = jnp.cos(scale * low.astype(jnp.float32))  5 us
  transfers between devices with their start and end apart: 3, of which 2 were waited for; matrix products, arithmetic and copies ran while one was open for 25% of the time, Pallas kernels for 0%

profile of v7, /device:TPU:1, one launch (start us, length us, event | category | flops | bytes accessed | tf_op | source)
XLA Modules:
  0.0 114.7 jit_solution(15194868653214489956)
XLA Ops:
  1.8 1.6 %multiply_convert_fusion.1 = (bf16[32,32,1024]{2,1,0:T(8,128)(2,1)S(1)}, bf16[32,32,1024]{2,1,0:T(8,128)(2,1)S(1)}) fusion(f32[32,1024]{1,0:T(8,128)S(1)} %get-tuple-element.70, f32[32,1024]{1,0:T(8,128)S(1)} %get-tuple-element.67, f32[32,1024]{1,0:T(8,128)S(1)} %get-tuple-element.71, f32[32,1024]{1,0:T(8,128)S(1)} %get-tuple-element.66), kind=kLoop, calls=%fused_computation.3 | loop fusion | flops 10485760 | bytes 4718592 | tf_op jit(solution)/shard_map/convert_element_type | solution.py:31
  3.4 2.6 %fusion.49 = f32[1024,512]{0,1:T(8,128)} fusion(bf16[512,1024]{1,0:T(8,128)(2,1)S(1)} %bitcast.47, bf16[1024,1024]{1,0:T(8,128)(2,1)S(1)} %bitcast.51), kind=kOutput, calls=%fused_computation.89 | convolution fusion | flops 1073741824 | bytes 5242880 | tf_op jit(solution)/shard_map/dot_general | solution.py:137
  6.0 2.6 %fusion.50 = f32[1024,512]{0,1:T(8,128)} fusion(bf16[512,1024]{1,0:T(8,128)(2,1)S(1)} %bitcast.46, bf16[1024,1024]{1,0:T(8,128)(2,1)S(1)} %bitcast.50), kind=kOutput, calls=%fused_computation.90 | convolution fusion | flops 1073741824 | bytes 5242880 | tf_op jit(solution)/shard_map/dot_general | solution.py:140
  8.5 6.4 %shard_map.50 = bf16[32,2,32,256]{3,2,1,0:T(8,128)(2,1)} custom-call(f32[8,2,32,1024]{3,2,1,0:T(8,128)} %bitcast.52, f32[8,2,32,1024]{3,2,1,0:T(8,128)} %bitcast.53), custom_call_target="tpu_custom_call" | custom-call | flops 1048576 | bytes 2621440 | tf_op jit(solution)/shard_map/pallas_call | solution.py:108
  14.9 14.0 %all-to-all-start = ((bf16[32,2,32,256]{3,2,1,0:T(8,128)(2,1)}), bf16[32,2,32,256]{3,2,1,0:T(8,128)(2,1)}, u32[]{:S(2)}, u32[]{:S(2)}) async-start(bf16[32,2,32,256]{3,2,1,0:T(8,128)(2,1)} %shard_map.50), calls=%async_computation | async-start | bytes 2097152 | tf_op jit(solution)/shard_map/all_to_all | solution.py:144
  28.9 5.0 %fusion.20 = (f32[32,32,1,32]{3,1,2,0:T(8,128)S(1)}, f32[32,32,1,32]{3,1,2,0:T(8,128)S(1)}, f32[32,32,1,32]{3,1,2,0:T(8,128)}, f32[32,32,1,32]{3,1,2,0:T(8,128)}) fusion(s32[32,32]{1,0:T(8,128)S(1)} %multiply_add_fusion, s32[32]{0:T(128)S(1)} %iota_multiply_fusion), kind=kLoop, calls=%fused_computation.37 | loop fusion | flops 917504 | bytes 528512 | tf_op jit(solution)/shard_map/cos | solution.py:26
  34.1 0.8 copy.55
  34.9 1.4 %mul.433 = f32[32,2048]{1,0:T(8,128)S(1)} reshape(f32[32,32,2,32]{3,2,1,0:T(2,128)S(1)} %copy.55) | data formatting | bytes 524288 | tf_op jit(solution)/shard_map/mul | solution.py:41
  36.3 1.8 %pad_maximum_fusion = (f32[32,32,2,32]{3,1,2,0:T(8,128)S(1)}, f32[32,32,2,32]{3,1,2,0:T(8,128)S(1)}) fusion(f32[32,32,1,32]{3,1,2,0:T(8,128)} %get-tuple-element.65, f32[32,32,1,32]{3,1,2,0:T(8,128)} %get-tuple-element.64), kind=kLoop, calls=%fused_computation.10 | loop fusion | flops 196608 | bytes 786432 | tf_op jit(solution)/shard_map/concatenate | solution.py:35
  38.1 1.8 %copy.52 = f32[32,32,2,32]{3,2,1,0:T(2,128)} copy(f32[32,32,2,32]{3,1,2,0:T(8,128)S(1)} %get-tuple-element.72) | data formatting | bytes 524288 | tf_op jit(solution)/shard_map/concatenate | solution.py:35
  39.9 3.3 %reshape.485 = f32[32,2048]{1,0:T(8,128)} reshape(f32[32,32,2,32]{3,2,1,0:T(2,128)} %copy.52) | data formatting | bytes 524288 | tf_op jit(solution)/shard_map/reshape | solution.py:35
  43.1 1.8 %copy.53 = f32[32,32,2,32]{3,2,1,0:T(2,128)} copy(f32[32,32,2,32]{3,1,2,0:T(8,128)S(1)} %get-tuple-element.73) | data formatting | bytes 524288 | tf_op jit(solution)/shard_map/neg | solution.py:39
  44.9 3.3 %neg.22 = f32[32,2048]{1,0:T(8,128)} reshape(f32[32,32,2,32]{3,2,1,0:T(2,128)} %copy.53) | data formatting | bytes 524288 | tf_op jit(solution)/shard_map/neg | solution.py:39
  49.0 1.4 %mul.429 = f32[32,2048]{1,0:T(8,128)S(1)} reshape(f32[32,32,2,32]{3,2,1,0:T(2,128)S(1)} %copy.54) | data formatting | bytes 524288 | tf_op jit(solution)/shard_map/mul | solution.py:41
  50.4 1.1 broadcast_select_fusion
  51.4 3.6 %multiply_convert_fusion = bf16[32,32,2048]{2,1,0:T(8,128)(2,1)} fusion(f32[32,2048]{1,0:T(8,128)S(1)} %mul.433, f32[32,2048]{1,0:T(8,128)S(1)} %get-tuple-element.57, f32[32,2048]{1,0:T(8,128)S(1)} %mul.429, f32[32,2048]{1,0:T(8,128)S(1)} %get-tuple-element.56), kind=kLoop, calls=%fused_computation | loop fusion | flops 10485760 | bytes 5242880 | tf_op jit(solution)/shard_map/convert_element_type | solution.py:42
  55.1 1.7 %copy.56 = bf16[256,2048]{1,0:T(8,128)(2,1)S(1)} copy(bf16[256,2048]{0,1:T(8,128)(2,1)} %bitcast.12) | data formatting | bytes 2097152 | tf_op jit(solution)/shard_map/dot_general | solution.py:147
  56.8 4.2 %multiply_reduce_fusion = (f32[]{:T(128)}, bf16[1024,8,32]{0,2,1:T(8,128)(2,1)S(1)}) fusion(bf16[8,32,2048]{2,1,0:T(8,128)(2,1)S(1)} %bitcast.54, bf16[1024,2048]{1,0:T(8,128)(2,1)} %bitcast.48, f32[1024,32]{0,1:T(8,128)S(1)} %add_multiply_fusion, f32[8]{0:T(128)S(1)} %multiply_multiply_fusion), kind=kOutput, calls=%fused_computation.16 | convolution fusion | flops 1075314688 | bytes 5898276 | tf_op jit(solution)/shard_map/dot_general | solution.py:147
  64.2 1.6 %copy.57 = bf16[16,65,256]{2,1,0:T(8,128)(2,1)} copy(bf16[16,65,256]{1,0,2:T(8,128)(2,1)S(1)} %pad_maximum_fusion.3) | data formatting | bytes 1064960 | tf_op jit(solution)/shard_map/concatenate | solution.py:170
  65.8 9.7 %all-to-all-start.1 = ((bf16[16,65,256]{2,1,0:T(8,128)(2,1)}), bf16[16,65,256]{2,1,0:T(8,128)(2,1)S(1)}, u32[]{:S(2)}, u32[]{:S(2)}) async-start(bf16[16,65,256]{2,1,0:T(8,128)(2,1)} %copy.57), calls=%async_computation.1 | async-start | bytes 1179648 | tf_op jit(solution)/shard_map/all_to_all | solution.py:177
  76.0 18.0 %all-to-all-done.1 = bf16[16,65,256]{2,1,0:T(8,128)(2,1)S(1)} async-done(((bf16[16,65,256]{2,1,0:T(8,128)(2,1)}), bf16[16,65,256]{2,1,0:T(8,128)(2,1)S(1)}, u32[]{:S(2)}, u32[]{:S(2)}) %all-to-all-start.1) | async-done | bytes 532512 | tf_op jit(solution)/shard_map/all_to_all | solution.py:177
  95.2 1.3 %broadcast_in_dim.16 = f32[32,1,128]{2,1,0:T(1,128)} broadcast(f32[]{:T(128)} %fusion.45), dimensions={} | broadcast | bytes 16388 | tf_op jit(solution)/shard_map/broadcast_in_dim | solution.py:180
  96.4 7.6 %all-to-all-start.2 = ((f32[32,1,128]{2,1,0:T(1,128)}), f32[32,1,128]{2,1,0:T(1,128)S(1)}, u32[]{:S(2)}, u32[]{:S(2)}) async-start(f32[32,1,128]{2,1,0:T(1,128)} %broadcast_in_dim.16), calls=%async_computation.2 | async-start | bytes 32768 | tf_op jit(solution)/shard_map/all_to_all | solution.py:179
  105.5 7.0 %all-to-all-done.2 = f32[32,1,128]{2,1,0:T(1,128)S(1)} async-done(((f32[32,1,128]{2,1,0:T(1,128)}), f32[32,1,128]{2,1,0:T(1,128)S(1)}, u32[]{:S(2)}, u32[]{:S(2)}) %all-to-all-start.2) | async-done | bytes 16416 | tf_op jit(solution)/shard_map/all_to_all | solution.py:179
  (39 shorter events, 8.6 us)
Async XLA Ops:
  0.6 2.7 %copy-start = (bf16[8,2,32,1024]{3,2,1,0:T(8,128)(2,1)S(1)}, bf16[8,2,32,1024]{3,2,1,0:T(8,128)(2,1)}, u32[]{:S(2)}) copy-start(bf16[8,2,32,1024]{3,2,1,0:T(8,128)(2,1)} %param.9) | copy-start | bytes 3145732
  14.9 40.2 %all-to-all-start = ((bf16[32,2,32,256]{3,2,1,0:T(8,128)(2,1)}), bf16[32,2,32,256]{3,2,1,0:T(8,128)(2,1)}, u32[]{:S(2)}, u32[]{:S(2)}) async-start(bf16[32,2,32,256]{3,2,1,0:T(8,128)(2,1)} %shard_map.50), calls=%async_computation | async-start | bytes 2097152 | tf_op jit(solution)/shard_map/all_to_all | solution.py:144
  62.3 13.1 %copy-start.2 = (f32[16,128]{1,0:T(8,128)S(1)}, f32[16,128]{1,0:T(8,128)}, u32[]{:S(2)}) copy-start(f32[16,128]{1,0:T(8,128)} %param.10) | copy-start | bytes 24580
  62.3 13.1 %copy-start.3 = (f32[9,128]{1,0:T(8,128)S(1)}, f32[9,128]{1,0:T(8,128)}, u32[]{:S(2)}) copy-start(f32[9,128]{1,0:T(8,128)} %constant.180.clone) | copy-start | bytes 13828
  63.6 40.5 %copy-start.1 = (bf16[9,16,8]{0,1,2:T(8,128)(2,1)S(1)}, bf16[9,16,8]{0,1,2:T(8,128)(2,1)}, u32[]{:S(2)}) copy-start(bf16[9,16,8]{0,1,2:T(8,128)(2,1)} %constant.185) | copy-start | bytes 6916
  65.8 28.2 %all-to-all-start.1 = ((bf16[16,65,256]{2,1,0:T(8,128)(2,1)}), bf16[16,65,256]{2,1,0:T(8,128)(2,1)S(1)}, u32[]{:S(2)}, u32[]{:S(2)}) async-start(bf16[16,65,256]{2,1,0:T(8,128)(2,1)} %copy.57), calls=%async_computation.1 | async-start | bytes 1179648 | tf_op jit(solution)/shard_map/all_to_all | solution.py:177
  96.4 16.2 %all-to-all-start.2 = ((f32[32,1,128]{2,1,0:T(1,128)}), f32[32,1,128]{2,1,0:T(1,128)S(1)}, u32[]{:S(2)}, u32[]{:S(2)}) async-start(f32[32,1,128]{2,1,0:T(1,128)} %broadcast_in_dim.16), calls=%async_computation.2 | async-start | bytes 32768 | tf_op jit(solution)/shard_map/all_to_all | solution.py:179

commit v8 on v4

--- a/solution.py
+++ b/solution.py
@@ -81,36 +81,40 @@
 
 def send_kernel(cos_ref, sin_ref, out_ref):
     channels = cos_ref.shape[0]
-    lanes = cos_ref.shape[3]
+    points = cos_ref.shape[3]
+    lanes = 128
     width = out_ref.shape[3] // channels
     per_vreg = lanes // width
     real = cos_ref[:, 0] - sin_ref[:, 1]
     imag = sin_ref[:, 0] + cos_ref[:, 1]
-    lane_group = lax.broadcasted_iota(jnp.int32, real.shape[1:], 1) // width
-    for q in range(out_ref.shape[0]):
+    lane_group = lax.broadcasted_iota(jnp.int32, (real.shape[1], lanes), 1) // width
+    for t in range(points // lanes):
         for p, part in enumerate((real, imag)):
-            for h in range(channels // per_vreg):
-                acc = jnp.zeros(part.shape[1:], jnp.float32)
-                for j in range(per_vreg):
-                    shift = (width * (j - q)) % lanes
-                    piece = part[h * per_vreg + j]
-                    if shift:
-                        piece = pltpu.roll(piece, shift, 1)
-                    acc = jnp.where(lane_group == j, piece, acc)
-                out_ref[q, p, :, h * lanes:(h + 1) * lanes] = acc.astype(out_ref.dtype)
+            block = part[:, :, t * lanes:(t + 1) * lanes]
+            for q in range(per_vreg):
+                for h in range(channels // per_vreg):
+                    acc = jnp.zeros(block.shape[1:], jnp.float32)
+                    for j in range(per_vreg):
+                        shift = (width * (j - q)) % lanes
+                        piece = block[h * per_vreg + j]
+                        if shift:
+                            piece = pltpu.roll(piece, shift, 1)
+                        acc = jnp.where(lane_group == j, piece, acc)
+                    out_ref[t * per_vreg + q, p, :, h * lanes:(h + 1) * lanes] = acc.astype(
+                        out_ref.dtype
+                    )
 
 
 def make_send(with_cos, with_sin, sky_count, columns):
     channels, _, row_count, points = with_cos.shape
-    lanes = 128
-    per_step = lanes // columns
-    spec_in = pl.BlockSpec((channels, 2, row_count, lanes), lambda t: (0, 0, 0, t))
+    rows = 8
+    spec_in = pl.BlockSpec((channels, 2, rows, points), lambda r: (0, 0, r, 0))
     return pl.pallas_call(
         send_kernel,
-        grid=(points // lanes,),
+        grid=(row_count // rows,),
         in_specs=[spec_in, spec_in],
         out_specs=pl.BlockSpec(
-            (per_step, 2, row_count, channels * columns), lambda t: (t, 0, 0, 0)
+            (sky_count, 2, rows, channels * columns), lambda r: (0, 0, r, 0)
         ),
         out_shape=jax.ShapeDtypeStruct(
             (sky_count, 2, row_count, channels * columns), jnp.bfloat16

time: 115 us -> 114 us (level)
  Pallas kernels: 6.36 us -> 4.51 us
    pallas_call x1, Pallas kernels: 6.36 us -> 4.51 us  [make_send(): pl.pallas_call(send_kernel, grid=(row_count // rows,), in_specs=[spec_in,...]
where the time goes in v8:
time: 114 us; the launch traced here: 113 us
  starting transfers between devices  31.3 us (27%)
  waiting for transfers between devices  25.1 us (22%)
  local copies, waits for them, and re-layouts  22.4 us (20%)
  other arithmetic  16.2 us (14%)
  matrix products  10.4 us (9%)
  Pallas kernels  4.51 us (4%)
  between operations  2.88 us (3%)
    all_to_all x1, waiting for transfers between devices, body(): gathered = lax.all_to_all(outgoing, 'freq', 0, 0, tiled=True)  18 us
    all_to_all x1, starting transfers between devices, body(): turned = lax.all_to_all(send, 'sky', 0, 0, tiled=True)  14 us
    all_to_all x1, starting transfers between devices, body(): gathered = lax.all_to_all(outgoing, 'freq', 0, 0, tiled=True)  9.69 us
    all_to_all x1, starting transfers between devices, body(): lax.all_to_all(jnp.broadcast_to(power_freq, (sky_count, 128)), 'sky', 0,...  7.63 us
    all_to_all x1, waiting for transfers between devices, body(): lax.all_to_all(jnp.broadcast_to(power_freq, (sky_count, 128)), 'sky', 0,...  7.04 us
    neg x2, local copies, waits for them, and re-layouts, tables(): first = jnp.where(part[None, :], hc, -hs)  5.05 us
    cos x1, other arithmetic, tables(): low_c = jnp.cos(scale * low.astype(jnp.float32))  5 us
    pallas_call x1, Pallas kernels, make_send(): pl.pallas_call(send_kernel, grid=(row_count // rows,), in_specs=[spec_in,...  4.51 us
  transfers between devices with their start and end apart: 3, of which 2 were waited for; matrix products, arithmetic and copies ran while one was open for 25% of the time, Pallas kernels for 0%

profile of v8, /device:TPU:1, one launch (start us, length us, event | category | flops | bytes accessed | tf_op | source)
XLA Modules:
  0.0 112.9 jit_solution(4042644492045377522)
XLA Ops:
  1.8 1.6 %multiply_convert_fusion.1 = (bf16[32,32,1024]{2,1,0:T(8,128)(2,1)S(1)}, bf16[32,32,1024]{2,1,0:T(8,128)(2,1)S(1)}) fusion(f32[32,1024]{1,0:T(8,128)S(1)} %get-tuple-element.70, f32[32,1024]{1,0:T(8,128)S(1)} %get-tuple-element.67, f32[32,1024]{1,0:T(8,128)S(1)} %get-tuple-element.71, f32[32,1024]{1,0:T(8,128)S(1)} %get-tuple-element.66), kind=kLoop, calls=%fused_computation.3 | loop fusion | flops 10485760 | bytes 4718592 | tf_op jit(solution)/shard_map/convert_element_type | solution.py:31
  3.4 2.6 %fusion.49 = f32[1024,512]{0,1:T(8,128)} fusion(bf16[512,1024]{1,0:T(8,128)(2,1)S(1)} %bitcast.47, bf16[1024,1024]{1,0:T(8,128)(2,1)S(1)} %bitcast.51), kind=kOutput, calls=%fused_computation.89 | convolution fusion | flops 1073741824 | bytes 5242880 | tf_op jit(solution)/shard_map/dot_general | solution.py:141
  6.0 2.6 %fusion.50 = f32[1024,512]{0,1:T(8,128)} fusion(bf16[512,1024]{1,0:T(8,128)(2,1)S(1)} %bitcast.46, bf16[1024,1024]{1,0:T(8,128)(2,1)S(1)} %bitcast.50), kind=kOutput, calls=%fused_computation.90 | convolution fusion | flops 1073741824 | bytes 5242880 | tf_op jit(solution)/shard_map/dot_general | solution.py:144
  8.5 4.5 %shard_map.50 = bf16[32,2,32,256]{3,2,1,0:T(8,128)(2,1)} custom-call(f32[8,2,32,1024]{3,2,1,0:T(8,128)} %bitcast.52, f32[8,2,32,1024]{3,2,1,0:T(8,128)} %bitcast.53), custom_call_target="tpu_custom_call" | custom-call | flops 1048576 | bytes 2621440 | tf_op jit(solution)/shard_map/pallas_call | solution.py:112
  13.0 14.0 %all-to-all-start = ((bf16[32,2,32,256]{3,2,1,0:T(8,128)(2,1)}), bf16[32,2,32,256]{3,2,1,0:T(8,128)(2,1)}, u32[]{:S(2)}, u32[]{:S(2)}) async-start(bf16[32,2,32,256]{3,2,1,0:T(8,128)(2,1)} %shard_map.50), calls=%async_computation | async-start | bytes 2097152 | tf_op jit(solution)/shard_map/all_to_all | solution.py:148
  27.1 5.0 %fusion.20 = (f32[32,32,1,32]{3,1,2,0:T(8,128)S(1)}, f32[32,32,1,32]{3,1,2,0:T(8,128)S(1)}, f32[32,32,1,32]{3,1,2,0:T(8,128)}, f32[32,32,1,32]{3,1,2,0:T(8,128)}) fusion(s32[32,32]{1,0:T(8,128)S(1)} %multiply_add_fusion, s32[32]{0:T(128)S(1)} %iota_multiply_fusion), kind=kLoop, calls=%fused_computation.37 | loop fusion | flops 917504 | bytes 528512 | tf_op jit(solution)/shard_map/cos | solution.py:26
  32.3 0.8 copy.55
  33.1 1.4 %mul.433 = f32[32,2048]{1,0:T(8,128)S(1)} reshape(f32[32,32,2,32]{3,2,1,0:T(2,128)S(1)} %copy.55) | data formatting | bytes 524288 | tf_op jit(solution)/shard_map/mul | solution.py:41
  34.4 1.8 %pad_maximum_fusion = (f32[32,32,2,32]{3,1,2,0:T(8,128)S(1)}, f32[32,32,2,32]{3,1,2,0:T(8,128)S(1)}) fusion(f32[32,32,1,32]{3,1,2,0:T(8,128)} %get-tuple-element.65, f32[32,32,1,32]{3,1,2,0:T(8,128)} %get-tuple-element.64), kind=kLoop, calls=%fused_computation.10 | loop fusion | flops 196608 | bytes 786432 | tf_op jit(solution)/shard_map/concatenate | solution.py:35
  36.2 1.8 %copy.52 = f32[32,32,2,32]{3,2,1,0:T(2,128)} copy(f32[32,32,2,32]{3,1,2,0:T(8,128)S(1)} %get-tuple-element.72) | data formatting | bytes 524288 | tf_op jit(solution)/shard_map/concatenate | solution.py:35
  38.0 3.3 %reshape.485 = f32[32,2048]{1,0:T(8,128)} reshape(f32[32,32,2,32]{3,2,1,0:T(2,128)} %copy.52) | data formatting | bytes 524288 | tf_op jit(solution)/shard_map/reshape | solution.py:35
  41.3 1.8 %copy.53 = f32[32,32,2,32]{3,2,1,0:T(2,128)} copy(f32[32,32,2,32]{3,1,2,0:T(8,128)S(1)} %get-tuple-element.73) | data formatting | bytes 524288 | tf_op jit(solution)/shard_map/neg | solution.py:39
  43.0 3.3 %neg.22 = f32[32,2048]{1,0:T(8,128)} reshape(f32[32,32,2,32]{3,2,1,0:T(2,128)} %copy.53) | data formatting | bytes 524288 | tf_op jit(solution)/shard_map/neg | solution.py:39
  47.2 1.4 %mul.429 = f32[32,2048]{1,0:T(8,128)S(1)} reshape(f32[32,32,2,32]{3,2,1,0:T(2,128)S(1)} %copy.54) | data formatting | bytes 524288 | tf_op jit(solution)/shard_map/mul | solution.py:41
  48.5 1.1 broadcast_select_fusion
  49.6 3.6 %multiply_convert_fusion = bf16[32,32,2048]{2,1,0:T(8,128)(2,1)} fusion(f32[32,2048]{1,0:T(8,128)S(1)} %mul.433, f32[32,2048]{1,0:T(8,128)S(1)} %get-tuple-element.57, f32[32,2048]{1,0:T(8,128)S(1)} %mul.429, f32[32,2048]{1,0:T(8,128)S(1)} %get-tuple-element.56), kind=kLoop, calls=%fused_computation | loop fusion | flops 10485760 | bytes 5242880 | tf_op jit(solution)/shard_map/convert_element_type | solution.py:42
  53.3 1.7 %copy.56 = bf16[256,2048]{1,0:T(8,128)(2,1)S(1)} copy(bf16[256,2048]{0,1:T(8,128)(2,1)} %bitcast.12) | data formatting | bytes 2097152 | tf_op jit(solution)/shard_map/dot_general | solution.py:151
  55.0 4.2 %multiply_reduce_fusion = (f32[]{:T(128)}, bf16[1024,8,32]{0,2,1:T(8,128)(2,1)S(1)}) fusion(bf16[8,32,2048]{2,1,0:T(8,128)(2,1)S(1)} %bitcast.54, bf16[1024,2048]{1,0:T(8,128)(2,1)} %bitcast.48, f32[1024,32]{0,1:T(8,128)S(1)} %add_multiply_fusion, f32[8]{0:T(128)S(1)} %multiply_multiply_fusion), kind=kOutput, calls=%fused_computation.16 | convolution fusion | flops 1075314688 | bytes 5898276 | tf_op jit(solution)/shard_map/dot_general | solution.py:151
  62.4 1.6 %copy.57 = bf16[16,65,256]{2,1,0:T(8,128)(2,1)} copy(bf16[16,65,256]{1,0,2:T(8,128)(2,1)S(1)} %pad_maximum_fusion.3) | data formatting | bytes 1064960 | tf_op jit(solution)/shard_map/concatenate | solution.py:174
  63.9 9.7 %all-to-all-start.1 = ((bf16[16,65,256]{2,1,0:T(8,128)(2,1)}), bf16[16,65,256]{2,1,0:T(8,128)(2,1)S(1)}, u32[]{:S(2)}, u32[]{:S(2)}) async-start(bf16[16,65,256]{2,1,0:T(8,128)(2,1)} %copy.57), calls=%async_computation.1 | async-start | bytes 1179648 | tf_op jit(solution)/shard_map/all_to_all | solution.py:181
  74.1 18.0 %all-to-all-done.1 = bf16[16,65,256]{2,1,0:T(8,128)(2,1)S(1)} async-done(((bf16[16,65,256]{2,1,0:T(8,128)(2,1)}), bf16[16,65,256]{2,1,0:T(8,128)(2,1)S(1)}, u32[]{:S(2)}, u32[]{:S(2)}) %all-to-all-start.1) | async-done | bytes 532512 | tf_op jit(solution)/shard_map/all_to_all | solution.py:181
  93.3 1.3 %broadcast_in_dim.16 = f32[32,1,128]{2,1,0:T(1,128)} broadcast(f32[]{:T(128)} %fusion.45), dimensions={} | broadcast | bytes 16388 | tf_op jit(solution)/shard_map/broadcast_in_dim | solution.py:184
  94.6 7.6 %all-to-all-start.2 = ((f32[32,1,128]{2,1,0:T(1,128)}), f32[32,1,128]{2,1,0:T(1,128)S(1)}, u32[]{:S(2)}, u32[]{:S(2)}) async-start(f32[32,1,128]{2,1,0:T(1,128)} %broadcast_in_dim.16), calls=%async_computation.2 | async-start | bytes 32768 | tf_op jit(solution)/shard_map/all_to_all | solution.py:183
  103.7 7.0 %all-to-all-done.2 = f32[32,1,128]{2,1,0:T(1,128)S(1)} async-done(((f32[32,1,128]{2,1,0:T(1,128)}), f32[32,1,128]{2,1,0:T(1,128)S(1)}, u32[]{:S(2)}, u32[]{:S(2)}) %all-to-all-start.2) | async-done | bytes 16416 | tf_op jit(solution)/shard_map/all_to_all | solution.py:183
  (39 shorter events, 8.6 us)
Async XLA Ops:
  0.6 2.7 %copy-start = (bf16[8,2,32,1024]{3,2,1,0:T(8,128)(2,1)S(1)}, bf16[8,2,32,1024]{3,2,1,0:T(8,128)(2,1)}, u32[]{:S(2)}) copy-start(bf16[8,2,32,1024]{3,2,1,0:T(8,128)(2,1)} %param.9) | copy-start | bytes 3145732
  13.0 40.2 %all-to-all-start = ((bf16[32,2,32,256]{3,2,1,0:T(8,128)(2,1)}), bf16[32,2,32,256]{3,2,1,0:T(8,128)(2,1)}, u32[]{:S(2)}, u32[]{:S(2)}) async-start(bf16[32,2,32,256]{3,2,1,0:T(8,128)(2,1)} %shard_map.50), calls=%async_computation | async-start | bytes 2097152 | tf_op jit(solution)/shard_map/all_to_all | solution.py:148
  60.5 13.1 %copy-start.2 = (f32[16,128]{1,0:T(8,128)S(1)}, f32[16,128]{1,0:T(8,128)}, u32[]{:S(2)}) copy-start(f32[16,128]{1,0:T(8,128)} %param.10) | copy-start | bytes 24580
  60.5 13.1 %copy-start.3 = (f32[9,128]{1,0:T(8,128)S(1)}, f32[9,128]{1,0:T(8,128)}, u32[]{:S(2)}) copy-start(f32[9,128]{1,0:T(8,128)} %constant.180.clone) | copy-start | bytes 13828
  61.8 40.5 %copy-start.1 = (bf16[9,16,8]{0,1,2:T(8,128)(2,1)S(1)}, bf16[9,16,8]{0,1,2:T(8,128)(2,1)}, u32[]{:S(2)}) copy-start(bf16[9,16,8]{0,1,2:T(8,128)(2,1)} %constant.185) | copy-start | bytes 6916
  63.9 28.2 %all-to-all-start.1 = ((bf16[16,65,256]{2,1,0:T(8,128)(2,1)}), bf16[16,65,256]{2,1,0:T(8,128)(2,1)S(1)}, u32[]{:S(2)}, u32[]{:S(2)}) async-start(bf16[16,65,256]{2,1,0:T(8,128)(2,1)} %copy.57), calls=%async_computation.1 | async-start | bytes 1179648 | tf_op jit(solution)/shard_map/all_to_all | solution.py:181
  94.6 16.2 %all-to-all-start.2 = ((f32[32,1,128]{2,1,0:T(1,128)}), f32[32,1,128]{2,1,0:T(1,128)S(1)}, u32[]{:S(2)}, u32[]{:S(2)}) async-start(f32[32,1,128]{2,1,0:T(1,128)} %broadcast_in_dim.16), calls=%async_computation.2 | async-start | bytes 32768 | tf_op jit(solution)/shard_map/all_to_all | solution.py:183

commit v9 on v8

--- a/solution.py
+++ b/solution.py
@@ -125,6 +125,72 @@
     )(with_cos, with_sin)
 
 
+def image_kernel(table_ref, turned_ref, rate_ref, across_ref, out_ref, power_ref):
+    step = pl.program_id(0)
+    tile = table_ref.shape[0]
+    lines = out_ref.shape[1] - 1
+    per_tile = tile // lines
+    points = tile * pl.num_programs(0)
+    half = jnp.float32(points / 2.0)
+    picture = jnp.dot(table_ref[...], turned_ref[...], preferred_element_type=jnp.float32)
+    row = (lax.broadcasted_iota(jnp.int32, picture.shape, 0) + step * tile).astype(jnp.float32)
+    row_term = (row - half) * (row - half)
+    dist = (row_term + across_ref[...]) / (half * half)
+    image = (jnp.exp(rate_ref[...] * dist) * picture).astype(out_ref.dtype)
+    for k in range(per_tile):
+        out_ref[pl.ds(step * per_tile + k, 1), pl.ds(0, lines), :] = image[
+            k * lines:(k + 1) * lines
+        ][None]
+    widened = image.astype(jnp.float32)
+    partial = jnp.sum(widened * widened, axis=0, keepdims=True)
+
+    @pl.when(step == 0)
+    def _():
+        power_ref[...] = jnp.zeros_like(power_ref)
+
+    power_ref[...] += partial
+
+    @pl.when(step == pl.num_programs(0) - 1)
+    def _():
+        total = jnp.sum(power_ref[...], axis=1, keepdims=True)
+        high = total.astype(out_ref.dtype)
+        rest = total - high.astype(jnp.float32)
+        middle = rest.astype(out_ref.dtype)
+        low = (rest - middle.astype(jnp.float32)).astype(out_ref.dtype)
+        lane = lax.broadcasted_iota(jnp.int32, power_ref.shape, 1)
+        zero = jnp.zeros(power_ref.shape, out_ref.dtype)
+        pieces = jnp.where(
+            lane == 0, high, jnp.where(lane == 1, middle, jnp.where(lane == 2, low, zero))
+        )
+        for f in range(out_ref.shape[0]):
+            out_ref[pl.ds(f, 1), pl.ds(lines, 1), :] = pieces[None]
+
+
+def make_images(table, turned, rate, across, freq_count):
+    points, depth = table.shape
+    width = turned.shape[1]
+    lines = points // freq_count
+    tile = 256
+    return pl.pallas_call(
+        image_kernel,
+        grid=(points // tile,),
+        in_specs=[
+            pl.BlockSpec((tile, depth), lambda i: (i, 0)),
+            pl.BlockSpec((depth, width), lambda i: (0, 0)),
+            pl.BlockSpec((1, width), lambda i: (0, 0)),
+            pl.BlockSpec((1, width), lambda i: (0, 0)),
+        ],
+        out_specs=pl.BlockSpec((freq_count, lines + 1, width), lambda i: (0, 0, 0)),
+        out_shape=jax.ShapeDtypeStruct((freq_count, lines + 1, width), jnp.bfloat16),
+        scratch_shapes=[pltpu.VMEM((1, width), jnp.float32)],
+        cost_estimate=pl.CostEstimate(
+            flops=2 * points * depth * width,
+            transcendentals=points * width,
+            bytes_accessed=2 * (points * depth + depth * width + points * width),
+        ),
+    )(table, turned, rate, across)
+
+
 def body(visibilities, templates):
     channels = visibilities.shape[0]
     row_count = visibilities.shape[2]
@@ -148,10 +214,6 @@
     turned = lax.all_to_all(send, "sky", 0, 0, tiled=True)
     turned = turned.reshape(sky_count * 2 * row_count, channels * columns)
 
-    picture = jnp.dot(table, turned, preferred_element_type=jnp.float32).reshape(
-        points, channels, columns
-    )
-    row_pos = jnp.arange(points, dtype=jnp.float32)
     col_pos = (lax.axis_index("sky") * columns + jnp.arange(columns, dtype=jnp.int32)).astype(
         jnp.float32
     )
@@ -160,24 +222,12 @@
     )
     stretch = 1.0 + 0.5 * chan_pos / jnp.float32(all_channels - 1)
     coef = -0.7 * stretch * stretch
-    dist = distances(row_pos, col_pos, points)
-    spectra = (jnp.exp(coef[None, :, None] * dist[:, None, :]) * picture).astype(jnp.bfloat16)
-    widened = spectra.astype(jnp.float32)
-    power_part = jnp.sum(widened * widened)
-
-    high = power_part.astype(jnp.bfloat16)
-    rest = power_part - high.astype(jnp.float32)
-    middle = rest.astype(jnp.bfloat16)
-    low = (rest - middle.astype(jnp.float32)).astype(jnp.bfloat16)
-    pieces = jnp.zeros((channels * columns,), jnp.bfloat16)
-    pieces = pieces.at[0].set(high).at[1].set(middle).at[2].set(low)
-    outgoing = jnp.concatenate(
-        [
-            spectra.reshape(freq_count, lines, channels * columns),
-            jnp.broadcast_to(pieces, (freq_count, 1, channels * columns)),
-        ],
-        axis=1,
-    )
+    half = jnp.float32(points / 2.0)
+    rate = jnp.broadcast_to(coef[:, None], (channels, columns)).reshape(1, channels * columns)
+    across = jnp.broadcast_to(
+        ((col_pos - half) * (col_pos - half))[None, :], (channels, columns)
+    ).reshape(1, channels * columns)
+    outgoing = make_images(table, turned, rate, across, freq_count)
     gathered = lax.all_to_all(outgoing, "freq", 0, 0, tiled=True)
     power_freq = jnp.sum(gathered[:, lines, :3].astype(jnp.float32))
     column_power = lax.all_to_all(

time: 114 us -> 106 us (0.930)
  local copies, waits for them, and re-layouts: 22.4 us -> 15 us
  Pallas kernels: 4.51 us -> 9.71 us
  matrix products: 10.4 us -> 6.23 us
  waiting for transfers between devices: 25.1 us -> 27.9 us
  starting transfers between devices: 31.3 us -> 29.2 us
  between operations: 2.88 us -> 1.51 us
    pallas_call x0 -> x1, Pallas kernels: none -> 5.21 us  [make_images(): pl.pallas_call(image_kernel, grid=(points // tile,), in_specs=[pl.BlockSp...]
    dot_general x1 -> x0, matrix products: 4.18 us -> none  [body(): jnp.dot(table, turned, preferred_element_type=jnp.float32)]
    all_to_all x1, waiting for transfers between devices: 0.01 us -> 2.84 us  [body(): turned = lax.all_to_all(send, 'sky', 0, 0, tiled=True)]
    all_to_all x1, starting transfers between devices: 7.63 us -> 5.3 us  [body(): lax.all_to_all(jnp.broadcast_to(power_freq, (sky_count, 128)), 'sky', 0,...]
    neg x2, local copies, waits for them, and re-layouts: 5.05 us -> 2.89 us  [tables(): first = jnp.where(part[None, :], hc, -hs)]
    dot_general x1 -> x0, local copies, waits for them, and re-layouts: 1.71 us -> none  [body(): jnp.dot(table, turned, preferred_element_type=jnp.float32)]
    concatenate x1 -> x0, local copies, waits for them, and re-layouts: 1.56 us -> none  [body(): jnp.concatenate([spectra.reshape(freq_count, lines, channels * columns),...]
    reshape x1, local copies, waits for them, and re-layouts: 3.26 us -> 2.05 us  [spread(): return jnp.concatenate([x, x], axis=2).reshape(block, sources * 2 * depth)]
  transfers between devices with their start and end apart: 3 -> 3, of which waited for: 2 -> 3; matrix products, arithmetic and copies ran while one was open for 25% -> 24% of each run, Pallas kernels for 0% -> 0%
where the time goes in v9:
time: 106 us; the launch traced here: 105 us
  starting transfers between devices  29.2 us (28%)
  waiting for transfers between devices  27.9 us (26%)
  other arithmetic  15.5 us (15%)
  local copies, waits for them, and re-layouts  15 us (14%)
  Pallas kernels  9.71 us (9%)
  matrix products  6.23 us (6%)
  between operations  1.51 us (1%)
    all_to_all x1, waiting for transfers between devices, body(): gathered = lax.all_to_all(outgoing, 'freq', 0, 0, tiled=True)  18 us
    all_to_all x1, starting transfers between devices, body(): turned = lax.all_to_all(send, 'sky', 0, 0, tiled=True)  14 us
    all_to_all x1, starting transfers between devices, body(): gathered = lax.all_to_all(outgoing, 'freq', 0, 0, tiled=True)  9.92 us
    all_to_all x1, waiting for transfers between devices, body(): lax.all_to_all(jnp.broadcast_to(power_freq, (sky_count, 128)), 'sky', 0,...  7.04 us
    all_to_all x1, starting transfers between devices, body(): lax.all_to_all(jnp.broadcast_to(power_freq, (sky_count, 128)), 'sky', 0,...  5.3 us
    pallas_call x1, Pallas kernels, make_images(): pl.pallas_call(image_kernel, grid=(points // tile,), in_specs=[pl.BlockSp...  5.21 us
    cos x1, other arithmetic, tables(): low_c = jnp.cos(scale * low.astype(jnp.float32))  4.96 us
    pallas_call x1, Pallas kernels, make_send(): pl.pallas_call(send_kernel, grid=(row_count // rows,), in_specs=[spec_in,...  4.51 us
  transfers between devices with their start and end apart: 3, of which 3 were waited for; matrix products, arithmetic and copies ran while one was open for 24% of the time, Pallas kernels for 0%

profile of v9, /device:TPU:1, one launch (start us, length us, event | category | flops | bytes accessed | tf_op | source)
XLA Modules:
  0.0 105.1 jit_solution(15906403649012111268)
XLA Ops:
  1.8 1.6 %multiply_convert_fusion.1 = (bf16[32,32,1024]{2,1,0:T(8,128)(2,1)S(1)}, bf16[32,32,1024]{2,1,0:T(8,128)(2,1)S(1)}) fusion(f32[32,1024]{1,0:T(8,128)S(1)} %get-tuple-element.34, f32[32,1024]{1,0:T(8,128)S(1)} %get-tuple-element.29, f32[32,1024]{1,0:T(8,128)S(1)} %get-tuple-element.35, f32[32,1024]{1,0:T(8,128)S(1)} %get-tuple-element.28), kind=kLoop, calls=%fused_computation.1 | loop fusion | flops 10485760 | bytes 4718592 | tf_op jit(solution)/shard_map/convert_element_type | solution.py:31
  3.4 2.6 %fusion.41 = f32[1024,512]{0,1:T(8,128)} fusion(bf16[512,1024]{1,0:T(8,128)(2,1)S(1)} %bitcast.29, bf16[1024,1024]{1,0:T(8,128)(2,1)S(1)} %bitcast.33), kind=kOutput, calls=%fused_computation.81 | convolution fusion | flops 1073741824 | bytes 5242880 | tf_op jit(solution)/shard_map/dot_general | solution.py:207
  5.9 2.6 %fusion.42 = f32[1024,512]{0,1:T(8,128)} fusion(bf16[512,1024]{1,0:T(8,128)(2,1)S(1)} %bitcast.28, bf16[1024,1024]{1,0:T(8,128)(2,1)S(1)} %bitcast.32), kind=kOutput, calls=%fused_computation.82 | convolution fusion | flops 1073741824 | bytes 5242880 | tf_op jit(solution)/shard_map/dot_general | solution.py:210
  8.5 4.5 %shard_map.50 = bf16[32,2,32,256]{3,2,1,0:T(8,128)(2,1)} custom-call(f32[8,2,32,1024]{3,2,1,0:T(8,128)} %bitcast.34, f32[8,2,32,1024]{3,2,1,0:T(8,128)} %bitcast.35), custom_call_target="tpu_custom_call" | custom-call | flops 1048576 | bytes 2621440 | tf_op jit(solution)/shard_map/pallas_call | solution.py:112
  13.0 14.0 %all-to-all-start = ((bf16[32,2,32,256]{3,2,1,0:T(8,128)(2,1)}), bf16[32,2,32,256]{3,2,1,0:T(8,128)(2,1)}, u32[]{:S(2)}, u32[]{:S(2)}) async-start(bf16[32,2,32,256]{3,2,1,0:T(8,128)(2,1)} %shard_map.50), calls=%async_computation | async-start | bytes 2097152 | tf_op jit(solution)/shard_map/all_to_all | solution.py:214
  27.1 5.0 %fusion.12 = (f32[32,32,1,32]{3,1,2,0:T(8,128)}, f32[32,32,1,32]{3,1,2,0:T(8,128)}, f32[32,32,1,32]{3,1,2,0:T(8,128)S(1)}, f32[32,32,1,32]{3,1,2,0:T(8,128)S(1)}) fusion(s32[32,32]{1,0:T(8,128)S(1)} %multiply_add_fusion, s32[32]{0:T(128)S(1)} %iota_multiply_fusion), kind=kLoop, calls=%fused_computation.31 | loop fusion | flops 917504 | bytes 528512 | tf_op jit(solution)/shard_map/cos | solution.py:26
  32.2 0.8 copy.38
  33.0 2.1 %neg.22 = f32[32,2048]{1,0:T(8,128)} reshape(f32[32,32,2,32]{3,2,1,0:T(2,128)S(1)} %copy.38) | data formatting | bytes 524288 | tf_op jit(solution)/shard_map/neg | solution.py:39
  35.1 0.8 copy.37
  35.9 2.1 %reshape.387 = f32[32,2048]{1,0:T(8,128)} reshape(f32[32,32,2,32]{3,2,1,0:T(2,128)S(1)} %copy.37) | data formatting | bytes 524288 | tf_op jit(solution)/shard_map/reshape | solution.py:35
  38.0 1.8 %pad_maximum_fusion.1 = (f32[32,32,2,32]{3,1,2,0:T(8,128)S(1)}, f32[32,32,2,32]{3,1,2,0:T(8,128)S(1)}) fusion(f32[32,32,1,32]{3,1,2,0:T(8,128)} %get-tuple-element.24, f32[32,32,1,32]{3,1,2,0:T(8,128)} %get-tuple-element.25), kind=kLoop, calls=%fused_computation.8 | loop fusion | flops 131072 | bytes 786432 | tf_op jit(solution)/shard_map/concatenate | solution.py:35
  39.8 0.8 copy.39
  40.6 1.4 %mul.394 = f32[32,2048]{1,0:T(8,128)S(1)} reshape(f32[32,32,2,32]{3,2,1,0:T(2,128)S(1)} %copy.39) | data formatting | bytes 524288 | tf_op jit(solution)/shard_map/mul | solution.py:41
  42.0 0.8 copy.40
  42.8 1.4 %mul.398 = f32[32,2048]{1,0:T(8,128)S(1)} reshape(f32[32,32,2,32]{3,2,1,0:T(2,128)S(1)} %copy.40) | data formatting | bytes 524288 | tf_op jit(solution)/shard_map/mul | solution.py:41
  44.2 1.1 %broadcast_select_fusion = (f32[32,2048]{1,0:T(8,128)S(1)}, f32[32,2048]{1,0:T(8,128)S(1)}) fusion(f32[32,2048]{1,0:T(8,128)} %reshape.387, f32[32,2048]{1,0:T(8,128)} %neg.22, pred[2048]{0:T(1024)(128)(4,1)S(1)} %fusion.34), kind=kLoop, calls=%fused_computation.52 | loop fusion | flops 196608 | bytes 1050624 | tf_op jit(solution)/shard_map/jit(_where)/select_n | solution.py:39
  45.2 3.6 %multiply_convert_fusion = bf16[32,32,2048]{2,1,0:T(8,128)(2,1)} fusion(f32[32,2048]{1,0:T(8,128)S(1)} %mul.398, f32[32,2048]{1,0:T(8,128)S(1)} %get-tuple-element.19, f32[32,2048]{1,0:T(8,128)S(1)} %mul.394, f32[32,2048]{1,0:T(8,128)S(1)} %get-tuple-element.18), kind=kLoop, calls=%fused_computation | loop fusion | flops 10485760 | bytes 5242880 | tf_op jit(solution)/shard_map/convert_element_type | solution.py:42
  50.2 2.8 %all-to-all-done = bf16[32,2,32,256]{3,2,1,0:T(8,128)(2,1)} async-done(((bf16[32,2,32,256]{3,2,1,0:T(8,128)(2,1)}), bf16[32,2,32,256]{3,2,1,0:T(8,128)(2,1)}, u32[]{:S(2)}, u32[]{:S(2)}) %all-to-all-start) | async-done | bytes 1048608 | tf_op jit(solution)/shard_map/all_to_all | solution.py:214
  53.0 5.2 %shard_map.51 = bf16[16,65,256]{2,1,0:T(8,128)(2,1)} custom-call(bf16[1024,2048]{1,0:T(8,128)(2,1)} %bitcast.30, bf16[2048,256]{1,0:T(8,128)(2,1)} %bitcast.10.turned_ref, f32[1,256]{1,0:T(1,128)} %reshape.392.rate_ref, f32[1,256]{1,0:T(1,128)} %reshape.393.across_ref), custom_call_target="tpu_custom_call" | custom-call | flops 1073741824 | bytes 5767168 | tf_op jit(solution)/shard_map/pallas_call | solution.py:174
  58.2 9.9 %all-to-all-start.1 = ((bf16[16,65,256]{2,1,0:T(8,128)(2,1)}), bf16[16,65,256]{2,1,0:T(8,128)(2,1)S(1)}, u32[]{:S(2)}, u32[]{:S(2)}) async-start(bf16[16,65,256]{2,1,0:T(8,128)(2,1)} %shard_map.51), calls=%async_computation.1 | async-start | bytes 1179648 | tf_op jit(solution)/shard_map/all_to_all | solution.py:231
  68.7 18.0 %all-to-all-done.1 = bf16[16,65,256]{2,1,0:T(8,128)(2,1)S(1)} async-done(((bf16[16,65,256]{2,1,0:T(8,128)(2,1)}), bf16[16,65,256]{2,1,0:T(8,128)(2,1)S(1)}, u32[]{:S(2)}, u32[]{:S(2)}) %all-to-all-start.1) | async-done | bytes 532512 | tf_op jit(solution)/shard_map/all_to_all | solution.py:231
  87.9 1.3 %broadcast_in_dim.22 = f32[32,1,128]{2,1,0:T(1,128)} broadcast(f32[]{:T(128)} %fusion.37), dimensions={} | broadcast | bytes 16388 | tf_op jit(solution)/shard_map/broadcast_in_dim | solution.py:234
  89.1 5.3 %all-to-all-start.2 = ((f32[32,1,128]{2,1,0:T(1,128)}), f32[32,1,128]{2,1,0:T(1,128)S(1)}, u32[]{:S(2)}, u32[]{:S(2)}) async-start(f32[32,1,128]{2,1,0:T(1,128)} %broadcast_in_dim.22), calls=%async_computation.2 | async-start | bytes 32768 | tf_op jit(solution)/shard_map/all_to_all | solution.py:233
  95.9 7.0 %all-to-all-done.2 = f32[32,1,128]{2,1,0:T(1,128)S(1)} async-done(((f32[32,1,128]{2,1,0:T(1,128)}), f32[32,1,128]{2,1,0:T(1,128)S(1)}, u32[]{:S(2)}, u32[]{:S(2)}) %all-to-all-start.2) | async-done | bytes 16416 | tf_op jit(solution)/shard_map/all_to_all | solution.py:233
  (33 shorter events, 7.2 us)
Async XLA Ops:
  0.6 2.7 %copy-start = (bf16[8,2,32,1024]{3,2,1,0:T(8,128)(2,1)S(1)}, bf16[8,2,32,1024]{3,2,1,0:T(8,128)(2,1)}, u32[]{:S(2)}) copy-start(bf16[8,2,32,1024]{3,2,1,0:T(8,128)(2,1)} %param.3) | copy-start | bytes 3145732
  13.0 40.0 %all-to-all-start = ((bf16[32,2,32,256]{3,2,1,0:T(8,128)(2,1)}), bf16[32,2,32,256]{3,2,1,0:T(8,128)(2,1)}, u32[]{:S(2)}, u32[]{:S(2)}) async-start(bf16[32,2,32,256]{3,2,1,0:T(8,128)(2,1)} %shard_map.50), calls=%async_computation | async-start | bytes 2097152 | tf_op jit(solution)/shard_map/all_to_all | solution.py:214
  48.8 19.4 %copy-start.2 = (f32[16,128]{1,0:T(8,128)S(1)}, f32[16,128]{1,0:T(8,128)}, u32[]{:S(2)}) copy-start(f32[16,128]{1,0:T(8,128)} %param.4) | copy-start | bytes 24580
  48.8 19.4 %copy-start.3 = (f32[9,128]{1,0:T(8,128)S(1)}, f32[9,128]{1,0:T(8,128)}, u32[]{:S(2)}) copy-start(f32[9,128]{1,0:T(8,128)} %constant.106.clone) | copy-start | bytes 13828
  53.0 41.4 %copy-start.1 = (bf16[9,16,8]{0,1,2:T(8,128)(2,1)S(1)}, bf16[9,16,8]{0,1,2:T(8,128)(2,1)}, u32[]{:S(2)}) copy-start(bf16[9,16,8]{0,1,2:T(8,128)(2,1)} %constant.109) | copy-start | bytes 6916
  58.2 28.5 %all-to-all-start.1 = ((bf16[16,65,256]{2,1,0:T(8,128)(2,1)}), bf16[16,65,256]{2,1,0:T(8,128)(2,1)S(1)}, u32[]{:S(2)}, u32[]{:S(2)}) async-start(bf16[16,65,256]{2,1,0:T(8,128)(2,1)} %shard_map.51), calls=%async_computation.1 | async-start | bytes 1179648 | tf_op jit(solution)/shard_map/all_to_all | solution.py:231
  89.1 13.8 %all-to-all-start.2 = ((f32[32,1,128]{2,1,0:T(1,128)}), f32[32,1,128]{2,1,0:T(1,128)S(1)}, u32[]{:S(2)}, u32[]{:S(2)}) async-start(f32[32,1,128]{2,1,0:T(1,128)} %broadcast_in_dim.22), calls=%async_computation.2 | async-start | bytes 32768 | tf_op jit(solution)/shard_map/all_to_all | solution.py:233

commit v10 on v9

--- a/solution.py
+++ b/solution.py
@@ -231,9 +231,9 @@
     gathered = lax.all_to_all(outgoing, "freq", 0, 0, tiled=True)
     power_freq = jnp.sum(gathered[:, lines, :3].astype(jnp.float32))
     column_power = lax.all_to_all(
-        jnp.broadcast_to(power_freq, (sky_count, 128)), "sky", 0, 0, tiled=True
-    )
-    power_sum = jnp.sum(column_power[:, 0])
+        jnp.broadcast_to(power_freq, (sky_count, 8, 128)), "sky", 0, 0, tiled=True
+    )
+    power_sum = jnp.sum(column_power[:, 0, 0])
     images = gathered[:, :lines].reshape(freq_count, lines, channels, columns)
     weights = filters(templates, all_channels, ORDER).reshape(-1, freq_count, channels)
     result = jnp.einsum(

time: 106 us -> 107 us (level)
  waiting for transfers between devices: 27.9 us -> 29 us
where the time goes in v10:
time: 107 us; the launch traced here: 106 us
  starting transfers between devices  29.2 us (27%)
  waiting for transfers between devices  29 us (27%)
  other arithmetic  15.5 us (14%)
  local copies, waits for them, and re-layouts  15 us (14%)
  Pallas kernels  9.71 us (9%)
  matrix products  6.21 us (6%)
  between operations  1.51 us (1%)
    all_to_all x1, waiting for transfers between devices, body(): gathered = lax.all_to_all(outgoing, 'freq', 0, 0, tiled=True)  18.4 us
    all_to_all x1, starting transfers between devices, body(): turned = lax.all_to_all(send, 'sky', 0, 0, tiled=True)  14 us
    all_to_all x1, starting transfers between devices, body(): gathered = lax.all_to_all(outgoing, 'freq', 0, 0, tiled=True)  9.92 us
    all_to_all x1, waiting for transfers between devices, body(): lax.all_to_all(jnp.broadcast_to(power_freq, (sky_count, 8, 128)), 'sky',...  7.78 us
    all_to_all x1, starting transfers between devices, body(): lax.all_to_all(jnp.broadcast_to(power_freq, (sky_count, 8, 128)), 'sky',...  5.3 us
    pallas_call x1, Pallas kernels, make_images(): pl.pallas_call(image_kernel, grid=(points // tile,), in_specs=[pl.BlockSp...  5.21 us
    cos x1, other arithmetic, tables(): low_c = jnp.cos(scale * low.astype(jnp.float32))  4.96 us
    pallas_call x1, Pallas kernels, make_send(): pl.pallas_call(send_kernel, grid=(row_count // rows,), in_specs=[spec_in,...  4.51 us
  transfers between devices with their start and end apart: 3, of which 3 were waited for; matrix products, arithmetic and copies ran while one was open for 24% of the time, Pallas kernels for 0%

profile of v10, /device:TPU:1, one launch (start us, length us, event | category | flops | bytes accessed | tf_op | source)
XLA Modules:
  0.0 106.3 jit_solution(8675346076763460846)
XLA Ops:
  1.8 1.6 %multiply_convert_fusion.1 = (bf16[32,32,1024]{2,1,0:T(8,128)(2,1)S(1)}, bf16[32,32,1024]{2,1,0:T(8,128)(2,1)S(1)}) fusion(f32[32,1024]{1,0:T(8,128)S(1)} %get-tuple-element.34, f32[32,1024]{1,0:T(8,128)S(1)} %get-tuple-element.29, f32[32,1024]{1,0:T(8,128)S(1)} %get-tuple-element.35, f32[32,1024]{1,0:T(8,128)S(1)} %get-tuple-element.28), kind=kLoop, calls=%fused_computation.1 | loop fusion | flops 10485760 | bytes 4718592 | tf_op jit(solution)/shard_map/convert_element_type | solution.py:31
  3.4 2.6 %fusion.41 = f32[1024,512]{0,1:T(8,128)} fusion(bf16[512,1024]{1,0:T(8,128)(2,1)S(1)} %bitcast.28, bf16[1024,1024]{1,0:T(8,128)(2,1)S(1)} %bitcast.32), kind=kOutput, calls=%fused_computation.81 | convolution fusion | flops 1073741824 | bytes 5242880 | tf_op jit(solution)/shard_map/dot_general | solution.py:207
  5.9 2.6 %fusion.42 = f32[1024,512]{0,1:T(8,128)} fusion(bf16[512,1024]{1,0:T(8,128)(2,1)S(1)} %bitcast.27, bf16[1024,1024]{1,0:T(8,128)(2,1)S(1)} %bitcast.31), kind=kOutput, calls=%fused_computation.82 | convolution fusion | flops 1073741824 | bytes 5242880 | tf_op jit(solution)/shard_map/dot_general | solution.py:210
  8.5 4.5 %shard_map.50 = bf16[32,2,32,256]{3,2,1,0:T(8,128)(2,1)} custom-call(f32[8,2,32,1024]{3,2,1,0:T(8,128)} %bitcast.33, f32[8,2,32,1024]{3,2,1,0:T(8,128)} %bitcast.34), custom_call_target="tpu_custom_call" | custom-call | flops 1048576 | bytes 2621440 | tf_op jit(solution)/shard_map/pallas_call | solution.py:112
  13.0 14.0 %all-to-all-start = ((bf16[32,2,32,256]{3,2,1,0:T(8,128)(2,1)}), bf16[32,2,32,256]{3,2,1,0:T(8,128)(2,1)}, u32[]{:S(2)}, u32[]{:S(2)}) async-start(bf16[32,2,32,256]{3,2,1,0:T(8,128)(2,1)} %shard_map.50), calls=%async_computation | async-start | bytes 2097152 | tf_op jit(solution)/shard_map/all_to_all | solution.py:214
  27.1 5.0 %fusion.12 = (f32[32,32,1,32]{3,1,2,0:T(8,128)}, f32[32,32,1,32]{3,1,2,0:T(8,128)}, f32[32,32,1,32]{3,1,2,0:T(8,128)S(1)}, f32[32,32,1,32]{3,1,2,0:T(8,128)S(1)}) fusion(s32[32,32]{1,0:T(8,128)S(1)} %multiply_add_fusion, s32[32]{0:T(128)S(1)} %iota_multiply_fusion), kind=kLoop, calls=%fused_computation.31 | loop fusion | flops 917504 | bytes 528512 | tf_op jit(solution)/shard_map/cos | solution.py:26
  32.2 0.8 copy.38
  33.0 2.1 %neg.22 = f32[32,2048]{1,0:T(8,128)} reshape(f32[32,32,2,32]{3,2,1,0:T(2,128)S(1)} %copy.38) | data formatting | bytes 524288 | tf_op jit(solution)/shard_map/neg | solution.py:39
  35.1 0.8 copy.37
  35.9 2.1 %reshape.385 = f32[32,2048]{1,0:T(8,128)} reshape(f32[32,32,2,32]{3,2,1,0:T(2,128)S(1)} %copy.37) | data formatting | bytes 524288 | tf_op jit(solution)/shard_map/reshape | solution.py:35
  38.0 1.8 %pad_maximum_fusion.1 = (f32[32,32,2,32]{3,1,2,0:T(8,128)S(1)}, f32[32,32,2,32]{3,1,2,0:T(8,128)S(1)}) fusion(f32[32,32,1,32]{3,1,2,0:T(8,128)} %get-tuple-element.24, f32[32,32,1,32]{3,1,2,0:T(8,128)} %get-tuple-element.25), kind=kLoop, calls=%fused_computation.8 | loop fusion | flops 131072 | bytes 786432 | tf_op jit(solution)/shard_map/concatenate | solution.py:35
  39.8 0.8 copy.39
  40.6 1.4 %mul.394 = f32[32,2048]{1,0:T(8,128)S(1)} reshape(f32[32,32,2,32]{3,2,1,0:T(2,128)S(1)} %copy.39) | data formatting | bytes 524288 | tf_op jit(solution)/shard_map/mul | solution.py:41
  42.0 0.8 copy.40
  42.8 1.4 %mul.398 = f32[32,2048]{1,0:T(8,128)S(1)} reshape(f32[32,32,2,32]{3,2,1,0:T(2,128)S(1)} %copy.40) | data formatting | bytes 524288 | tf_op jit(solution)/shard_map/mul | solution.py:41
  44.2 1.1 %broadcast_select_fusion = (f32[32,2048]{1,0:T(8,128)S(1)}, f32[32,2048]{1,0:T(8,128)S(1)}) fusion(f32[32,2048]{1,0:T(8,128)} %reshape.385, f32[32,2048]{1,0:T(8,128)} %neg.22, pred[2048]{0:T(1024)(128)(4,1)S(1)} %fusion.34), kind=kLoop, calls=%fused_computation.52 | loop fusion | flops 196608 | bytes 1050624 | tf_op jit(solution)/shard_map/jit(_where)/select_n | solution.py:39
  45.2 3.6 %multiply_convert_fusion = bf16[32,32,2048]{2,1,0:T(8,128)(2,1)} fusion(f32[32,2048]{1,0:T(8,128)S(1)} %mul.398, f32[32,2048]{1,0:T(8,128)S(1)} %get-tuple-element.19, f32[32,2048]{1,0:T(8,128)S(1)} %mul.394, f32[32,2048]{1,0:T(8,128)S(1)} %get-tuple-element.18), kind=kLoop, calls=%fused_computation | loop fusion | flops 10485760 | bytes 5242880 | tf_op jit(solution)/shard_map/convert_element_type | solution.py:42
  50.2 2.8 %all-to-all-done = bf16[32,2,32,256]{3,2,1,0:T(8,128)(2,1)} async-done(((bf16[32,2,32,256]{3,2,1,0:T(8,128)(2,1)}), bf16[32,2,32,256]{3,2,1,0:T(8,128)(2,1)}, u32[]{:S(2)}, u32[]{:S(2)}) %all-to-all-start) | async-done | bytes 1048608 | tf_op jit(solution)/shard_map/all_to_all | solution.py:214
  53.0 5.2 %shard_map.51 = bf16[16,65,256]{2,1,0:T(8,128)(2,1)} custom-call(bf16[1024,2048]{1,0:T(8,128)(2,1)} %bitcast.29, bf16[2048,256]{1,0:T(8,128)(2,1)} %bitcast.10.turned_ref, f32[1,256]{1,0:T(1,128)} %reshape.390.rate_ref, f32[1,256]{1,0:T(1,128)} %reshape.391.across_ref), custom_call_target="tpu_custom_call" | custom-call | flops 1073741824 | bytes 5767168 | tf_op jit(solution)/shard_map/pallas_call | solution.py:174
  58.2 9.9 %all-to-all-start.1 = ((bf16[16,65,256]{2,1,0:T(8,128)(2,1)}), bf16[16,65,256]{2,1,0:T(8,128)(2,1)S(1)}, u32[]{:S(2)}, u32[]{:S(2)}) async-start(bf16[16,65,256]{2,1,0:T(8,128)(2,1)} %shard_map.51), calls=%async_computation.1 | async-start | bytes 1179648 | tf_op jit(solution)/shard_map/all_to_all | solution.py:231
  68.3 18.4 %all-to-all-done.1 = bf16[16,65,256]{2,1,0:T(8,128)(2,1)S(1)} async-done(((bf16[16,65,256]{2,1,0:T(8,128)(2,1)}), bf16[16,65,256]{2,1,0:T(8,128)(2,1)S(1)}, u32[]{:S(2)}, u32[]{:S(2)}) %all-to-all-start.1) | async-done | bytes 532512 | tf_op jit(solution)/shard_map/all_to_all | solution.py:231
  87.3 1.3 %broadcast_in_dim.22 = f32[32,8,128]{2,1,0:T(8,128)} broadcast(f32[]{:T(128)} %fusion.37), dimensions={} | broadcast | bytes 131076 | tf_op jit(solution)/shard_map/broadcast_in_dim | solution.py:234
  88.6 5.3 %all-to-all-start.2 = ((f32[32,8,128]{2,1,0:T(8,128)}), f32[32,8,128]{2,1,0:T(8,128)S(1)}, u32[]{:S(2)}, u32[]{:S(2)}) async-start(f32[32,8,128]{2,1,0:T(8,128)} %broadcast_in_dim.22), calls=%async_computation.2 | async-start | bytes 262144 | tf_op jit(solution)/shard_map/all_to_all | solution.py:233
  96.3 7.8 %all-to-all-done.2 = f32[32,8,128]{2,1,0:T(8,128)S(1)} async-done(((f32[32,8,128]{2,1,0:T(8,128)}), f32[32,8,128]{2,1,0:T(8,128)S(1)}, u32[]{:S(2)}, u32[]{:S(2)}) %all-to-all-start.2) | async-done | bytes 131104 | tf_op jit(solution)/shard_map/all_to_all | solution.py:233
  (33 shorter events, 7.2 us)
Async XLA Ops:
  0.6 2.7 %copy-start = (bf16[8,2,32,1024]{3,2,1,0:T(8,128)(2,1)S(1)}, bf16[8,2,32,1024]{3,2,1,0:T(8,128)(2,1)}, u32[]{:S(2)}) copy-start(bf16[8,2,32,1024]{3,2,1,0:T(8,128)(2,1)} %param.3) | copy-start | bytes 3145732
  13.0 40.0 %all-to-all-start = ((bf16[32,2,32,256]{3,2,1,0:T(8,128)(2,1)}), bf16[32,2,32,256]{3,2,1,0:T(8,128)(2,1)}, u32[]{:S(2)}, u32[]{:S(2)}) async-start(bf16[32,2,32,256]{3,2,1,0:T(8,128)(2,1)} %shard_map.50), calls=%async_computation | async-start | bytes 2097152 | tf_op jit(solution)/shard_map/all_to_all | solution.py:214
  48.8 19.4 %copy-start.2 = (f32[16,128]{1,0:T(8,128)S(1)}, f32[16,128]{1,0:T(8,128)}, u32[]{:S(2)}) copy-start(f32[16,128]{1,0:T(8,128)} %param.4) | copy-start | bytes 24580
  48.8 19.4 %copy-start.3 = (f32[9,128]{1,0:T(8,128)S(1)}, f32[9,128]{1,0:T(8,128)}, u32[]{:S(2)}) copy-start(f32[9,128]{1,0:T(8,128)} %constant.106.clone) | copy-start | bytes 13828
  53.0 41.8 %copy-start.1 = (bf16[9,16,8]{0,1,2:T(8,128)(2,1)S(1)}, bf16[9,16,8]{0,1,2:T(8,128)(2,1)}, u32[]{:S(2)}) copy-start(bf16[9,16,8]{0,1,2:T(8,128)(2,1)} %constant.109) | copy-start | bytes 6916
  58.2 28.5 %all-to-all-start.1 = ((bf16[16,65,256]{2,1,0:T(8,128)(2,1)}), bf16[16,65,256]{2,1,0:T(8,128)(2,1)S(1)}, u32[]{:S(2)}, u32[]{:S(2)}) async-start(bf16[16,65,256]{2,1,0:T(8,128)(2,1)} %shard_map.51), calls=%async_computation.1 | async-start | bytes 1179648 | tf_op jit(solution)/shard_map/all_to_all | solution.py:231
  88.6 15.5 %all-to-all-start.2 = ((f32[32,8,128]{2,1,0:T(8,128)}), f32[32,8,128]{2,1,0:T(8,128)S(1)}, u32[]{:S(2)}, u32[]{:S(2)}) async-start(f32[32,8,128]{2,1,0:T(8,128)} %broadcast_in_dim.22), calls=%async_computation.2 | async-start | bytes 262144 | tf_op jit(solution)/shard_map/all_to_all | solution.py:233

commit v11 on v9

--- a/solution.py
+++ b/solution.py
@@ -170,7 +170,7 @@
     points, depth = table.shape
     width = turned.shape[1]
     lines = points // freq_count
-    tile = 256
+    tile = 512
     return pl.pallas_call(
         image_kernel,
         grid=(points // tile,),

time: 106 us -> 105 us (level)
  no operation moved by 1% of the time
where the time goes in v11:
time: 105 us; the launch traced here: 104 us
  starting transfers between devices  29.2 us (28%)
  waiting for transfers between devices  27.9 us (27%)
  other arithmetic  15.5 us (15%)
  local copies, waits for them, and re-layouts  15 us (14%)
  Pallas kernels  8.86 us (8%)
  matrix products  6.23 us (6%)
  between operations  1.51 us (1%)
    all_to_all x1, waiting for transfers between devices, body(): gathered = lax.all_to_all(outgoing, 'freq', 0, 0, tiled=True)  18 us
    all_to_all x1, starting transfers between devices, body(): turned = lax.all_to_all(send, 'sky', 0, 0, tiled=True)  14 us
    all_to_all x1, starting transfers between devices, body(): gathered = lax.all_to_all(outgoing, 'freq', 0, 0, tiled=True)  9.92 us
    all_to_all x1, waiting for transfers between devices, body(): lax.all_to_all(jnp.broadcast_to(power_freq, (sky_count, 128)), 'sky', 0,...  7.04 us
    all_to_all x1, starting transfers between devices, body(): lax.all_to_all(jnp.broadcast_to(power_freq, (sky_count, 128)), 'sky', 0,...  5.3 us
    cos x1, other arithmetic, tables(): low_c = jnp.cos(scale * low.astype(jnp.float32))  4.96 us
    pallas_call x1, Pallas kernels, make_send(): pl.pallas_call(send_kernel, grid=(row_count // rows,), in_specs=[spec_in,...  4.51 us
    pallas_call x1, Pallas kernels, make_images(): pl.pallas_call(image_kernel, grid=(points // tile,), in_specs=[pl.BlockSp...  4.35 us
  transfers between devices with their start and end apart: 3, of which 3 were waited for; matrix products, arithmetic and copies ran while one was open for 24% of the time, Pallas kernels for 0%

profile of v11, /device:TPU:1, one launch (start us, length us, event | category | flops | bytes accessed | tf_op | source)
XLA Modules:
  0.0 104.2 jit_solution(6459851755833778246)
XLA Ops:
  1.8 1.6 %multiply_convert_fusion.1 = (bf16[32,32,1024]{2,1,0:T(8,128)(2,1)S(1)}, bf16[32,32,1024]{2,1,0:T(8,128)(2,1)S(1)}) fusion(f32[32,1024]{1,0:T(8,128)S(1)} %get-tuple-element.34, f32[32,1024]{1,0:T(8,128)S(1)} %get-tuple-element.29, f32[32,1024]{1,0:T(8,128)S(1)} %get-tuple-element.35, f32[32,1024]{1,0:T(8,128)S(1)} %get-tuple-element.28), kind=kLoop, calls=%fused_computation.1 | loop fusion | flops 10485760 | bytes 4718592 | tf_op jit(solution)/shard_map/convert_element_type | solution.py:31
  3.4 2.6 %fusion.41 = f32[1024,512]{0,1:T(8,128)} fusion(bf16[512,1024]{1,0:T(8,128)(2,1)S(1)} %bitcast.29, bf16[1024,1024]{1,0:T(8,128)(2,1)S(1)} %bitcast.33), kind=kOutput, calls=%fused_computation.81 | convolution fusion | flops 1073741824 | bytes 5242880 | tf_op jit(solution)/shard_map/dot_general | solution.py:207
  5.9 2.6 %fusion.42 = f32[1024,512]{0,1:T(8,128)} fusion(bf16[512,1024]{1,0:T(8,128)(2,1)S(1)} %bitcast.28, bf16[1024,1024]{1,0:T(8,128)(2,1)S(1)} %bitcast.32), kind=kOutput, calls=%fused_computation.82 | convolution fusion | flops 1073741824 | bytes 5242880 | tf_op jit(solution)/shard_map/dot_general | solution.py:210
  8.5 4.5 %shard_map.50 = bf16[32,2,32,256]{3,2,1,0:T(8,128)(2,1)} custom-call(f32[8,2,32,1024]{3,2,1,0:T(8,128)} %bitcast.34, f32[8,2,32,1024]{3,2,1,0:T(8,128)} %bitcast.35), custom_call_target="tpu_custom_call" | custom-call | flops 1048576 | bytes 2621440 | tf_op jit(solution)/shard_map/pallas_call | solution.py:112
  13.0 14.0 %all-to-all-start = ((bf16[32,2,32,256]{3,2,1,0:T(8,128)(2,1)}), bf16[32,2,32,256]{3,2,1,0:T(8,128)(2,1)}, u32[]{:S(2)}, u32[]{:S(2)}) async-start(bf16[32,2,32,256]{3,2,1,0:T(8,128)(2,1)} %shard_map.50), calls=%async_computation | async-start | bytes 2097152 | tf_op jit(solution)/shard_map/all_to_all | solution.py:214
  27.1 5.0 %fusion.12 = (f32[32,32,1,32]{3,1,2,0:T(8,128)}, f32[32,32,1,32]{3,1,2,0:T(8,128)}, f32[32,32,1,32]{3,1,2,0:T(8,128)S(1)}, f32[32,32,1,32]{3,1,2,0:T(8,128)S(1)}) fusion(s32[32,32]{1,0:T(8,128)S(1)} %multiply_add_fusion, s32[32]{0:T(128)S(1)} %iota_multiply_fusion), kind=kLoop, calls=%fused_computation.31 | loop fusion | flops 917504 | bytes 528512 | tf_op jit(solution)/shard_map/cos | solution.py:26
  32.2 0.8 copy.38
  33.0 2.1 %neg.22 = f32[32,2048]{1,0:T(8,128)} reshape(f32[32,32,2,32]{3,2,1,0:T(2,128)S(1)} %copy.38) | data formatting | bytes 524288 | tf_op jit(solution)/shard_map/neg | solution.py:39
  35.1 0.8 copy.37
  35.9 2.1 %reshape.387 = f32[32,2048]{1,0:T(8,128)} reshape(f32[32,32,2,32]{3,2,1,0:T(2,128)S(1)} %copy.37) | data formatting | bytes 524288 | tf_op jit(solution)/shard_map/reshape | solution.py:35
  38.0 1.8 %pad_maximum_fusion.1 = (f32[32,32,2,32]{3,1,2,0:T(8,128)S(1)}, f32[32,32,2,32]{3,1,2,0:T(8,128)S(1)}) fusion(f32[32,32,1,32]{3,1,2,0:T(8,128)} %get-tuple-element.24, f32[32,32,1,32]{3,1,2,0:T(8,128)} %get-tuple-element.25), kind=kLoop, calls=%fused_computation.8 | loop fusion | flops 131072 | bytes 786432 | tf_op jit(solution)/shard_map/concatenate | solution.py:35
  39.8 0.8 copy.39
  40.6 1.4 %mul.394 = f32[32,2048]{1,0:T(8,128)S(1)} reshape(f32[32,32,2,32]{3,2,1,0:T(2,128)S(1)} %copy.39) | data formatting | bytes 524288 | tf_op jit(solution)/shard_map/mul | solution.py:41
  42.0 0.8 copy.40
  42.8 1.4 %mul.398 = f32[32,2048]{1,0:T(8,128)S(1)} reshape(f32[32,32,2,32]{3,2,1,0:T(2,128)S(1)} %copy.40) | data formatting | bytes 524288 | tf_op jit(solution)/shard_map/mul | solution.py:41
  44.2 1.1 %broadcast_select_fusion = (f32[32,2048]{1,0:T(8,128)S(1)}, f32[32,2048]{1,0:T(8,128)S(1)}) fusion(f32[32,2048]{1,0:T(8,128)} %reshape.387, f32[32,2048]{1,0:T(8,128)} %neg.22, pred[2048]{0:T(1024)(128)(4,1)S(1)} %fusion.34), kind=kLoop, calls=%fused_computation.52 | loop fusion | flops 196608 | bytes 1050624 | tf_op jit(solution)/shard_map/jit(_where)/select_n | solution.py:39
  45.2 3.6 %multiply_convert_fusion = bf16[32,32,2048]{2,1,0:T(8,128)(2,1)} fusion(f32[32,2048]{1,0:T(8,128)S(1)} %mul.398, f32[32,2048]{1,0:T(8,128)S(1)} %get-tuple-element.19, f32[32,2048]{1,0:T(8,128)S(1)} %mul.394, f32[32,2048]{1,0:T(8,128)S(1)} %get-tuple-element.18), kind=kLoop, calls=%fused_computation | loop fusion | flops 10485760 | bytes 5242880 | tf_op jit(solution)/shard_map/convert_element_type | solution.py:42
  50.2 2.8 %all-to-all-done = bf16[32,2,32,256]{3,2,1,0:T(8,128)(2,1)} async-done(((bf16[32,2,32,256]{3,2,1,0:T(8,128)(2,1)}), bf16[32,2,32,256]{3,2,1,0:T(8,128)(2,1)}, u32[]{:S(2)}, u32[]{:S(2)}) %all-to-all-start) | async-done | bytes 1048608 | tf_op jit(solution)/shard_map/all_to_all | solution.py:214
  53.0 4.3 %shard_map.51 = bf16[16,65,256]{2,1,0:T(8,128)(2,1)} custom-call(bf16[1024,2048]{1,0:T(8,128)(2,1)} %bitcast.30, bf16[2048,256]{1,0:T(8,128)(2,1)} %bitcast.10.turned_ref, f32[1,256]{1,0:T(1,128)} %reshape.392.rate_ref, f32[1,256]{1,0:T(1,128)} %reshape.393.across_ref), custom_call_target="tpu_custom_call" | custom-call | flops 1073741824 | bytes 5767168 | tf_op jit(solution)/shard_map/pallas_call | solution.py:174
  57.4 9.9 %all-to-all-start.1 = ((bf16[16,65,256]{2,1,0:T(8,128)(2,1)}), bf16[16,65,256]{2,1,0:T(8,128)(2,1)S(1)}, u32[]{:S(2)}, u32[]{:S(2)}) async-start(bf16[16,65,256]{2,1,0:T(8,128)(2,1)} %shard_map.51), calls=%async_computation.1 | async-start | bytes 1179648 | tf_op jit(solution)/shard_map/all_to_all | solution.py:231
  67.8 18.0 %all-to-all-done.1 = bf16[16,65,256]{2,1,0:T(8,128)(2,1)S(1)} async-done(((bf16[16,65,256]{2,1,0:T(8,128)(2,1)}), bf16[16,65,256]{2,1,0:T(8,128)(2,1)S(1)}, u32[]{:S(2)}, u32[]{:S(2)}) %all-to-all-start.1) | async-done | bytes 532512 | tf_op jit(solution)/shard_map/all_to_all | solution.py:231
  87.0 1.3 %broadcast_in_dim.22 = f32[32,1,128]{2,1,0:T(1,128)} broadcast(f32[]{:T(128)} %fusion.37), dimensions={} | broadcast | bytes 16388 | tf_op jit(solution)/shard_map/broadcast_in_dim | solution.py:234
  88.3 5.3 %all-to-all-start.2 = ((f32[32,1,128]{2,1,0:T(1,128)}), f32[32,1,128]{2,1,0:T(1,128)S(1)}, u32[]{:S(2)}, u32[]{:S(2)}) async-start(f32[32,1,128]{2,1,0:T(1,128)} %broadcast_in_dim.22), calls=%async_computation.2 | async-start | bytes 32768 | tf_op jit(solution)/shard_map/all_to_all | solution.py:233
  95.1 7.0 %all-to-all-done.2 = f32[32,1,128]{2,1,0:T(1,128)S(1)} async-done(((f32[32,1,128]{2,1,0:T(1,128)}), f32[32,1,128]{2,1,0:T(1,128)S(1)}, u32[]{:S(2)}, u32[]{:S(2)}) %all-to-all-start.2) | async-done | bytes 16416 | tf_op jit(solution)/shard_map/all_to_all | solution.py:233
  (33 shorter events, 7.2 us)
Async XLA Ops:
  0.6 2.7 %copy-start = (bf16[8,2,32,1024]{3,2,1,0:T(8,128)(2,1)S(1)}, bf16[8,2,32,1024]{3,2,1,0:T(8,128)(2,1)}, u32[]{:S(2)}) copy-start(bf16[8,2,32,1024]{3,2,1,0:T(8,128)(2,1)} %param.3) | copy-start | bytes 3145732
  13.0 40.0 %all-to-all-start = ((bf16[32,2,32,256]{3,2,1,0:T(8,128)(2,1)}), bf16[32,2,32,256]{3,2,1,0:T(8,128)(2,1)}, u32[]{:S(2)}, u32[]{:S(2)}) async-start(bf16[32,2,32,256]{3,2,1,0:T(8,128)(2,1)} %shard_map.50), calls=%async_computation | async-start | bytes 2097152 | tf_op jit(solution)/shard_map/all_to_all | solution.py:214
  48.8 18.5 %copy-start.2 = (f32[16,128]{1,0:T(8,128)S(1)}, f32[16,128]{1,0:T(8,128)}, u32[]{:S(2)}) copy-start(f32[16,128]{1,0:T(8,128)} %param.4) | copy-start | bytes 24580
  48.8 18.5 %copy-start.3 = (f32[9,128]{1,0:T(8,128)S(1)}, f32[9,128]{1,0:T(8,128)}, u32[]{:S(2)}) copy-start(f32[9,128]{1,0:T(8,128)} %constant.106.clone) | copy-start | bytes 13828
  53.0 40.5 %copy-start.1 = (bf16[9,16,8]{0,1,2:T(8,128)(2,1)S(1)}, bf16[9,16,8]{0,1,2:T(8,128)(2,1)}, u32[]{:S(2)}) copy-start(bf16[9,16,8]{0,1,2:T(8,128)(2,1)} %constant.109) | copy-start | bytes 6916
  57.4 28.5 %all-to-all-start.1 = ((bf16[16,65,256]{2,1,0:T(8,128)(2,1)}), bf16[16,65,256]{2,1,0:T(8,128)(2,1)S(1)}, u32[]{:S(2)}, u32[]{:S(2)}) async-start(bf16[16,65,256]{2,1,0:T(8,128)(2,1)} %shard_map.51), calls=%async_computation.1 | async-start | bytes 1179648 | tf_op jit(solution)/shard_map/all_to_all | solution.py:231
  88.3 13.8 %all-to-all-start.2 = ((f32[32,1,128]{2,1,0:T(1,128)}), f32[32,1,128]{2,1,0:T(1,128)S(1)}, u32[]{:S(2)}, u32[]{:S(2)}) async-start(f32[32,1,128]{2,1,0:T(1,128)} %broadcast_in_dim.22), calls=%async_computation.2 | async-start | bytes 32768 | tf_op jit(solution)/shard_map/all_to_all | solution.py:233

commit v12 on v11

--- a/solution.py
+++ b/solution.py
@@ -107,7 +107,7 @@
 
 def make_send(with_cos, with_sin, sky_count, columns):
     channels, _, row_count, points = with_cos.shape
-    rows = 8
+    rows = 16
     spec_in = pl.BlockSpec((channels, 2, rows, points), lambda r: (0, 0, r, 0))
     return pl.pallas_call(
         send_kernel,

time: 105 us -> 104 us (level)
  no operation moved by 1% of the time
where the time goes in v12:
time: 104 us; the launch traced here: 103 us
  starting transfers between devices  29.2 us (28%)
  waiting for transfers between devices  27.9 us (27%)
  other arithmetic  15.5 us (15%)
  local copies, waits for them, and re-layouts  15 us (14%)
  Pallas kernels  7.9 us (8%)
  matrix products  6.23 us (6%)
  between operations  1.51 us (1%)
    all_to_all x1, waiting for transfers between devices, body(): gathered = lax.all_to_all(outgoing, 'freq', 0, 0, tiled=True)  18 us
    all_to_all x1, starting transfers between devices, body(): turned = lax.all_to_all(send, 'sky', 0, 0, tiled=True)  14 us
    all_to_all x1, starting transfers between devices, body(): gathered = lax.all_to_all(outgoing, 'freq', 0, 0, tiled=True)  9.92 us
    all_to_all x1, waiting for transfers between devices, body(): lax.all_to_all(jnp.broadcast_to(power_freq, (sky_count, 128)), 'sky', 0,...  7.04 us
    all_to_all x1, starting transfers between devices, body(): lax.all_to_all(jnp.broadcast_to(power_freq, (sky_count, 128)), 'sky', 0,...  5.3 us
    cos x1, other arithmetic, tables(): low_c = jnp.cos(scale * low.astype(jnp.float32))  4.96 us
    pallas_call x1, Pallas kernels, make_images(): pl.pallas_call(image_kernel, grid=(points // tile,), in_specs=[pl.BlockSp...  4.35 us
    convert_element_type x1, other arithmetic, tables(): (table * factor).astype(jnp.bfloat16).reshape(points, sources * 2 * depth)  3.57 us
  transfers between devices with their start and end apart: 3, of which 3 were waited for; matrix products, arithmetic and copies ran while one was open for 24% of the time, Pallas kernels for 0%

profile of v12, /device:TPU:1, one launch (start us, length us, event | category | flops | bytes accessed | tf_op | source)
XLA Modules:
  0.0 103.3 jit_solution(11353403478429221177)
XLA Ops:
  1.8 1.6 %multiply_convert_fusion.1 = (bf16[32,32,1024]{2,1,0:T(8,128)(2,1)S(1)}, bf16[32,32,1024]{2,1,0:T(8,128)(2,1)S(1)}) fusion(f32[32,1024]{1,0:T(8,128)S(1)} %get-tuple-element.34, f32[32,1024]{1,0:T(8,128)S(1)} %get-tuple-element.29, f32[32,1024]{1,0:T(8,128)S(1)} %get-tuple-element.35, f32[32,1024]{1,0:T(8,128)S(1)} %get-tuple-element.28), kind=kLoop, calls=%fused_computation.1 | loop fusion | flops 10485760 | bytes 4718592 | tf_op jit(solution)/shard_map/convert_element_type | solution.py:31
  3.4 2.6 %fusion.41 = f32[1024,512]{0,1:T(8,128)} fusion(bf16[512,1024]{1,0:T(8,128)(2,1)S(1)} %bitcast.29, bf16[1024,1024]{1,0:T(8,128)(2,1)S(1)} %bitcast.33), kind=kOutput, calls=%fused_computation.81 | convolution fusion | flops 1073741824 | bytes 5242880 | tf_op jit(solution)/shard_map/dot_general | solution.py:207
  5.9 2.6 %fusion.42 = f32[1024,512]{0,1:T(8,128)} fusion(bf16[512,1024]{1,0:T(8,128)(2,1)S(1)} %bitcast.28, bf16[1024,1024]{1,0:T(8,128)(2,1)S(1)} %bitcast.32), kind=kOutput, calls=%fused_computation.82 | convolution fusion | flops 1073741824 | bytes 5242880 | tf_op jit(solution)/shard_map/dot_general | solution.py:210
  8.5 3.5 %shard_map.50 = bf16[32,2,32,256]{3,2,1,0:T(8,128)(2,1)} custom-call(f32[8,2,32,1024]{3,2,1,0:T(8,128)} %bitcast.34, f32[8,2,32,1024]{3,2,1,0:T(8,128)} %bitcast.35), custom_call_target="tpu_custom_call" | custom-call | flops 1048576 | bytes 2621440 | tf_op jit(solution)/shard_map/pallas_call | solution.py:112
  12.1 14.0 %all-to-all-start = ((bf16[32,2,32,256]{3,2,1,0:T(8,128)(2,1)}), bf16[32,2,32,256]{3,2,1,0:T(8,128)(2,1)}, u32[]{:S(2)}, u32[]{:S(2)}) async-start(bf16[32,2,32,256]{3,2,1,0:T(8,128)(2,1)} %shard_map.50), calls=%async_computation | async-start | bytes 2097152 | tf_op jit(solution)/shard_map/all_to_all | solution.py:214
  26.1 5.0 %fusion.12 = (f32[32,32,1,32]{3,1,2,0:T(8,128)}, f32[32,32,1,32]{3,1,2,0:T(8,128)}, f32[32,32,1,32]{3,1,2,0:T(8,128)S(1)}, f32[32,32,1,32]{3,1,2,0:T(8,128)S(1)}) fusion(s32[32,32]{1,0:T(8,128)S(1)} %multiply_add_fusion, s32[32]{0:T(128)S(1)} %iota_multiply_fusion), kind=kLoop, calls=%fused_computation.31 | loop fusion | flops 917504 | bytes 528512 | tf_op jit(solution)/shard_map/cos | solution.py:26
  31.2 0.8 copy.38
  32.1 2.1 %neg.22 = f32[32,2048]{1,0:T(8,128)} reshape(f32[32,32,2,32]{3,2,1,0:T(2,128)S(1)} %copy.38) | data formatting | bytes 524288 | tf_op jit(solution)/shard_map/neg | solution.py:39
  34.1 0.8 copy.37
  35.0 2.1 %reshape.387 = f32[32,2048]{1,0:T(8,128)} reshape(f32[32,32,2,32]{3,2,1,0:T(2,128)S(1)} %copy.37) | data formatting | bytes 524288 | tf_op jit(solution)/shard_map/reshape | solution.py:35
  37.0 1.8 %pad_maximum_fusion.1 = (f32[32,32,2,32]{3,1,2,0:T(8,128)S(1)}, f32[32,32,2,32]{3,1,2,0:T(8,128)S(1)}) fusion(f32[32,32,1,32]{3,1,2,0:T(8,128)} %get-tuple-element.24, f32[32,32,1,32]{3,1,2,0:T(8,128)} %get-tuple-element.25), kind=kLoop, calls=%fused_computation.8 | loop fusion | flops 131072 | bytes 786432 | tf_op jit(solution)/shard_map/concatenate | solution.py:35
  38.8 0.8 copy.39
  39.7 1.4 %mul.394 = f32[32,2048]{1,0:T(8,128)S(1)} reshape(f32[32,32,2,32]{3,2,1,0:T(2,128)S(1)} %copy.39) | data formatting | bytes 524288 | tf_op jit(solution)/shard_map/mul | solution.py:41
  41.0 0.8 copy.40
  41.8 1.4 %mul.398 = f32[32,2048]{1,0:T(8,128)S(1)} reshape(f32[32,32,2,32]{3,2,1,0:T(2,128)S(1)} %copy.40) | data formatting | bytes 524288 | tf_op jit(solution)/shard_map/mul | solution.py:41
  43.2 1.1 %broadcast_select_fusion = (f32[32,2048]{1,0:T(8,128)S(1)}, f32[32,2048]{1,0:T(8,128)S(1)}) fusion(f32[32,2048]{1,0:T(8,128)} %reshape.387, f32[32,2048]{1,0:T(8,128)} %neg.22, pred[2048]{0:T(1024)(128)(4,1)S(1)} %fusion.34), kind=kLoop, calls=%fused_computation.52 | loop fusion | flops 196608 | bytes 1050624 | tf_op jit(solution)/shard_map/jit(_where)/select_n | solution.py:39
  44.3 3.6 %multiply_convert_fusion = bf16[32,32,2048]{2,1,0:T(8,128)(2,1)} fusion(f32[32,2048]{1,0:T(8,128)S(1)} %mul.398, f32[32,2048]{1,0:T(8,128)S(1)} %get-tuple-element.19, f32[32,2048]{1,0:T(8,128)S(1)} %mul.394, f32[32,2048]{1,0:T(8,128)S(1)} %get-tuple-element.18), kind=kLoop, calls=%fused_computation | loop fusion | flops 10485760 | bytes 5242880 | tf_op jit(solution)/shard_map/convert_element_type | solution.py:42
  49.2 2.8 %all-to-all-done = bf16[32,2,32,256]{3,2,1,0:T(8,128)(2,1)} async-done(((bf16[32,2,32,256]{3,2,1,0:T(8,128)(2,1)}), bf16[32,2,32,256]{3,2,1,0:T(8,128)(2,1)}, u32[]{:S(2)}, u32[]{:S(2)}) %all-to-all-start) | async-done | bytes 1048608 | tf_op jit(solution)/shard_map/all_to_all | solution.py:214
  52.1 4.3 %shard_map.51 = bf16[16,65,256]{2,1,0:T(8,128)(2,1)} custom-call(bf16[1024,2048]{1,0:T(8,128)(2,1)} %bitcast.30, bf16[2048,256]{1,0:T(8,128)(2,1)} %bitcast.10.turned_ref, f32[1,256]{1,0:T(1,128)} %reshape.392.rate_ref, f32[1,256]{1,0:T(1,128)} %reshape.393.across_ref), custom_call_target="tpu_custom_call" | custom-call | flops 1073741824 | bytes 5767168 | tf_op jit(solution)/shard_map/pallas_call | solution.py:174
  56.4 9.9 %all-to-all-start.1 = ((bf16[16,65,256]{2,1,0:T(8,128)(2,1)}), bf16[16,65,256]{2,1,0:T(8,128)(2,1)S(1)}, u32[]{:S(2)}, u32[]{:S(2)}) async-start(bf16[16,65,256]{2,1,0:T(8,128)(2,1)} %shard_map.51), calls=%async_computation.1 | async-start | bytes 1179648 | tf_op jit(solution)/shard_map/all_to_all | solution.py:231
  66.9 18.0 %all-to-all-done.1 = bf16[16,65,256]{2,1,0:T(8,128)(2,1)S(1)} async-done(((bf16[16,65,256]{2,1,0:T(8,128)(2,1)}), bf16[16,65,256]{2,1,0:T(8,128)(2,1)S(1)}, u32[]{:S(2)}, u32[]{:S(2)}) %all-to-all-start.1) | async-done | bytes 532512 | tf_op jit(solution)/shard_map/all_to_all | solution.py:231
  86.0 1.3 %broadcast_in_dim.22 = f32[32,1,128]{2,1,0:T(1,128)} broadcast(f32[]{:T(128)} %fusion.37), dimensions={} | broadcast | bytes 16388 | tf_op jit(solution)/shard_map/broadcast_in_dim | solution.py:234
  87.3 5.3 %all-to-all-start.2 = ((f32[32,1,128]{2,1,0:T(1,128)}), f32[32,1,128]{2,1,0:T(1,128)S(1)}, u32[]{:S(2)}, u32[]{:S(2)}) async-start(f32[32,1,128]{2,1,0:T(1,128)} %broadcast_in_dim.22), calls=%async_computation.2 | async-start | bytes 32768 | tf_op jit(solution)/shard_map/all_to_all | solution.py:233
  94.1 7.0 %all-to-all-done.2 = f32[32,1,128]{2,1,0:T(1,128)S(1)} async-done(((f32[32,1,128]{2,1,0:T(1,128)}), f32[32,1,128]{2,1,0:T(1,128)S(1)}, u32[]{:S(2)}, u32[]{:S(2)}) %all-to-all-start.2) | async-done | bytes 16416 | tf_op jit(solution)/shard_map/all_to_all | solution.py:233
  (33 shorter events, 7.2 us)
Async XLA Ops:
  0.6 2.7 %copy-start = (bf16[8,2,32,1024]{3,2,1,0:T(8,128)(2,1)S(1)}, bf16[8,2,32,1024]{3,2,1,0:T(8,128)(2,1)}, u32[]{:S(2)}) copy-start(bf16[8,2,32,1024]{3,2,1,0:T(8,128)(2,1)} %param.3) | copy-start | bytes 3145732
  12.1 40.0 %all-to-all-start = ((bf16[32,2,32,256]{3,2,1,0:T(8,128)(2,1)}), bf16[32,2,32,256]{3,2,1,0:T(8,128)(2,1)}, u32[]{:S(2)}, u32[]{:S(2)}) async-start(bf16[32,2,32,256]{3,2,1,0:T(8,128)(2,1)} %shard_map.50), calls=%async_computation | async-start | bytes 2097152 | tf_op jit(solution)/shard_map/all_to_all | solution.py:214
  47.9 18.5 %copy-start.2 = (f32[16,128]{1,0:T(8,128)S(1)}, f32[16,128]{1,0:T(8,128)}, u32[]{:S(2)}) copy-start(f32[16,128]{1,0:T(8,128)} %param.4) | copy-start | bytes 24580
  47.9 18.5 %copy-start.3 = (f32[9,128]{1,0:T(8,128)S(1)}, f32[9,128]{1,0:T(8,128)}, u32[]{:S(2)}) copy-start(f32[9,128]{1,0:T(8,128)} %constant.106.clone) | copy-start | bytes 13828
  52.1 40.5 %copy-start.1 = (bf16[9,16,8]{0,1,2:T(8,128)(2,1)S(1)}, bf16[9,16,8]{0,1,2:T(8,128)(2,1)}, u32[]{:S(2)}) copy-start(bf16[9,16,8]{0,1,2:T(8,128)(2,1)} %constant.109) | copy-start | bytes 6916
  56.4 28.5 %all-to-all-start.1 = ((bf16[16,65,256]{2,1,0:T(8,128)(2,1)}), bf16[16,65,256]{2,1,0:T(8,128)(2,1)S(1)}, u32[]{:S(2)}, u32[]{:S(2)}) async-start(bf16[16,65,256]{2,1,0:T(8,128)(2,1)} %shard_map.51), calls=%async_computation.1 | async-start | bytes 1179648 | tf_op jit(solution)/shard_map/all_to_all | solution.py:231
  87.3 13.8 %all-to-all-start.2 = ((f32[32,1,128]{2,1,0:T(1,128)}), f32[32,1,128]{2,1,0:T(1,128)S(1)}, u32[]{:S(2)}, u32[]{:S(2)}) async-start(f32[32,1,128]{2,1,0:T(1,128)} %broadcast_in_dim.22), calls=%async_computation.2 | async-start | bytes 32768 | tf_op jit(solution)/shard_map/all_to_all | solution.py:233
